TPU v7x, 128 devices: a whole 4x4x4 slice. The times are simulated.
128 devices in a mesh: ctx: 8 (over y, core), head: 16 (over z, x).
Axes of the slice: x: 4, y: 4, z: 4, core: 2. Of those that a mesh axis runs over, the one named last changes fastest.
Arguments:
- conv_input: bfloat16 [32768, 20480], P(('ctx', 'head')), may hold values from -6 to 6
- dt_raw: bfloat16 [32768, 256], P(('ctx', 'head')), as said below
- conv_weight: bfloat16 [4, 20480], replicated, may hold values from -3 to 3
- conv_bias: float32 [20480], replicated, may hold values from -3 to 3
- a_log: float32 [256], replicated, may hold values from -0.2 to 0.2
- dt_bias: float32 [256], replicated, as said below
- d_skip: float32 [256], replicated, may hold values from 0.5 to 1.5
Outputs:
- scan_out: bfloat16 [32768, 16384], P('ctx', 'head')
Inputs may be any that keep to these rules, and one draw needn't show every extreme that they name: softplus(dt_bias[h]) lies between 0.02 / 32768 and 0.04 for every head. softplus(dt_raw[t, h] + dt_bias[h]) lies between 0.02 / 32768 and 0.5 for every token and head.
All inputs are finite; a program needn't handle non-finite values.
Results may differ from a plain program's by a relative error of at most 0.0046.
Values may be sent and summed in bfloat16 or wider, within the bound.
No kernel may reach another device: no remote copies, remote signals or barrier semaphores. Data moves between devices by JAX's collectives and lax.ppermute only.
A program may use at most 256 MiB of HBM per device.

v0:
```python
import jax
import jax.numpy as jnp
from jax import lax
from jax.sharding import PartitionSpec as P

HEADS = 256
HEADDIM = 64
STATE = 256
GROUPS = 8
CONV = 4
SPAN = 512


def shifted(value, axis, by):
    size = lax.axis_size(axis)
    pairs = [(i, i + by) for i in range(size) if 0 <= i + by < size]
    return lax.ppermute(value, axis, pairs)


def prefix(value, axis, combine, identity):
    size, position = (lax.axis_size(axis), lax.axis_index(axis))
    everything = jax.tree.map(lambda part: lax.all_gather(part, axis), value)
    start = jax.tree.map(
        lambda part, zero: jnp.broadcast_to(jnp.asarray(zero, part.dtype), part.shape),
        value,
        identity,
    )

    def turn(k, before):
        reached = k < position
        new = combine(before, jax.tree.map(lambda part: part[k], everything))
        return jax.tree.map(lambda a, b: jnp.where(reached, a, b), new, before)

    return lax.fori_loop(0, size, turn, start)


def compose(earlier, later):
    fade = jnp.exp(jnp.repeat(later[1], HEADDIM, axis=-1))
    return (earlier[0] * fade[..., None, :] + later[0], earlier[1] + later[1])


def on_device(conv_input, dt_raw, conv_weight, conv_bias, a_log, dt_bias, d_skip):
    f32 = jnp.float32
    head_count = lax.axis_size("head")
    heads_dev = HEADS // head_count
    repeat_count = head_count // GROUPS
    head_pos = lax.axis_index("head")
    group = head_pos // repeat_count
    rows = conv_input.shape[0]
    x_width = HEADS * HEADDIM
    slab = heads_dev * HEADDIM
    x_part = conv_input[:, :x_width].reshape(rows, head_count, slab)
    step_part = dt_raw.reshape(rows, head_count, heads_dev)
    arrived, steps = (
        lax.all_to_all(x_part, "head", split_axis=1, concat_axis=0, tiled=True),
        lax.all_to_all(step_part, "head", split_axis=1, concat_axis=0, tiled=True),
    )
    length = arrived.shape[0]
    shared = lax.all_gather(conv_input[:, x_width:], "head", axis=0, tiled=True)
    b_cols = lax.dynamic_slice_in_dim(shared, group * STATE, STATE, 1)
    c_cols = lax.dynamic_slice_in_dim(shared, (GROUPS + group) * STATE, STATE, 1)
    local = jnp.concatenate([arrived.reshape(length, slab), b_cols, c_cols], 1)
    steps = steps.reshape(length, heads_dev)

    def columns(table):
        last = table.ndim - 1
        return jnp.concatenate(
            [
                lax.dynamic_slice_in_dim(table, head_pos * slab, slab, last),
                lax.dynamic_slice_in_dim(table, x_width + group * STATE, STATE, last),
                lax.dynamic_slice_in_dim(table, x_width + (GROUPS + group) * STATE, STATE, last),
            ],
            last,
        )

    kernel = columns(conv_weight).astype(f32)
    offset = columns(conv_bias)
    rim = shifted(local[length - (CONV - 1) :], "ctx", 1)
    padded = jnp.concatenate([rim, local], 0)
    total = padded[0:length].astype(f32) * kernel[0]
    for k in range(1, CONV):
        total = total + padded[k : k + length].astype(f32) * kernel[k]
    act = jax.nn.silu(total + offset).astype(jnp.bfloat16)
    rate = -jnp.exp(lax.dynamic_slice_in_dim(a_log, head_pos * heads_dev, heads_dev, 0))
    bias = lax.dynamic_slice_in_dim(dt_bias, head_pos * heads_dev, heads_dev, 0)
    skip = jnp.repeat(lax.dynamic_slice_in_dim(d_skip, head_pos * heads_dev, heads_dev, 0), HEADDIM)
    step = jax.nn.softplus(steps.astype(f32) + bias)
    blocks = length // SPAN
    x_blocks = act[:, :slab].reshape(blocks, SPAN, slab)
    b_blocks = act[:, slab : slab + STATE].reshape(blocks, SPAN, STATE)
    c_blocks = act[:, slab + STATE :].reshape(blocks, SPAN, STATE)
    step_blocks = step.reshape(blocks, SPAN, heads_dev)
    cum = jnp.cumsum((rate * step).reshape(blocks, SPAN, heads_dev), axis=1)
    tri = lax.broadcasted_iota(jnp.int32, (SPAN, SPAN), 0) >= lax.broadcasted_iota(
        jnp.int32, (SPAN, SPAN), 1
    )

    def local_block(state, inputs):
        x_now, b_now, c_now, step_now, cum_now = inputs
        gram = jnp.dot(c_now, b_now.T, preferred_element_type=f32)
        cum_t = cum_now.T
        decay = jnp.exp(jnp.where(tri[None], cum_t[:, :, None] - cum_t[:, None, :], -jnp.inf))
        mix = (gram[None] * decay * step_now.T[:, None, :]).astype(jnp.bfloat16)
        x_heads = x_now.reshape(SPAN, heads_dev, HEADDIM)
        y_block = jnp.einsum("hts,shp->thp", mix, x_heads, preferred_element_type=f32).reshape(
            SPAN, slab
        )
        weight = jnp.exp(cum_now[-1][None, :] - cum_now) * step_now
        xw = (x_heads.astype(f32) * weight[:, :, None]).astype(jnp.bfloat16).reshape(SPAN, slab)
        contrib = jnp.einsum("sn,sc->nc", b_now, xw, preferred_element_type=f32)
        fade = jnp.exp(jnp.repeat(cum_now[-1], HEADDIM))
        return (state * fade[None, :] + contrib, (y_block, state))

    start_state = jnp.zeros((STATE, slab), f32)
    final, (y_blocks, entering) = lax.scan(
        local_block, start_state, (x_blocks, b_blocks, c_blocks, step_blocks, cum)
    )
    block_totals = cum[:, -1, :]
    totals = jnp.sum(block_totals, axis=0)
    incoming, passed = prefix(
        (final, totals),
        "ctx",
        compose,
        (jnp.zeros((STATE, slab), f32), jnp.zeros((heads_dev,), f32)),
    )
    before = jnp.concatenate(
        [jnp.zeros((1, heads_dev), f32), jnp.cumsum(block_totals, axis=0)[:-1]], 0
    )
    carried = jnp.exp(jnp.repeat(before, HEADDIM, axis=1))[:, None, :] * incoming[None]
    full_state = entering + carried
    grown = jnp.exp(jnp.repeat(cum, HEADDIM, axis=2))
    y_state = grown * jnp.einsum(
        "bqn,bnc->bqc", c_blocks.astype(f32), full_state, precision=lax.Precision.HIGHEST
    )
    result = y_blocks + y_state + skip * x_blocks.astype(f32)
    return result.astype(jnp.bfloat16).reshape(length, slab)


def solution(mesh):
    placed = (P(("ctx", "head"), None), P(("ctx", "head"), None), P(), P(), P(), P(), P())
    return jax.shard_map(
        on_device, mesh=mesh, in_specs=placed, out_specs=P("ctx", "head"), check_vma=False
    )
```

profile of v0, /device:TPU:30, one launch (start us, length us, event | category | flops | bytes accessed | tf_op | source)
XLA Modules:
  0.0 622.2 jit_solution(14649506826397201722)
XLA Ops:
  6.5 3.1 slice.59
  11.4 8.3 %all-to-all-start = ((bf16[256,16,16]{0,2,1:T(8,128)(2,1)}), bf16[256,16,16]{0,2,1:T(8,128)(2,1)S(1)}, u32[]{:S(2)}, u32[]{:S(2)}) async-start(bf16[256,16,16]{0,2,1:T(8,128)(2,1)} %bitcast), calls=%async_computation | async-start | bytes 262144 | tf_op jit(solution)/shard_map/all_to_all | solution.py:56
  19.6 8.7 %slice.58 = bf16[256,16384]{1,0:T(8,128)(2,1)} slice(bf16[256,20480]{1,0:T(8,128)(2,1)} %param.11), slice={[0:256], [0:16384]} | slice | bytes 16777216 | tf_op jit(solution)/shard_map/slice | solution.py:52
  28.4 12.0 %copy.62 = bf16[256,16384]{0,1:T(8,128)(2,1)} copy(bf16[256,16384]{1,0:T(8,128)(2,1)} %slice.58) | data formatting | bytes 16777216
  40.3 12.3 %copy.53 = bf16[256,16,1024]{2,0,1:T(8,128)(2,1)} copy(bf16[256,16,1024]{0,2,1:T(8,128)(2,1)} %bitcast.115) | data formatting | bytes 16777216 | tf_op jit(solution)/shard_map/reshape | solution.py:52
  52.7 7.3 %all-to-all-start.1 = ((bf16[256,16,1024]{2,0,1:T(8,128)(2,1)}), bf16[256,16,1024]{2,0,1:T(8,128)(2,1)}, u32[]{:S(2)}, u32[]{:S(2)}) async-start(bf16[256,16,1024]{2,0,1:T(8,128)(2,1)} %copy.53), calls=%async_computation.1 | async-start | bytes 16777216 | tf_op jit(solution)/shard_map/all_to_all | solution.py:55
  64.6 9.1 %reduce-window.6 = f32[8,16,4,128]{3,1,2,0:T(8,128)S(1)} reduce-window(f32[8,16,4,128]{3,1,2,0:T(8,128)S(1)} %copy.48, f32[]{:T(128)} %constant.84.clone.1), window={size=1x1x1x128 pad=0_0x0_0x0_0x127_0}, to_apply=%region_0.1 | reduce-window | flops 8323072 | bytes 524292 | tf_op jit(solution)/shard_map/reduce-window
  74.2 213.2 %all-gather.5.cloned.1.call-done = bf16[4096,4096]{1,0:T(8,128)(2,1)} async-done(((bf16[256,4096]{1,0:T(8,128)(2,1)}), bf16[4096,4096]{1,0:T(8,128)(2,1)}) %all-gather.5.cloned.1.call-update) | async-done | bytes 33554448 | tf_op jit(solution)/shard_map/all_gather | solution.py:59
  287.4 3.8 constant_dynamic-slice_fusion.6
  291.2 6.0 pad_maximum_fusion
  302.2 7.5 %maximum_maximum_fusion = bf16[4099,1536]{1,0:T(8,128)(2,1)S(1)} fusion(bf16[4096,256]{1,0:T(8,128)(2,1)S(1)} %copy-done.2, bf16[4096,256]{1,0:T(8,128)(2,1)S(1)} %get-tuple-element.290, bf16[4096,1024]{1,0:T(8,128)(2,1)} %bitcast.10, bf16[3,1536]{1,0:T(4,128)(2,1)S(1)} %collective-permute-done), kind=kLoop, calls=%fused_computation.32 | loop fusion | flops 50368512 | bytes 25184256 | tf_op jit(solution)/shard_map/concatenate | solution.py:79
  309.7 23.0 %multiply_convert_fusion.3 = bf16[4096,1536]{1,0:T(8,128)(2,1)} fusion(bf16[4099,1536]{1,0:T(8,128)(2,1)S(1)} %maximum_maximum_fusion, f32[1536]{0:T(1024)S(1)} %pad_maximum_fusion.1, f32[1536]{0:T(1024)S(1)} %get-tuple-element.255, f32[1536]{0:T(1024)S(1)} %get-tuple-element.256, f32[1536]{0:T(1024)S(1)} %get-tuple-element.257, ...), kind=kLoop, calls=%fused_computation.30 | loop fusion | flops 138412032 | bytes 62945280 | tf_op jit(solution)/shard_map/convert_element_type | solution.py:83
  332.8 7.8 %slice.85 = bf16[4096,1024]{1,0:T(8,128)(2,1)} slice(bf16[4096,1536]{1,0:T(8,128)(2,1)} %multiply_convert_fusion.3), slice={[0:4096], [0:1024]} | slice | bytes 16777216 | tf_op jit(solution)/shard_map/slice | solution.py:89
  340.5 4.5 fusion.23
  345.0 180.6 %while.29 = (s32[]{:T(128)}, f32[256,1024]{1,0:T(8,128)S(1)}, f32[8,512,1024]{2,1,0:T(8,128)}, f32[8,256,1024]{2,1,0:T(8,128)}, f32[8,512,16]{1,2,0:T(8,128)}, /...) while((s32[]{:T(128)}, f32[256,1024]{1,0:T(8,128)S(1)}, ...), condition=%wide.region_3.4_spmd.clone, body=%wide.region_2.3_spmd.clone.sunk | while | flops 963395584 | bytes 31083584 | solution.py:115
  346.7 2.3 fusion.41
  351.0 7.1 %fusion.42 = f32[16,64,512]{2,1,0:T(8,128)} fusion(bf16[512,16,64]{0,2,1:T(8,128)(2,1)S(1)} %bitcast.110, f32[16,512]{1,0:T(8,128)S(1)} %get-tuple-element.381, f32[16,512]{1,0:T(8,128)S(1)} %get-tuple-element.382, f32[512,512]{1,0:T(8,128)} %fusion.41, pred[512,512]{1,0:T(8,128)(4,1)S(1)} %iota_compare_fusion.2), kind=kOutput, calls=%fused_computation.5.clone.1 | convolution fusion | flops 557842432 | bytes 4521984 | tf_op jit(solution)/shard_map/while/body/eval_jaxpr/hts,shp->thp/dot_general | solution.py:105
  369.3 2.3 fusion.41
  373.6 7.1 %fusion.42 = f32[16,64,512]{2,1,0:T(8,128)} fusion(bf16[512,16,64]{0,2,1:T(8,128)(2,1)S(1)} %bitcast.110, f32[16,512]{1,0:T(8,128)S(1)} %get-tuple-element.381, f32[16,512]{1,0:T(8,128)S(1)} %get-tuple-element.382, f32[512,512]{1,0:T(8,128)} %fusion.41, pred[512,512]{1,0:T(8,128)(4,1)S(1)} %iota_compare_fusion.2), kind=kOutput, calls=%fused_computation.5.clone.1 | convolution fusion | flops 557842432 | bytes 4521984 | tf_op jit(solution)/shard_map/while/body/eval_jaxpr/hts,shp->thp/dot_general | solution.py:105
  396.2 7.1 %fusion.42 = f32[16,64,512]{2,1,0:T(8,128)} fusion(bf16[512,16,64]{0,2,1:T(8,128)(2,1)S(1)} %bitcast.110, f32[16,512]{1,0:T(8,128)S(1)} %get-tuple-element.381, f32[16,512]{1,0:T(8,128)S(1)} %get-tuple-element.382, f32[512,512]{1,0:T(8,128)} %fusion.41, pred[512,512]{1,0:T(8,128)(4,1)S(1)} %iota_compare_fusion.2), kind=kOutput, calls=%fused_computation.5.clone.1 | convolution fusion | flops 557842432 | bytes 4521984 | tf_op jit(solution)/shard_map/while/body/eval_jaxpr/hts,shp->thp/dot_general | solution.py:105
  418.8 7.1 %fusion.42 = f32[16,64,512]{2,1,0:T(8,128)} fusion(bf16[512,16,64]{0,2,1:T(8,128)(2,1)S(1)} %bitcast.110, f32[16,512]{1,0:T(8,128)S(1)} %get-tuple-element.381, f32[16,512]{1,0:T(8,128)S(1)} %get-tuple-element.382, f32[512,512]{1,0:T(8,128)} %fusion.41, pred[512,512]{1,0:T(8,128)(4,1)S(1)} %iota_compare_fusion.2), kind=kOutput, calls=%fused_computation.5.clone.1 | convolution fusion | flops 557842432 | bytes 4521984 | tf_op jit(solution)/shard_map/while/body/eval_jaxpr/hts,shp->thp/dot_general | solution.py:105
  441.3 7.1 %fusion.42 = f32[16,64,512]{2,1,0:T(8,128)} fusion(bf16[512,16,64]{0,2,1:T(8,128)(2,1)S(1)} %bitcast.110, f32[16,512]{1,0:T(8,128)S(1)} %get-tuple-element.381, f32[16,512]{1,0:T(8,128)S(1)} %get-tuple-element.382, f32[512,512]{1,0:T(8,128)} %fusion.41, pred[512,512]{1,0:T(8,128)(4,1)S(1)} %iota_compare_fusion.2), kind=kOutput, calls=%fused_computation.5.clone.1 | convolution fusion | flops 557842432 | bytes 4521984 | tf_op jit(solution)/shard_map/while/body/eval_jaxpr/hts,shp->thp/dot_general | solution.py:105
  463.9 7.1 %fusion.42 = f32[16,64,512]{2,1,0:T(8,128)} fusion(bf16[512,16,64]{0,2,1:T(8,128)(2,1)S(1)} %bitcast.110, f32[16,512]{1,0:T(8,128)S(1)} %get-tuple-element.381, f32[16,512]{1,0:T(8,128)S(1)} %get-tuple-element.382, f32[512,512]{1,0:T(8,128)} %fusion.41, pred[512,512]{1,0:T(8,128)(4,1)S(1)} %iota_compare_fusion.2), kind=kOutput, calls=%fused_computation.5.clone.1 | convolution fusion | flops 557842432 | bytes 4521984 | tf_op jit(solution)/shard_map/while/body/eval_jaxpr/hts,shp->thp/dot_general | solution.py:105
  486.5 7.1 %fusion.42 = f32[16,64,512]{2,1,0:T(8,128)} fusion(bf16[512,16,64]{0,2,1:T(8,128)(2,1)S(1)} %bitcast.110, f32[16,512]{1,0:T(8,128)S(1)} %get-tuple-element.381, f32[16,512]{1,0:T(8,128)S(1)} %get-tuple-element.382, f32[512,512]{1,0:T(8,128)} %fusion.41, pred[512,512]{1,0:T(8,128)(4,1)S(1)} %iota_compare_fusion.2), kind=kOutput, calls=%fused_computation.5.clone.1 | convolution fusion | flops 557842432 | bytes 4521984 | tf_op jit(solution)/shard_map/while/body/eval_jaxpr/hts,shp->thp/dot_general | solution.py:105
  504.8 2.3 fusion.41
  509.1 7.1 %fusion.42 = f32[16,64,512]{2,1,0:T(8,128)} fusion(bf16[512,16,64]{0,2,1:T(8,128)(2,1)S(1)} %bitcast.110, f32[16,512]{1,0:T(8,128)S(1)} %get-tuple-element.381, f32[16,512]{1,0:T(8,128)S(1)} %get-tuple-element.382, f32[512,512]{1,0:T(8,128)} %fusion.41, pred[512,512]{1,0:T(8,128)(4,1)S(1)} %iota_compare_fusion.2), kind=kOutput, calls=%fused_computation.5.clone.1 | convolution fusion | flops 557842432 | bytes 4521984 | tf_op jit(solution)/shard_map/while/body/eval_jaxpr/hts,shp->thp/dot_general | solution.py:105
  529.6 10.2 %all-reduce.1 = f32[128]{0:T(128)S(1)} all-reduce(f32[128]{0:T(128)S(1)} %dynamic-update-slice), channel_id=2, replica_groups=mesh['ctx'=8,'head'=16] {'ctx'}, use_global_device_ids=true, to_apply=%add.1 | all-reduce | flops 128 | bytes 1024
  540.3 8.1 %broadcast_in_dim.62 = f32[8,512,16,64]{1,3,2,0:T(8,128)} broadcast(f32[8,512,16]{1,2,0:T(8,128)S(1)} %fusion.22), dimensions={0,1,2} | broadcast | bytes 17039360 | tf_op jit(solution)/shard_map/broadcast_in_dim | solution.py:131
  548.4 16.5 %copy.56 = f32[8,512,1024]{2,1,0:T(8,128)} copy(f32[8,512,1024]{1,2,0:T(8,128)} %bitcast.112) | data formatting | bytes 33554432 | tf_op jit(solution)/shard_map/exp | solution.py:131
  564.9 9.7 %all-gather.7.cloned.1.call-done = f32[2048,1024]{1,0:T(8,128)} async-done(((f32[256,1024]{1,0:T(8,128)}), f32[2048,1024]{1,0:T(8,128)}) %all-gather.7.cloned.1.call-update) | async-done | bytes 8388624 | tf_op jit(solution)/shard_map/all_gather | solution.py:22
  574.6 18.5 %while.30 = (s32[]{:T(128)}, f32[256,1024]{1,0:T(8,128)S(1)}, s32[]{:T(128)}, f32[8,16]{1,0:T(8,128)S(1)}, f32[8,256,1024]{2,1,0:T(8,128)}, /*index=5*/s32[]{:T(128)}, s32[]{:T(128)}) while((s32[]{:T(128)}, f32[256,1024]{1,0:T(8,128)S(1)}, s32[]{:T(128)}, f32[8,16]{1,0:T(8,128)S(1)}, f32[8,256,1024]{2,1,0:T(8,128)}, ...), condition=%wide.region_7.8_spmd.clone, body=%wide.region_6.7_spmd.clone.sunk | while | flops 1048580 | bytes 3162409 | solution.py:34
  593.1 22.2 %add_convert_fusion = bf16[8,512,1024]{2,1,0:T(8,128)(2,1)} fusion(bf16[8,512,1024]{2,1,0:T(8,128)(2,1)} %get-tuple-element.449, f32[8,512,1024]{2,1,0:T(8,128)} %get-tuple-element.153, f32[8,512,1024]{2,1,0:T(8,128)} %copy.56, bf16[8,512,256]{2,1,0:T(8,128)(2,1)} %bitcast.13, f32[1024]{0:T(1024)S(1)} %mul.190, f32[8,256,1024]{2,1,0:T(8,128)} %get-tuple-element.154, ...), kind=kOutput, calls=%fused_computation.31 | convolution fusion | flops 12914262016 | bytes 61902848 | tf_op jit(solution)/shard_map/bqn,bnc->bqc/dot_general | solution.py:132
  (232 shorter events, 149.8 us)
Async XLA Ops:
  6.5 280.8 %all-gather.5.cloned.1.call-start = ((), (), s32[]{:S(2)}) async-start(), calls=%async_computation.2 | async-start | bytes 35651584 | tf_op jit(solution)/shard_map/all_gather | solution.py:59
  11.4 41.3 %all-to-all-start = ((bf16[256,16,16]{0,2,1:T(8,128)(2,1)}), bf16[256,16,16]{0,2,1:T(8,128)(2,1)S(1)}, u32[]{:S(2)}, u32[]{:S(2)}) async-start(bf16[256,16,16]{0,2,1:T(8,128)(2,1)} %bitcast), calls=%async_computation | async-start | bytes 262144 | tf_op jit(solution)/shard_map/all_to_all | solution.py:56
  52.6 8.1 %copy-start.3 = (f32[256]{0:T(256)S(1)}, f32[256]{0:T(256)}, u32[]{:S(2)}) copy-start(f32[256]{0:T(256)} %param.16) | copy-start | bytes 3076
  52.6 8.2 %copy-start.4 = (f32[256]{0:T(256)S(1)}, f32[256]{0:T(256)}, u32[]{:S(2)}) copy-start(f32[256]{0:T(256)} %param.15) | copy-start | bytes 3076
  52.7 238.6 %all-to-all-start.1 = ((bf16[256,16,1024]{2,0,1:T(8,128)(2,1)}), bf16[256,16,1024]{2,0,1:T(8,128)(2,1)}, u32[]{:S(2)}, u32[]{:S(2)}) async-start(bf16[256,16,1024]{2,0,1:T(8,128)(2,1)} %copy.53), calls=%async_computation.1 | async-start | bytes 16777216 | tf_op jit(solution)/shard_map/all_to_all | solution.py:55
  59.9 514.7 %all-gather.7.cloned.1.call-start = ((), (), s32[]{:S(2)}) async-start(), calls=%async_computation.3 | async-start | bytes 9437184 | tf_op jit(solution)/shard_map/all_gather | solution.py:22
  291.2 11.0 %copy-start.2 = (bf16[4096,256]{1,0:T(8,128)(2,1)S(1)}, bf16[4096,256]{1,0:T(8,128)(2,1)}, u32[]{:S(2)}) copy-start(bf16[4096,256]{1,0:T(8,128)(2,1)} %get-tuple-element.291) | copy-start | bytes 6291460
  297.2 5.0 collective-permute-start
  345.0 181.7 %copy-start.5 = (f32[256]{0:T(256)S(1)}, f32[256]{0:T(256)}, u32[]{:S(2)}) copy-start(f32[256]{0:T(256)} %param.17) | copy-start | bytes 3076
  345.0 181.9 %copy-start.6 = (u32[128]{0:T(128)S(1)}, u32[128]{0:T(128)}, u32[]{:S(2)}) copy-start(u32[128]{0:T(128)} %constant.103) | copy-start | bytes 1540
  350.9 7.2 %copy-start.1 = (bf16[1,512,1024]{1,2,0:T(8,128)(2,1)}, bf16[1,512,1024]{1,2,0:T(8,128)(2,1)S(1)}, u32[]{:S(2)}) copy-start(bf16[1,512,1024]{1,2,0:T(8,128)(2,1)S(1)} %copy.80) | copy-start | bytes 3145732 | tf_op jit(solution)/shard_map/while
  373.5 7.2 %copy-start.1 = (bf16[1,512,1024]{1,2,0:T(8,128)(2,1)}, bf16[1,512,1024]{1,2,0:T(8,128)(2,1)S(1)}, u32[]{:S(2)}) copy-start(bf16[1,512,1024]{1,2,0:T(8,128)(2,1)S(1)} %copy.80) | copy-start | bytes 3145732 | tf_op jit(solution)/shard_map/while
  396.1 7.2 %copy-start.1 = (bf16[1,512,1024]{1,2,0:T(8,128)(2,1)}, bf16[1,512,1024]{1,2,0:T(8,128)(2,1)S(1)}, u32[]{:S(2)}) copy-start(bf16[1,512,1024]{1,2,0:T(8,128)(2,1)S(1)} %copy.80) | copy-start | bytes 3145732 | tf_op jit(solution)/shard_map/while
  418.7 7.2 %copy-start.1 = (bf16[1,512,1024]{1,2,0:T(8,128)(2,1)}, bf16[1,512,1024]{1,2,0:T(8,128)(2,1)S(1)}, u32[]{:S(2)}) copy-start(bf16[1,512,1024]{1,2,0:T(8,128)(2,1)S(1)} %copy.80) | copy-start | bytes 3145732 | tf_op jit(solution)/shard_map/while
  441.2 7.2 %copy-start.1 = (bf16[1,512,1024]{1,2,0:T(8,128)(2,1)}, bf16[1,512,1024]{1,2,0:T(8,128)(2,1)S(1)}, u32[]{:S(2)}) copy-start(bf16[1,512,1024]{1,2,0:T(8,128)(2,1)S(1)} %copy.80) | copy-start | bytes 3145732 | tf_op jit(solution)/shard_map/while
  463.8 7.2 %copy-start.1 = (bf16[1,512,1024]{1,2,0:T(8,128)(2,1)}, bf16[1,512,1024]{1,2,0:T(8,128)(2,1)S(1)}, u32[]{:S(2)}) copy-start(bf16[1,512,1024]{1,2,0:T(8,128)(2,1)S(1)} %copy.80) | copy-start | bytes 3145732 | tf_op jit(solution)/shard_map/while
  486.4 7.2 %copy-start.1 = (bf16[1,512,1024]{1,2,0:T(8,128)(2,1)}, bf16[1,512,1024]{1,2,0:T(8,128)(2,1)S(1)}, u32[]{:S(2)}) copy-start(bf16[1,512,1024]{1,2,0:T(8,128)(2,1)S(1)} %copy.80) | copy-start | bytes 3145732 | tf_op jit(solution)/shard_map/while
  509.0 7.2 %copy-start.1 = (bf16[1,512,1024]{1,2,0:T(8,128)(2,1)}, bf16[1,512,1024]{1,2,0:T(8,128)(2,1)S(1)}, u32[]{:S(2)}) copy-start(bf16[1,512,1024]{1,2,0:T(8,128)(2,1)S(1)} %copy.80) | copy-start | bytes 3145732 | tf_op jit(solution)/shard_map/while
  525.6 1.0 copy-start
Sparse Core Ops, SparseCore 0:
  9.8 277.5 all-gather.4
  526.8 47.7 all-gather.6
where the time goes:
time: 631 us; the launch traced here: 622 us
  waiting for transfers between devices  225 us (36%)
  local copies, waits for them, and re-layouts  150 us (24%)
  matrix products  111 us (18%)
  other arithmetic  93.5 us (15%)
  starting transfers between devices  17.7 us (3%)
  between operations  14.4 us (2%)
  blocking collectives  10.2 us (2%)
    all_gather x1, waiting for transfers between devices, on_device(): shared = lax.all_gather(conv_input[:, x_width:], 'head', axis=0, tiled=True)  213 us
    dot_general x8, matrix products, local_block(): jnp.einsum('hts,shp->thp', mix, x_heads, preferred_element_type=f32)  57 us
    dynamic_update_slice x16, local copies, waits for them, and re-layouts, on_device(): lax.scan(local_block, start_state, (x_blocks, b_blocks, c_blocks, step_bl...  27.1 us
    convert_element_type x1, other arithmetic, on_device(): act = jax.nn.silu(total + offset).astype(jnp.bfloat16)  23 us
    dynamic_slice x24, local copies, waits for them, and re-layouts, on_device(): lax.scan(local_block, start_state, (x_blocks, b_blocks, c_blocks, step_bl...  22.6 us
    dot_general x1, matrix products, on_device(): jnp.einsum('bqn,bnc->bqc', c_blocks.astype(f32), full_state, precision=la...  22.2 us
    dot_general x8, matrix products, local_block(): gram = jnp.dot(c_now, b_now.T, preferred_element_type=f32)  18.5 us
    select_n x8, other arithmetic, turn(): return jax.tree.map(lambda a, b: jnp.where(reached, a, b), new, before)  17.1 us
  transfers between devices with their start and end apart: 5, of which 3 were waited for; matrix products, arithmetic and copies ran while one was open for 13% of the time, Pallas kernels for 0%

commit v1 on v0

--- a/solution.py
+++ b/solution.py
@@ -17,28 +17,6 @@
     return lax.ppermute(value, axis, pairs)
 
 
-def prefix(value, axis, combine, identity):
-    size, position = (lax.axis_size(axis), lax.axis_index(axis))
-    everything = jax.tree.map(lambda part: lax.all_gather(part, axis), value)
-    start = jax.tree.map(
-        lambda part, zero: jnp.broadcast_to(jnp.asarray(zero, part.dtype), part.shape),
-        value,
-        identity,
-    )
-
-    def turn(k, before):
-        reached = k < position
-        new = combine(before, jax.tree.map(lambda part: part[k], everything))
-        return jax.tree.map(lambda a, b: jnp.where(reached, a, b), new, before)
-
-    return lax.fori_loop(0, size, turn, start)
-
-
-def compose(earlier, later):
-    fade = jnp.exp(jnp.repeat(later[1], HEADDIM, axis=-1))
-    return (earlier[0] * fade[..., None, :] + later[0], earlier[1] + later[1])
-
-
 def on_device(conv_input, dt_raw, conv_weight, conv_bias, a_log, dt_bias, d_skip):
     f32 = jnp.float32
     head_count = lax.axis_size("head")
@@ -50,16 +28,18 @@
     x_width = HEADS * HEADDIM
     slab = heads_dev * HEADDIM
     x_part = conv_input[:, :x_width].reshape(rows, head_count, slab)
+    bc = conv_input[:, x_width:].reshape(rows, 2, GROUPS, STATE)
+    b_part = jnp.repeat(bc[:, 0], repeat_count, axis=1)
+    c_part = jnp.repeat(bc[:, 1], repeat_count, axis=1)
+    send = jnp.concatenate([x_part, b_part, c_part], axis=2)
     step_part = dt_raw.reshape(rows, head_count, heads_dev)
     arrived, steps = (
-        lax.all_to_all(x_part, "head", split_axis=1, concat_axis=0, tiled=True),
+        lax.all_to_all(send, "head", split_axis=1, concat_axis=0, tiled=True),
         lax.all_to_all(step_part, "head", split_axis=1, concat_axis=0, tiled=True),
     )
     length = arrived.shape[0]
-    shared = lax.all_gather(conv_input[:, x_width:], "head", axis=0, tiled=True)
-    b_cols = lax.dynamic_slice_in_dim(shared, group * STATE, STATE, 1)
-    c_cols = lax.dynamic_slice_in_dim(shared, (GROUPS + group) * STATE, STATE, 1)
-    local = jnp.concatenate([arrived.reshape(length, slab), b_cols, c_cols], 1)
+    width = slab + 2 * STATE
+    local = arrived.reshape(length, width)
     steps = steps.reshape(length, heads_dev)
 
     def columns(table):
@@ -105,34 +85,43 @@
         y_block = jnp.einsum("hts,shp->thp", mix, x_heads, preferred_element_type=f32).reshape(
             SPAN, slab
         )
+        grown = jnp.repeat(jnp.exp(cum_now), HEADDIM, axis=1)
+        y_state = grown * jnp.dot(
+            c_now.astype(f32), state, precision=lax.Precision.HIGHEST, preferred_element_type=f32
+        )
+        y_now = y_block + y_state + skip * x_now.astype(f32)
         weight = jnp.exp(cum_now[-1][None, :] - cum_now) * step_now
         xw = (x_heads.astype(f32) * weight[:, :, None]).astype(jnp.bfloat16).reshape(SPAN, slab)
         contrib = jnp.einsum("sn,sc->nc", b_now, xw, preferred_element_type=f32)
         fade = jnp.exp(jnp.repeat(cum_now[-1], HEADDIM))
-        return (state * fade[None, :] + contrib, (y_block, state))
+        return (state * fade[None, :] + contrib, y_now)
 
     start_state = jnp.zeros((STATE, slab), f32)
-    final, (y_blocks, entering) = lax.scan(
+    final, y_blocks = lax.scan(
         local_block, start_state, (x_blocks, b_blocks, c_blocks, step_blocks, cum)
     )
     block_totals = cum[:, -1, :]
     totals = jnp.sum(block_totals, axis=0)
-    incoming, passed = prefix(
-        (final, totals),
-        "ctx",
-        compose,
-        (jnp.zeros((STATE, slab), f32), jnp.zeros((heads_dev,), f32)),
-    )
+    tail = jnp.broadcast_to(jnp.repeat(totals, HEADDIM)[None, :], (8, slab))
+    gathered = lax.all_gather(jnp.concatenate([final, tail], 0), "ctx")
+    shards = gathered.shape[0]
+    position = lax.axis_index("ctx")
+    finals = gathered[:, :STATE]
+    shard_totals = gathered[:, STATE]
+    before_shard = jnp.cumsum(shard_totals, axis=0) - shard_totals
+    reach = jnp.sum(jnp.where(jnp.arange(shards)[:, None] < position, shard_totals, 0.0), axis=0)
+    after_own = before_shard + shard_totals
+    live = jnp.arange(shards)[:, None] < position
+    weights = jnp.where(live, jnp.exp(jnp.where(live, reach[None] - after_own, 0.0)), 0.0)
+    incoming = jnp.sum(weights[:, None, :] * finals, axis=0)
     before = jnp.concatenate(
         [jnp.zeros((1, heads_dev), f32), jnp.cumsum(block_totals, axis=0)[:-1]], 0
     )
-    carried = jnp.exp(jnp.repeat(before, HEADDIM, axis=1))[:, None, :] * incoming[None]
-    full_state = entering + carried
-    grown = jnp.exp(jnp.repeat(cum, HEADDIM, axis=2))
-    y_state = grown * jnp.einsum(
-        "bqn,bnc->bqc", c_blocks.astype(f32), full_state, precision=lax.Precision.HIGHEST
+    lifted = jnp.exp(jnp.repeat(cum + before[:, None, :], HEADDIM, axis=2))
+    y_in = lifted * jnp.einsum(
+        "bqn,nc->bqc", c_blocks.astype(f32), incoming, precision=lax.Precision.HIGHEST
     )
-    result = y_blocks + y_state + skip * x_blocks.astype(f32)
+    result = y_blocks + y_in
     return result.astype(jnp.bfloat16).reshape(length, slab)
 
 

time: 631 us -> 621 us (0.984)
  matrix products: 111 us -> 147 us
  waiting for transfers between devices: 225 us -> 195 us
  other arithmetic: 93.5 us -> 76.7 us
  local copies, waits for them, and re-layouts: 150 us -> 162 us
  blocking collectives: 10.2 us -> 0 us
    all_gather x2 -> x1, waiting for transfers between devices: 223 us -> 24.6 us  [on_device(): gathered = lax.all_gather(jnp.concatenate([final, tail], 0), 'ctx')]
    all_to_all x1, waiting for transfers between devices: 0.01 us -> 169 us  [on_device(): lax.all_to_all(send, 'head', split_axis=1, concat_axis=0, tiled=True)]
    dot_general x1 -> x9, matrix products: 22.2 us -> 59 us  [the longest x8 41.8 us: local_block(): jnp.dot(c_now.astype(f32), state, precision=lax.Precision.HIGHEST, prefer...]
    dynamic_update_slice x16 -> x0, local copies, waits for them, and re-layouts: 27.1 us -> none  [on_device(): lax.scan(local_block, start_state, (x_blocks, b_blocks, c_blocks, step_bl...]
    reshape x1 -> x17, local copies, waits for them, and re-layouts: 12.3 us -> 38.3 us  [the longest x8 23.6 us: local_block(): jnp.einsum('hts,shp->thp', mix, x_heads, preferred_element_type=f32)]
    select_n x8 -> x0, other arithmetic: 17.1 us -> none  [turn(): return jax.tree.map(lambda a, b: jnp.where(reached, a, b), new, before)]
    concatenate x0 -> x2, local copies, waits for them, and re-layouts: none -> 16.6 us  [the longest x1 16.6 us: on_device(): send = jnp.concatenate([x_part, b_part, c_part], axis=2)]
    unnamed x1 -> x0, blocking collectives: 10.2 us -> none
  transfers between devices with their start and end apart: 5 -> 4, of which waited for: 3 -> 3; matrix products, arithmetic and copies ran while one was open for 13% -> 15% of each run, Pallas kernels for 0% -> 0%
where the time goes in v1:
time: 621 us; the launch traced here: 613 us
  waiting for transfers between devices  195 us (31%)
  local copies, waits for them, and re-layouts  162 us (26%)
  matrix products  147 us (24%)
  other arithmetic  76.7 us (12%)
  starting transfers between devices  17.8 us (3%)
  between operations  13.7 us (2%)
    all_to_all x1, waiting for transfers between devices, on_device(): lax.all_to_all(send, 'head', split_axis=1, concat_axis=0, tiled=True)  169 us
    dot_general x8, matrix products, local_block(): jnp.einsum('hts,shp->thp', mix, x_heads, preferred_element_type=f32)  56.8 us
    dot_general x8, matrix products, local_block(): jnp.dot(c_now.astype(f32), state, precision=lax.Precision.HIGHEST, prefer...  41.8 us
    convert_element_type x1, other arithmetic, on_device(): act = jax.nn.silu(total + offset).astype(jnp.bfloat16)  27.2 us
    all_gather x1, waiting for transfers between devices, on_device(): gathered = lax.all_gather(jnp.concatenate([final, tail], 0), 'ctx')  24.6 us
    reshape x8, local copies, waits for them, and re-layouts, local_block(): jnp.einsum('hts,shp->thp', mix, x_heads, preferred_element_type=f32)  23.6 us
    dynamic_slice x24, local copies, waits for them, and re-layouts, on_device(): lax.scan(local_block, start_state, (x_blocks, b_blocks, c_blocks, step_bl...  22.5 us
    dot_general x8, matrix products, local_block(): gram = jnp.dot(c_now, b_now.T, preferred_element_type=f32)  18.8 us
  transfers between devices with their start and end apart: 4, of which 3 were waited for; matrix products, arithmetic and copies ran while one was open for 15% of the time, Pallas kernels for 0%

profile of v1, /device:TPU:30, one launch (start us, length us, event | category | flops | bytes accessed | tf_op | source)
XLA Modules:
  0.0 613.2 jit_solution(1693921439631359238)
XLA Ops:
  8.3 8.3 %all-to-all-start = ((bf16[256,16,16]{0,2,1:T(8,128)(2,1)}), bf16[256,16,16]{0,2,1:T(8,128)(2,1)S(1)}, u32[]{:S(2)}, u32[]{:S(2)}) async-start(bf16[256,16,16]{0,2,1:T(8,128)(2,1)} %bitcast), calls=%async_computation | async-start | bytes 262144 | tf_op jit(solution)/shard_map/all_to_all | solution.py:38
  16.6 7.7 %slice.70 = bf16[256,16384]{1,0:T(8,128)(2,1)} slice(bf16[256,20480]{1,0:T(8,128)(2,1)} %param.9), slice={[0:256], [0:16384]} | slice | bytes 16777216 | tf_op jit(solution)/shard_map/slice | solution.py:30
  26.7 11.9 %copy.70 = bf16[256,16384]{0,1:T(8,128)(2,1)} copy(bf16[256,16384]{1,0:T(8,128)(2,1)} %slice.70) | data formatting | bytes 16777216
  39.1 11.3 %pad_maximum_fusion.1 = bf16[256,16,1536]{0,2,1:T(8,128)(2,1)} fusion(bf16[256,16,256]{0,2,1:T(8,128)(2,1)S(1)} %bitcast.139, bf16[256,16,256]{0,2,1:T(8,128)(2,1)S(1)} %bitcast.140, bf16[256,16,1024]{0,2,1:T(8,128)(2,1)} %bitcast.137), kind=kLoop, calls=%fused_computation.45 | loop fusion | flops 37748736 | bytes 25165824 | tf_op jit(solution)/shard_map/concatenate | solution.py:34
  50.4 16.6 %copy.64 = bf16[256,16,1536]{2,0,1:T(8,128)(2,1)} copy(bf16[256,16,1536]{0,2,1:T(8,128)(2,1)} %pad_maximum_fusion.1) | data formatting | bytes 25165824 | tf_op jit(solution)/shard_map/concatenate | solution.py:34
  67.0 7.4 %all-to-all-start.1 = ((bf16[256,16,1536]{2,0,1:T(8,128)(2,1)}), bf16[256,16,1536]{2,0,1:T(8,128)(2,1)}, u32[]{:S(2)}, u32[]{:S(2)}) async-start(bf16[256,16,1536]{2,0,1:T(8,128)(2,1)} %copy.64), calls=%async_computation.1 | async-start | bytes 25165824 | tf_op jit(solution)/shard_map/all_to_all | solution.py:37
  79.0 9.1 %reduce-window.6 = f32[8,16,4,128]{3,1,2,0:T(8,128)S(1)} reduce-window(f32[8,16,4,128]{3,1,2,0:T(8,128)S(1)} %copy.57, f32[]{:T(128)} %constant.61.clone.1), window={size=1x1x1x128 pad=0_0x0_0x0_0x127_0}, to_apply=%region_0.1 | reduce-window | flops 8323072 | bytes 524292 | tf_op jit(solution)/shard_map/reduce-window
  89.5 168.6 %all-to-all-done.1 = bf16[256,16,1536]{2,0,1:T(8,128)(2,1)} async-done(((bf16[256,16,1536]{2,0,1:T(8,128)(2,1)}), bf16[256,16,1536]{2,0,1:T(8,128)(2,1)}, u32[]{:S(2)}, u32[]{:S(2)}) %all-to-all-start.1) | async-done | bytes 12582944 | tf_op jit(solution)/shard_map/all_to_all | solution.py:37
  263.9 27.2 %multiply_convert_fusion.3 = bf16[4096,1536]{1,0:T(8,128)(2,1)} fusion(bf16[4096,1536]{1,0:T(8,128)(2,1)} %bitcast.14, bf16[3,1536]{1,0:T(4,128)(2,1)S(1)} %collective-permute-done, f32[1536]{0:T(1024)S(1)} %pad_maximum_fusion.3, f32[1536]{0:T(1024)S(1)} %get-tuple-element.143, f32[1536]{0:T(1024)S(1)} %get-tuple-element.144, ...), kind=kLoop, calls=%fused_computation.38 | loop fusion | flops 163577856 | bytes 25205760 | tf_op jit(solution)/shard_map/convert_element_type | solution.py:63
  291.0 7.8 %slice.104 = bf16[4096,1024]{1,0:T(8,128)(2,1)} slice(bf16[4096,1536]{1,0:T(8,128)(2,1)} %multiply_convert_fusion.3), slice={[0:4096], [0:1024]} | slice | bytes 16777216 | tf_op jit(solution)/shard_map/slice | solution.py:69
  303.4 228.4 %while.13 = (s32[]{:T(128)}, f32[256,1024]{1,0:T(8,128)S(1)}, f32[8,512,1024]{2,1,0:T(8,128)}, f32[8,512,16]{1,2,0:T(8,128)}, bf16[8,512,256]{2,1,0:T(8,128)(2,1...) while((s32[]{:T(128)}, f32[256,1024]{1,0:T(8,128)S(1)}, ...), condition=%wide.region_3.4_spmd.clone, body=%wide.region_2.3_spmd.clone.sunk | while | flops 2576629760 | bytes 39816320 | solution.py:100
  309.4 7.1 %fusion.63 = f32[16,64,512]{2,1,0:T(8,128)} fusion(bf16[512,16,64]{0,2,1:T(8,128)(2,1)S(1)} %bitcast.132, f32[16,512]{1,0:T(8,128)S(1)} %get-tuple-element.238, f32[16,512]{1,0:T(8,128)S(1)} %get-tuple-element.239, f32[512,512]{1,0:T(8,128)} %fusion.62, pred[512,512]{1,0:T(8,128)(4,1)S(1)} %iota_compare_fusion.3), kind=kOutput, calls=%fused_computation.3.clone.1 | convolution fusion | flops 557842432 | bytes 4521984 | tf_op jit(solution)/shard_map/while/body/eval_jaxpr/hts,shp->thp/dot_general | solution.py:85
  323.4 5.2 fusion.64
  337.9 7.1 %fusion.63 = f32[16,64,512]{2,1,0:T(8,128)} fusion(bf16[512,16,64]{0,2,1:T(8,128)(2,1)S(1)} %bitcast.132, f32[16,512]{1,0:T(8,128)S(1)} %get-tuple-element.238, f32[16,512]{1,0:T(8,128)S(1)} %get-tuple-element.239, f32[512,512]{1,0:T(8,128)} %fusion.62, pred[512,512]{1,0:T(8,128)(4,1)S(1)} %iota_compare_fusion.3), kind=kOutput, calls=%fused_computation.3.clone.1 | convolution fusion | flops 557842432 | bytes 4521984 | tf_op jit(solution)/shard_map/while/body/eval_jaxpr/hts,shp->thp/dot_general | solution.py:85
  351.9 5.2 fusion.64
  366.4 7.1 %fusion.63 = f32[16,64,512]{2,1,0:T(8,128)} fusion(bf16[512,16,64]{0,2,1:T(8,128)(2,1)S(1)} %bitcast.132, f32[16,512]{1,0:T(8,128)S(1)} %get-tuple-element.238, f32[16,512]{1,0:T(8,128)S(1)} %get-tuple-element.239, f32[512,512]{1,0:T(8,128)} %fusion.62, pred[512,512]{1,0:T(8,128)(4,1)S(1)} %iota_compare_fusion.3), kind=kOutput, calls=%fused_computation.3.clone.1 | convolution fusion | flops 557842432 | bytes 4521984 | tf_op jit(solution)/shard_map/while/body/eval_jaxpr/hts,shp->thp/dot_general | solution.py:85
  380.4 5.2 fusion.64
  394.9 7.1 %fusion.63 = f32[16,64,512]{2,1,0:T(8,128)} fusion(bf16[512,16,64]{0,2,1:T(8,128)(2,1)S(1)} %bitcast.132, f32[16,512]{1,0:T(8,128)S(1)} %get-tuple-element.238, f32[16,512]{1,0:T(8,128)S(1)} %get-tuple-element.239, f32[512,512]{1,0:T(8,128)} %fusion.62, pred[512,512]{1,0:T(8,128)(4,1)S(1)} %iota_compare_fusion.3), kind=kOutput, calls=%fused_computation.3.clone.1 | convolution fusion | flops 557842432 | bytes 4521984 | tf_op jit(solution)/shard_map/while/body/eval_jaxpr/hts,shp->thp/dot_general | solution.py:85
  408.9 5.2 fusion.64
  423.5 7.1 %fusion.63 = f32[16,64,512]{2,1,0:T(8,128)} fusion(bf16[512,16,64]{0,2,1:T(8,128)(2,1)S(1)} %bitcast.132, f32[16,512]{1,0:T(8,128)S(1)} %get-tuple-element.238, f32[16,512]{1,0:T(8,128)S(1)} %get-tuple-element.239, f32[512,512]{1,0:T(8,128)} %fusion.62, pred[512,512]{1,0:T(8,128)(4,1)S(1)} %iota_compare_fusion.3), kind=kOutput, calls=%fused_computation.3.clone.1 | convolution fusion | flops 557842432 | bytes 4521984 | tf_op jit(solution)/shard_map/while/body/eval_jaxpr/hts,shp->thp/dot_general | solution.py:85
  437.5 5.3 fusion.64
  452.0 7.1 %fusion.63 = f32[16,64,512]{2,1,0:T(8,128)} fusion(bf16[512,16,64]{0,2,1:T(8,128)(2,1)S(1)} %bitcast.132, f32[16,512]{1,0:T(8,128)S(1)} %get-tuple-element.238, f32[16,512]{1,0:T(8,128)S(1)} %get-tuple-element.239, f32[512,512]{1,0:T(8,128)} %fusion.62, pred[512,512]{1,0:T(8,128)(4,1)S(1)} %iota_compare_fusion.3), kind=kOutput, calls=%fused_computation.3.clone.1 | convolution fusion | flops 557842432 | bytes 4521984 | tf_op jit(solution)/shard_map/while/body/eval_jaxpr/hts,shp->thp/dot_general | solution.py:85
  466.0 5.2 fusion.64
  480.5 7.1 %fusion.63 = f32[16,64,512]{2,1,0:T(8,128)} fusion(bf16[512,16,64]{0,2,1:T(8,128)(2,1)S(1)} %bitcast.132, f32[16,512]{1,0:T(8,128)S(1)} %get-tuple-element.238, f32[16,512]{1,0:T(8,128)S(1)} %get-tuple-element.239, f32[512,512]{1,0:T(8,128)} %fusion.62, pred[512,512]{1,0:T(8,128)(4,1)S(1)} %iota_compare_fusion.3), kind=kOutput, calls=%fused_computation.3.clone.1 | convolution fusion | flops 557842432 | bytes 4521984 | tf_op jit(solution)/shard_map/while/body/eval_jaxpr/hts,shp->thp/dot_general | solution.py:85
  494.5 5.3 fusion.64
  509.1 7.1 %fusion.63 = f32[16,64,512]{2,1,0:T(8,128)} fusion(bf16[512,16,64]{0,2,1:T(8,128)(2,1)S(1)} %bitcast.132, f32[16,512]{1,0:T(8,128)S(1)} %get-tuple-element.238, f32[16,512]{1,0:T(8,128)S(1)} %get-tuple-element.239, f32[512,512]{1,0:T(8,128)} %fusion.62, pred[512,512]{1,0:T(8,128)(4,1)S(1)} %iota_compare_fusion.3), kind=kOutput, calls=%fused_computation.3.clone.1 | convolution fusion | flops 557842432 | bytes 4521984 | tf_op jit(solution)/shard_map/while/body/eval_jaxpr/hts,shp->thp/dot_general | solution.py:85
  523.1 5.2 fusion.64
  533.1 7.9 %broadcast_in_dim.94 = f32[8,512,16,64]{1,3,2,0:T(8,128)} broadcast(f32[8,512,16]{1,2,0:T(8,128)S(1)} %add_exponential_fusion), dimensions={0,1,2} | broadcast | bytes 17039360 | tf_op jit(solution)/shard_map/broadcast_in_dim | solution.py:120
  541.0 16.7 %copy.66 = f32[8,512,1024]{2,1,0:T(8,128)} copy(f32[8,512,1024]{1,2,0:T(8,128)} %bitcast.134) | data formatting | bytes 33554432 | tf_op jit(solution)/shard_map/exp | solution.py:120
  557.7 24.6 %all-gather.3.cloned.1.call-done = f32[2112,1024]{1,0:T(8,128)} async-done(((f32[264,1024]{1,0:T(8,128)}), f32[2112,1024]{1,0:T(8,128)}) %all-gather.3.cloned.1.call-update) | async-done | bytes 8650768 | tf_op jit(solution)/shard_map/all_gather | solution.py:106
  584.6 4.6 fusion.29
  589.2 17.1 %add_convert_fusion = bf16[8,512,1024]{2,1,0:T(8,128)(2,1)} fusion(f32[8,512,1024]{2,1,0:T(8,128)} %get-tuple-element.58, f32[8,512,1024]{2,1,0:T(8,128)} %copy.66, bf16[8,512,256]{2,1,0:T(8,128)(2,1)} %bitcast.19, f32[256,1024]{1,0:T(8,128)S(1)} %fusion.29), kind=kOutput, calls=%fused_computation.41 | convolution fusion | flops 12897484800 | bytes 45088768 | tf_op jit(solution)/shard_map/bqn,nc->bqc/dot_general | solution.py:121
  (218 shorter events, 153.2 us)
Async XLA Ops:
  6.5 17.7 %slice-start = ((bf16[256,20480]{1,0:T(8,128)(2,1)}), bf16[256,4096]{1,0:T(8,128)(2,1)S(1)}, s32[]{:S(2)}) async-start(bf16[256,20480]{1,0:T(8,128)(2,1)} %param.9), calls=%async_computation.3 | async-start | bytes 4194304 | tf_op jit(solution)/shard_map/slice | solution.py:31
  8.3 58.6 %all-to-all-start = ((bf16[256,16,16]{0,2,1:T(8,128)(2,1)}), bf16[256,16,16]{0,2,1:T(8,128)(2,1)S(1)}, u32[]{:S(2)}, u32[]{:S(2)}) async-start(bf16[256,16,16]{0,2,1:T(8,128)(2,1)} %bitcast), calls=%async_computation | async-start | bytes 262144 | tf_op jit(solution)/shard_map/all_to_all | solution.py:38
  67.0 7.5 %copy-start.1 = (f32[256]{0:T(256)S(1)}, f32[256]{0:T(256)}, u32[]{:S(2)}) copy-start(f32[256]{0:T(256)} %param.14) | copy-start | bytes 3076
  67.0 7.6 %copy-start.2 = (f32[256]{0:T(256)S(1)}, f32[256]{0:T(256)}, u32[]{:S(2)}) copy-start(f32[256]{0:T(256)} %param.15) | copy-start | bytes 3076
  67.0 8.3 %copy-start.3 = (f32[256]{0:T(256)S(1)}, f32[256]{0:T(256)}, u32[]{:S(2)}) copy-start(f32[256]{0:T(256)} %param.13) | copy-start | bytes 3076
  67.0 191.1 %all-to-all-start.1 = ((bf16[256,16,1536]{2,0,1:T(8,128)(2,1)}), bf16[256,16,1536]{2,0,1:T(8,128)(2,1)}, u32[]{:S(2)}, u32[]{:S(2)}) async-start(bf16[256,16,1536]{2,0,1:T(8,128)(2,1)} %copy.64), calls=%async_computation.1 | async-start | bytes 25165824 | tf_op jit(solution)/shard_map/all_to_all | solution.py:37
  74.4 508.0 %all-gather.3.cloned.1.call-start = ((), (), s32[]{:S(2)}) async-start(), calls=%async_computation.2 | async-start | bytes 9732096 | tf_op jit(solution)/shard_map/all_gather | solution.py:106
  258.9 5.0 collective-permute-start
  309.3 7.2 %copy-start = (bf16[1,512,1024]{1,2,0:T(8,128)(2,1)}, bf16[1,512,1024]{1,2,0:T(8,128)(2,1)S(1)}, u32[]{:S(2)}) copy-start(bf16[1,512,1024]{1,2,0:T(8,128)(2,1)S(1)} %copy.86) | copy-start | bytes 3145732 | tf_op jit(solution)/shard_map/while
  337.8 7.2 %copy-start = (bf16[1,512,1024]{1,2,0:T(8,128)(2,1)}, bf16[1,512,1024]{1,2,0:T(8,128)(2,1)S(1)}, u32[]{:S(2)}) copy-start(bf16[1,512,1024]{1,2,0:T(8,128)(2,1)S(1)} %copy.86) | copy-start | bytes 3145732 | tf_op jit(solution)/shard_map/while
  366.3 7.2 %copy-start = (bf16[1,512,1024]{1,2,0:T(8,128)(2,1)}, bf16[1,512,1024]{1,2,0:T(8,128)(2,1)S(1)}, u32[]{:S(2)}) copy-start(bf16[1,512,1024]{1,2,0:T(8,128)(2,1)S(1)} %copy.86) | copy-start | bytes 3145732 | tf_op jit(solution)/shard_map/while
  394.8 7.2 %copy-start = (bf16[1,512,1024]{1,2,0:T(8,128)(2,1)}, bf16[1,512,1024]{1,2,0:T(8,128)(2,1)S(1)}, u32[]{:S(2)}) copy-start(bf16[1,512,1024]{1,2,0:T(8,128)(2,1)S(1)} %copy.86) | copy-start | bytes 3145732 | tf_op jit(solution)/shard_map/while
  423.4 7.2 %copy-start = (bf16[1,512,1024]{1,2,0:T(8,128)(2,1)}, bf16[1,512,1024]{1,2,0:T(8,128)(2,1)S(1)}, u32[]{:S(2)}) copy-start(bf16[1,512,1024]{1,2,0:T(8,128)(2,1)S(1)} %copy.86) | copy-start | bytes 3145732 | tf_op jit(solution)/shard_map/while
  452.0 7.2 %copy-start = (bf16[1,512,1024]{1,2,0:T(8,128)(2,1)}, bf16[1,512,1024]{1,2,0:T(8,128)(2,1)S(1)}, u32[]{:S(2)}) copy-start(bf16[1,512,1024]{1,2,0:T(8,128)(2,1)S(1)} %copy.86) | copy-start | bytes 3145732 | tf_op jit(solution)/shard_map/while
  480.4 7.2 %copy-start = (bf16[1,512,1024]{1,2,0:T(8,128)(2,1)}, bf16[1,512,1024]{1,2,0:T(8,128)(2,1)S(1)}, u32[]{:S(2)}) copy-start(bf16[1,512,1024]{1,2,0:T(8,128)(2,1)S(1)} %copy.86) | copy-start | bytes 3145732 | tf_op jit(solution)/shard_map/while
  509.0 7.2 %copy-start = (bf16[1,512,1024]{1,2,0:T(8,128)(2,1)}, bf16[1,512,1024]{1,2,0:T(8,128)(2,1)S(1)}, u32[]{:S(2)}) copy-start(bf16[1,512,1024]{1,2,0:T(8,128)(2,1)S(1)} %copy.86) | copy-start | bytes 3145732 | tf_op jit(solution)/shard_map/while
Sparse Core Ops, SparseCore 0:
  533.0 49.2 all-gather.2

commit v2 on v1

v2 whole, which is shorter than its diff:
```python
import jax
import jax.numpy as jnp
from jax import lax
from jax.sharding import PartitionSpec as P

HEADS = 256
HEADDIM = 64
STATE = 256
GROUPS = 8
CONV = 4
SPAN = 512


def on_device(conv_input, dt_raw, conv_weight, conv_bias, a_log, dt_bias, d_skip):
    f32 = jnp.float32
    head_count = lax.axis_size("head")
    ctx_count = lax.axis_size("ctx")
    heads_dev = HEADS // head_count
    repeat_count = head_count // GROUPS
    head_pos = lax.axis_index("head")
    rows = conv_input.shape[0]
    x_width = HEADS * HEADDIM
    slab = heads_dev * HEADDIM
    devices = ctx_count * head_count
    rim = lax.ppermute(
        conv_input[rows - (CONV - 1) :], ("ctx", "head"), [(i, i + 1) for i in range(devices - 1)]
    )
    padded = jnp.concatenate([rim, conv_input], 0)
    taps = conv_weight.astype(f32)
    total = padded[0:rows].astype(f32) * taps[0]
    for k in range(1, CONV):
        total = total + padded[k : k + rows].astype(f32) * taps[k]
    act = jax.nn.silu(total + conv_bias).astype(jnp.bfloat16)

    def payload(target):
        group = target // repeat_count
        return jnp.concatenate(
            [
                lax.dynamic_slice_in_dim(act, target * slab, slab, 1),
                lax.dynamic_slice_in_dim(act, x_width + group * STATE, STATE, 1),
                lax.dynamic_slice_in_dim(act, x_width + (GROUPS + group) * STATE, STATE, 1),
                lax.dynamic_slice_in_dim(dt_raw, target * heads_dev, heads_dev, 1),
            ],
            1,
        )

    rate = -jnp.exp(lax.dynamic_slice_in_dim(a_log, head_pos * heads_dev, heads_dev, 0))
    bias = lax.dynamic_slice_in_dim(dt_bias, head_pos * heads_dev, heads_dev, 0)
    skip = jnp.repeat(lax.dynamic_slice_in_dim(d_skip, head_pos * heads_dev, heads_dev, 0), HEADDIM)
    tri = lax.broadcasted_iota(jnp.int32, (SPAN, SPAN), 0) >= lax.broadcasted_iota(
        jnp.int32, (SPAN, SPAN), 1
    )
    pairs = head_count // 2
    blocks = pairs
    parity = head_pos % 2
    y_acc = jnp.zeros((blocks, SPAN, slab), f32)
    c_acc = jnp.zeros((blocks, SPAN, STATE), jnp.bfloat16)
    cum_acc = jnp.zeros((blocks, SPAN, heads_dev), f32)
    contrib_acc = jnp.zeros((blocks, STATE, slab), f32)
    done = []
    for m in range(blocks):
        same = [(i, 2 * ((i // 2 + m) % pairs) + i % 2) for i in range(head_count)]
        other = [(i, 2 * ((i // 2 + m) % pairs) + 1 - i % 2) for i in range(head_count)]
        t_same = 2 * ((head_pos // 2 + m) % pairs) + parity
        t_other = 2 * ((head_pos // 2 + m) % pairs) + 1 - parity
        p_same, p_other = payload(t_same), payload(t_other)
        if m >= 2:
            p_same, p_other, _ = lax.optimization_barrier((p_same, p_other, done[m - 2]))
        r_same = lax.ppermute(p_same, "head", same)
        r_other = lax.ppermute(p_other, "head", other)
        first = jnp.where(parity == 0, r_same, r_other)
        second = jnp.where(parity == 0, r_other, r_same)
        blk = jnp.concatenate([first, second], 0)
        k = (head_pos // 2 - m) % pairs
        x_now = blk[:, :slab]
        b_now = blk[:, slab : slab + STATE]
        c_now = blk[:, slab + STATE : slab + 2 * STATE]
        step_now = jax.nn.softplus(blk[:, slab + 2 * STATE :].astype(f32) + bias)
        cum_now = jnp.cumsum(rate * step_now, axis=0)
        gram = jnp.dot(c_now, b_now.T, preferred_element_type=f32)
        cum_t = cum_now.T
        decay = jnp.exp(jnp.where(tri[None], cum_t[:, :, None] - cum_t[:, None, :], -jnp.inf))
        mix = (gram[None] * decay * step_now.T[:, None, :]).astype(jnp.bfloat16)
        x_heads = x_now.reshape(SPAN, heads_dev, HEADDIM)
        y_block = jnp.einsum("hts,shp->thp", mix, x_heads, preferred_element_type=f32).reshape(
            SPAN, slab
        )
        y_now = y_block + skip * x_now.astype(f32)
        weight = jnp.exp(cum_now[-1][None, :] - cum_now) * step_now
        xw = (x_heads.astype(f32) * weight[:, :, None]).astype(jnp.bfloat16).reshape(SPAN, slab)
        contrib = jnp.einsum("sn,sc->nc", b_now, xw, preferred_element_type=f32)
        y_acc = lax.dynamic_update_index_in_dim(y_acc, y_now, k, 0)
        c_acc = lax.dynamic_update_index_in_dim(c_acc, c_now, k, 0)
        cum_acc = lax.dynamic_update_index_in_dim(cum_acc, cum_now, k, 0)
        contrib_acc = lax.dynamic_update_index_in_dim(contrib_acc, contrib, k, 0)
        done.append((contrib, y_now))

    block_totals = cum_acc[:, -1, :]
    state = jnp.zeros((STATE, slab), f32)
    entering = []
    for k in range(blocks):
        entering.append(state)
        fade = jnp.exp(jnp.repeat(block_totals[k], HEADDIM))
        state = state * fade[None, :] + contrib_acc[k]
    final = state
    entering = jnp.stack(entering)
    totals = jnp.sum(block_totals, axis=0)
    tail = jnp.broadcast_to(jnp.repeat(totals, HEADDIM)[None, :], (8, slab))
    gathered = lax.all_gather(jnp.concatenate([final, tail], 0), "ctx")
    shards = gathered.shape[0]
    position = lax.axis_index("ctx")
    finals = gathered[:, :STATE]
    shard_totals = gathered[:, STATE]
    before_shard = jnp.cumsum(shard_totals, axis=0) - shard_totals
    reach = jnp.sum(jnp.where(jnp.arange(shards)[:, None] < position, shard_totals, 0.0), axis=0)
    after_own = before_shard + shard_totals
    live = jnp.arange(shards)[:, None] < position
    weights = jnp.where(live, jnp.exp(jnp.where(live, reach[None] - after_own, 0.0)), 0.0)
    incoming = jnp.sum(weights[:, None, :] * finals, axis=0)
    before = jnp.concatenate(
        [jnp.zeros((1, heads_dev), f32), jnp.cumsum(block_totals, axis=0)[:-1]], 0
    )
    carried = jnp.exp(jnp.repeat(before, HEADDIM, axis=1))[:, None, :] * incoming[None]
    full_state = entering + carried
    grown = jnp.exp(jnp.repeat(cum_acc, HEADDIM, axis=2))
    y_state = grown * jnp.einsum(
        "bqn,bnc->bqc", c_acc.astype(f32), full_state, precision=lax.Precision.HIGHEST
    )
    result = y_acc + y_state
    return result.astype(jnp.bfloat16).reshape(blocks * SPAN, slab)


def solution(mesh):
    placed = (P(("ctx", "head"), None), P(("ctx", "head"), None), P(), P(), P(), P(), P())
    return jax.shard_map(
        on_device, mesh=mesh, in_specs=placed, out_specs=P("ctx", "head"), check_vma=False
    )
```

time: 621 us -> 592 us (0.953)
  matrix products: 147 us -> 86.6 us
  other arithmetic: 76.7 us -> 123 us
  local copies, waits for them, and re-layouts: 162 us -> 139 us
  starting transfers between devices: 17.8 us -> 36.8 us
  waiting for transfers between devices: 195 us -> 181 us
    ppermute x1 -> x17, waiting for transfers between devices: 1.65 us -> 181 us  [the longest x8 115 us: on_device(): r_same = lax.ppermute(p_same, 'head', same)]
    all_to_all x2 -> x0, waiting for transfers between devices: 169 us -> none  [the longest x1 169 us: on_device(): lax.all_to_all(send, 'head', split_axis=1, concat_axis=0, tiled=True)]
    dot_general x33 -> x25, matrix products: 147 us -> 86.6 us  [the longest x8 39.7 us: on_device(): jnp.einsum('hts,shp->thp', mix, x_heads, preferred_element_type=f32)]
    broadcast_in_dim x19 -> x30, local copies, waits for them, and re-layouts: 10.9 us -> 52.4 us  [the longest x8 23.1 us: on_device(): y_acc = lax.dynamic_update_index_in_dim(y_acc, y_now, k, 0)]
    reshape x17 -> x1, local copies, waits for them, and re-layouts: 38.3 us -> 0.01 us  [the longest x8 23.6 us: local_block(): jnp.einsum('hts,shp->thp', mix, x_heads, preferred_element_type=f32)]
    ppermute x1 -> x17, starting transfers between devices: 2.1 us -> 36.8 us  [the longest x8 22.3 us: on_device(): r_same = lax.ppermute(p_same, 'head', same)]
    dynamic_update_slice x0 -> x19, local copies, waits for them, and re-layouts: none -> 26.4 us  [the longest x8 17.5 us: on_device(): y_acc = lax.dynamic_update_index_in_dim(y_acc, y_now, k, 0)]
    slice x17 -> x11, local copies, waits for them, and re-layouts: 28.2 us -> 2.92 us  [the longest x8 1.49 us: on_device(): weight = jnp.exp(cum_now[-1][None, :] - cum_now) * step_now]
  transfers between devices with their start and end apart: 4 -> 18, of which waited for: 3 -> 11; matrix products, arithmetic and copies ran while one was open for 15% -> 32% of each run, Pallas kernels for 0% -> 0%
where the time goes in v2:
time: 592 us; the launch traced here: 582 us
  waiting for transfers between devices  181 us (31%)
  local copies, waits for them, and re-layouts  139 us (23%)
  other arithmetic  123 us (21%)
  matrix products  86.6 us (15%)
  starting transfers between devices  36.8 us (6%)
  between operations  15.7 us (3%)
    ppermute x8, waiting for transfers between devices, on_device(): r_same = lax.ppermute(p_same, 'head', same)  115 us
    ppermute x8, waiting for transfers between devices, on_device(): r_other = lax.ppermute(p_other, 'head', other)  65.9 us
    dot_general x8, matrix products, on_device(): jnp.einsum('hts,shp->thp', mix, x_heads, preferred_element_type=f32)  39.7 us
    convert_element_type x1, other arithmetic, on_device(): act = jax.nn.silu(total + conv_bias).astype(jnp.bfloat16)  36.7 us
    unnamed x293, local copies, waits for them, and re-layouts  27.1 us
    dot_general x1, matrix products, on_device(): jnp.einsum('bqn,bnc->bqc', c_acc.astype(f32), full_state, precision=lax.P...  23.9 us
    broadcast_in_dim x8, local copies, waits for them, and re-layouts, on_device(): y_acc = lax.dynamic_update_index_in_dim(y_acc, y_now, k, 0)  23.1 us
    ppermute x8, starting transfers between devices, on_device(): r_same = lax.ppermute(p_same, 'head', same)  22.3 us
  transfers between devices with their start and end apart: 18, of which 11 were waited for; matrix products, arithmetic and copies ran while one was open for 32% of the time, Pallas kernels for 0%

profile of v2, /device:TPU:30, one launch (start us, length us, event | category | flops | bytes accessed | tf_op | source)
XLA Modules:
  0.0 581.7 jit_solution(3510361340544848762)
XLA Ops:
  7.6 3.7 collective-permute-start
  11.7 13.8 %copy.474 = bf16[256,20480]{0,1:T(8,128)(2,1)} copy(bf16[256,20480]{1,0:T(8,128)(2,1)} %param.7) | data formatting | bytes 20971520 | tf_op args[0]
  33.6 3.6 copy.473
  37.2 36.7 %multiply_convert_fusion = bf16[256,20480]{0,1:T(8,128)(2,1)S(1)} fusion(bf16[256,20480]{0,1:T(8,128)(2,1)} %copy.474, bf16[3,20480]{0,1:T(8,128)(2,1)} %copy.473, f32[20480]{0:T(1024)S(1)} %copy-done.103, f32[20480]{0:T(1024)S(1)} %bitcast.409, f32[20480]{0:T(1024)S(1)} %bitcast.408, f32[20480]{0:T(1024)S(1)} %bitcast.407, f32[20480]{0:T(1024)S(1)} %bitcast.406), kind=kLoop, calls=%fused_computation | loop fusion | flops 136314880 | bytes 21504000 | tf_op jit(solution)/shard_map/convert_element_type | solution.py:33
  82.4 7.2 %collective-permute-start.1 = (bf16[256,1552]{0,1:T(8,128)(2,1)}, bf16[256,1552]{0,1:T(8,128)(2,1)}, u32[]{:S(2)}, u32[]{:S(2)}) collective-permute-start(bf16[256,1552]{0,1:T(8,128)(2,1)} %pad_maximum_fusion.2), channel_id=1, source_target_pairs={{0,0},{1,1},{2,2},{3,3},{4,4},{5,5},{6,6},{7,7},{8,8},{9,9},{10,10... | collective-permute-start | bytes 2383880 | tf_op jit(solution)/shard_map/ppermute | solution.py:69
  93.4 4.4 collective-permute-done.3
  97.7 16.9 %collective-permute-done.4 = bf16[256,1552]{0,1:T(8,128)(2,1)S(1)} collective-permute-done((bf16[256,1552]{0,1:T(8,128)(2,1)S(1)}, bf16[256,1552]{0,1:T(8,128)(2,1)S(1)}, u32[]{:S(2)}, u32[]{:S(2)}) %collective-permute-start.4) | collective-permute-done | bytes 794656 | tf_op jit(solution)/shard_map/ppermute | solution.py:70
  119.9 4.9 fusion.6
  126.5 5.3 collective-permute-start.7
  136.5 14.3 %collective-permute-done.7 = bf16[256,1552]{0,1:T(8,128)(2,1)S(1)} collective-permute-done((bf16[256,1552]{0,1:T(8,128)(2,1)S(1)}, bf16[256,1552]{0,1:T(8,128)(2,1)S(1)}, u32[]{:S(2)}, u32[]{:S(2)}) %collective-permute-start.7) | collective-permute-done | bytes 794656 | tf_op jit(solution)/shard_map/ppermute | solution.py:69
  150.8 16.0 %collective-permute-done.8 = bf16[256,1552]{0,1:T(8,128)(2,1)S(1)} collective-permute-done((bf16[256,1552]{0,1:T(8,128)(2,1)S(1)}, bf16[256,1552]{0,1:T(8,128)(2,1)S(1)}, u32[]{:S(2)}, u32[]{:S(2)}) %collective-permute-start.8) | collective-permute-done | bytes 794656 | tf_op jit(solution)/shard_map/ppermute | solution.py:70
  170.9 4.9 fusion.8
  188.5 14.2 %collective-permute-done.11 = bf16[256,1552]{0,1:T(8,128)(2,1)S(1)} collective-permute-done((bf16[256,1552]{0,1:T(8,128)(2,1)S(1)}, bf16[256,1552]{0,1:T(8,128)(2,1)S(1)}, u32[]{:S(2)}, u32[]{:S(2)}) %collective-permute-start.11) | collective-permute-done | bytes 794656 | tf_op jit(solution)/shard_map/ppermute | solution.py:69
  202.6 16.9 %collective-permute-done.12 = bf16[256,1552]{0,1:T(8,128)(2,1)S(1)} collective-permute-done((bf16[256,1552]{0,1:T(8,128)(2,1)S(1)}, bf16[256,1552]{0,1:T(8,128)(2,1)S(1)}, u32[]{:S(2)}, u32[]{:S(2)}) %collective-permute-start.12) | collective-permute-done | bytes 794656 | tf_op jit(solution)/shard_map/ppermute | solution.py:70
  230.1 5.0 fusion.10
  235.1 5.0 fusion.5
  246.5 4.5 broadcast_in_dim.348
  255.1 10.6 %collective-permute-done.15 = bf16[256,1552]{0,1:T(8,128)(2,1)S(1)} collective-permute-done((bf16[256,1552]{0,1:T(8,128)(2,1)S(1)}, bf16[256,1552]{0,1:T(8,128)(2,1)S(1)}, u32[]{:S(2)}, u32[]{:S(2)}) %collective-permute-start.15) | collective-permute-done | bytes 794656 | tf_op jit(solution)/shard_map/ppermute | solution.py:69
  265.7 16.0 %collective-permute-done.16 = bf16[256,1552]{0,1:T(8,128)(2,1)S(1)} collective-permute-done((bf16[256,1552]{0,1:T(8,128)(2,1)S(1)}, bf16[256,1552]{0,1:T(8,128)(2,1)S(1)}, u32[]{:S(2)}, u32[]{:S(2)}) %collective-permute-start.16) | collective-permute-done | bytes 794656 | tf_op jit(solution)/shard_map/ppermute | solution.py:70
  283.3 6.4 %collective-permute-done.5 = bf16[256,1552]{0,1:T(8,128)(2,1)S(1)} collective-permute-done((bf16[256,1552]{0,1:T(8,128)(2,1)S(1)}, bf16[256,1552]{0,1:T(8,128)(2,1)S(1)}, u32[]{:S(2)}, u32[]{:S(2)}) %collective-permute-start.5) | collective-permute-done | bytes 794656 | tf_op jit(solution)/shard_map/ppermute | solution.py:69
  298.0 5.0 fusion.12
  303.1 5.0 fusion.7
  316.7 32.1 %collective-permute-done.9 = bf16[256,1552]{0,1:T(8,128)(2,1)S(1)} collective-permute-done((bf16[256,1552]{0,1:T(8,128)(2,1)S(1)}, bf16[256,1552]{0,1:T(8,128)(2,1)S(1)}, u32[]{:S(2)}, u32[]{:S(2)}) %collective-permute-start.9) | collective-permute-done | bytes 794656 | tf_op jit(solution)/shard_map/ppermute | solution.py:69
  359.5 4.9 fusion.9
  370.3 32.8 %collective-permute-done.13 = bf16[256,1552]{0,1:T(8,128)(2,1)S(1)} collective-permute-done((bf16[256,1552]{0,1:T(8,128)(2,1)S(1)}, bf16[256,1552]{0,1:T(8,128)(2,1)S(1)}, u32[]{:S(2)}, u32[]{:S(2)}) %collective-permute-start.13) | collective-permute-done | bytes 794656 | tf_op jit(solution)/shard_map/ppermute | solution.py:69
  418.7 4.4 fusion.56
  447.6 8.1 %broadcast_in_dim.315 = f32[8,512,1024]{2,1,0:T(8,128)} broadcast(f32[]{:T(128)} %constant.425.clone.1), dimensions={} | broadcast | bytes 16777220 | tf_op jit(solution)/shard_map/broadcast_in_dim | solution.py:56
  485.4 4.9 fusion.11
  494.8 8.0 %broadcast_in_dim.336 = f32[8,512,16,64]{1,3,2,0:T(8,128)} broadcast(f32[8,512,16]{1,2,0:T(8,128)S(1)} %exp.234), dimensions={0,1,2} | broadcast | bytes 17039360 | tf_op jit(solution)/shard_map/broadcast_in_dim | solution.py:125
  502.8 16.4 %copy.524 = f32[8,512,1024]{2,1,0:T(8,128)} copy(f32[8,512,1024]{1,2,0:T(8,128)} %bitcast.388) | data formatting | bytes 33554432 | tf_op jit(solution)/shard_map/exp | solution.py:125
  546.1 4.6 fusion.2
  550.7 23.9 %add_convert_fusion = bf16[8,512,1024]{2,1,0:T(8,128)(2,1)} fusion(f32[8,512,1024]{2,1,0:T(8,128)} %constant_dynamic-update-slice_fusion.8, f32[8,512,1024]{2,1,0:T(8,128)} %copy.524, bf16[8,512,256]{2,1,0:T(8,128)(2,1)} %constant_dynamic-update-slice_fusion, f32[8,256,1024]{2,1,0:T(8,128)} %add_dynamic-update-slice_fusion, f32[256,1024]{1,0:T(8,128)S(1)} %fusion.2, ...), kind=kOutput, calls=%fused_computation.3 | convolution fusion | flops 12901679104 | bytes 53510144 | tf_op jit(solution)/shard_map/bqn,bnc->bqc/dot_general | solution.py:126
  (536 shorter events, 205.5 us)
Async XLA Ops:
  6.5 537.3 %all-gather.3.cloned.1.call-start = ((), (), s32[]{:S(2)}) async-start(), calls=%async_computation | async-start | bytes 9732096 | tf_op jit(solution)/shard_map/all_gather | solution.py:109
  7.6 26.0 %collective-permute-start = (bf16[3,20480]{1,0:T(4,128)(2,1)S(1)}, bf16[3,20480]{1,0:T(4,128)(2,1)S(1)}, u32[]{:S(2)}, u32[]{:S(2)}) collective-permute-start(bf16[3,20480]{1,0:T(4,128)(2,1)S(1)} %slice.268), channel_id=1, source_target_pairs={{0,1},{1,2},{2,3},{3,4},{4,5},{5,6},{6,7},{7,8},{8,9},{9,10},{10,1... | collective-permute-start | bytes 368648 | tf_op jit(solution)/shard_map/ppermute | solution.py:25
  11.6 14.0 %copy-start.38 = (bf16[256,256]{1,0:T(8,128)(2,1)S(1)}, bf16[256,256]{1,0:T(8,128)(2,1)}, u32[]{:S(2)}) copy-start(bf16[256,256]{1,0:T(8,128)(2,1)} %param.8) | copy-start | bytes 393220
  25.5 90.7 %copy-start.119 = (f32[16]{0:T(128)}, f32[16]{0:T(128)S(1)}, u32[]{:S(2)}) copy-start(f32[16]{0:T(128)S(1)} %exponential_negate_fusion) | copy-start | bytes 196
  25.6 90.7 %copy-start.124 = (f32[16]{0:T(128)}, f32[16]{0:T(128)S(1)}, u32[]{:S(2)}) copy-start(f32[16]{0:T(128)S(1)} %dynamic_slice.210) | copy-start | bytes 196
  76.9 20.8 %collective-permute-start.3 = (bf16[256,1552]{0,1:T(8,128)(2,1)S(1)}, bf16[256,1552]{0,1:T(8,128)(2,1)S(1)}, u32[]{:S(2)}, u32[]{:S(2)}) collective-permute-start(bf16[256,1552]{0,1:T(8,128)(2,1)S(1)} %pad_maximum_fusion.4), channel_id=1, source_target_pairs={{0,2},{1,3},{2,4},{3,5},{4,6},{5,7},{6,8},{7,9},{8,10},{9,11},{10,... | collective-permute-start | bytes 2383880 | tf_op jit(solution)/shard_map/ppermute | solution.py:69
  79.4 35.2 %collective-permute-start.4 = (bf16[256,1552]{0,1:T(8,128)(2,1)S(1)}, bf16[256,1552]{0,1:T(8,128)(2,1)S(1)}, u32[]{:S(2)}, u32[]{:S(2)}) collective-permute-start(bf16[256,1552]{0,1:T(8,128)(2,1)S(1)} %pad_maximum_fusion.5), channel_id=1, source_target_pairs={{0,3},{1,2},{2,5},{3,4},{4,7},{5,6},{6,9},{7,8},{8,11},{9,10},{10,... | collective-permute-start | bytes 2383880 | tf_op jit(solution)/shard_map/ppermute | solution.py:70
  82.4 103.0 %collective-permute-start.1 = (bf16[256,1552]{0,1:T(8,128)(2,1)}, bf16[256,1552]{0,1:T(8,128)(2,1)}, u32[]{:S(2)}, u32[]{:S(2)}) collective-permute-start(bf16[256,1552]{0,1:T(8,128)(2,1)} %pad_maximum_fusion.2), channel_id=1, source_target_pairs={{0,0},{1,1},{2,2},{3,3},{4,4},{5,5},{6,6},{7,7},{8,8},{9,9},{10,10... | collective-permute-start | bytes 2383880 | tf_op jit(solution)/shard_map/ppermute | solution.py:69
  126.5 24.2 %collective-permute-start.7 = (bf16[256,1552]{0,1:T(8,128)(2,1)S(1)}, bf16[256,1552]{0,1:T(8,128)(2,1)S(1)}, u32[]{:S(2)}, u32[]{:S(2)}) collective-permute-start(bf16[256,1552]{0,1:T(8,128)(2,1)S(1)} %copy-done.75), channel_id=1, source_target_pairs={{0,6},{1,7},{2,8},{3,9},{4,10},{5,11},{6,12},{7,13},{8,14},{9,15},... | collective-permute-start | bytes 2383880 | tf_op jit(solution)/shard_map/ppermute | solution.py:69
  131.8 35.0 %collective-permute-start.8 = (bf16[256,1552]{0,1:T(8,128)(2,1)S(1)}, bf16[256,1552]{0,1:T(8,128)(2,1)S(1)}, u32[]{:S(2)}, u32[]{:S(2)}) collective-permute-start(bf16[256,1552]{0,1:T(8,128)(2,1)S(1)} %copy-done.77), channel_id=1, source_target_pairs={{0,7},{1,6},{2,9},{3,8},{4,11},{5,10},{6,13},{7,12},{8,15},{9,14},... | collective-permute-start | bytes 2383880 | tf_op jit(solution)/shard_map/ppermute | solution.py:70
  133.6 51.8 %collective-permute-start.2 = (bf16[256,1552]{0,1:T(8,128)(2,1)}, bf16[256,1552]{0,1:T(8,128)(2,1)}, u32[]{:S(2)}, u32[]{:S(2)}) collective-permute-start(bf16[256,1552]{0,1:T(8,128)(2,1)} %pad_maximum_fusion.3), channel_id=1, source_target_pairs={{0,1},{1,0},{2,3},{3,2},{4,5},{5,4},{6,7},{7,6},{8,9},{9,8},{10,11... | collective-permute-start | bytes 2383880 | tf_op jit(solution)/shard_map/ppermute | solution.py:70
  136.5 30.4 %copy-start.120 = (f32[16]{0:T(128)S(1)}, f32[16]{0:T(128)}, u32[]{:S(2)}) copy-start(f32[16]{0:T(128)} %copy-done.119) | copy-start | bytes 196
  136.5 30.4 %copy-start.125 = (f32[16]{0:T(128)S(1)}, f32[16]{0:T(128)}, u32[]{:S(2)}) copy-start(f32[16]{0:T(128)} %copy-done.124) | copy-start | bytes 196
  179.0 23.6 %collective-permute-start.11 = (bf16[256,1552]{0,1:T(8,128)(2,1)S(1)}, bf16[256,1552]{0,1:T(8,128)(2,1)S(1)}, u32[]{:S(2)}, u32[]{:S(2)}) collective-permute-start(bf16[256,1552]{0,1:T(8,128)(2,1)S(1)} %copy-done.76), channel_id=1, source_target_pairs={{0,10},{1,11},{2,12},{3,13},{4,14},{5,15},{6,0},{7,1},{8,2},{9,3},... | collective-permute-start | bytes 2383880 | tf_op jit(solution)/shard_map/ppermute | solution.py:69
  182.4 37.1 %collective-permute-start.12 = (bf16[256,1552]{0,1:T(8,128)(2,1)S(1)}, bf16[256,1552]{0,1:T(8,128)(2,1)S(1)}, u32[]{:S(2)}, u32[]{:S(2)}) collective-permute-start(bf16[256,1552]{0,1:T(8,128)(2,1)S(1)} %copy-done.78), channel_id=1, source_target_pairs={{0,11},{1,10},{2,13},{3,12},{4,15},{5,14},{6,1},{7,0},{8,3},{9,2},... | collective-permute-start | bytes 2383880 | tf_op jit(solution)/shard_map/ppermute | solution.py:70
  186.9 32.8 %copy-start.8 = (bf16[256,1552]{0,1:T(8,128)(2,1)}, bf16[256,1552]{0,1:T(8,128)(2,1)S(1)}, u32[]{:S(2)}) copy-start(bf16[256,1552]{0,1:T(8,128)(2,1)S(1)} %get-tuple-element.139) | copy-start | bytes 2383876
  186.9 32.8 %copy-start.10 = (bf16[256,1552]{0,1:T(8,128)(2,1)}, bf16[256,1552]{0,1:T(8,128)(2,1)S(1)}, u32[]{:S(2)}) copy-start(bf16[256,1552]{0,1:T(8,128)(2,1)S(1)} %get-tuple-element.140) | copy-start | bytes 2383876
  188.5 31.2 %copy-start.121 = (f32[16]{0:T(128)S(1)}, f32[16]{0:T(128)}, u32[]{:S(2)}) copy-start(f32[16]{0:T(128)} %copy-done.119) | copy-start | bytes 196
  188.5 31.3 %copy-start.126 = (f32[16]{0:T(128)S(1)}, f32[16]{0:T(128)}, u32[]{:S(2)}) copy-start(f32[16]{0:T(128)} %copy-done.124) | copy-start | bytes 196
  242.7 23.0 %collective-permute-start.15 = (bf16[256,1552]{0,1:T(8,128)(2,1)S(1)}, bf16[256,1552]{0,1:T(8,128)(2,1)S(1)}, u32[]{:S(2)}, u32[]{:S(2)}) collective-permute-start(bf16[256,1552]{0,1:T(8,128)(2,1)S(1)} %copy-done.74), channel_id=1, source_target_pairs={{0,14},{1,15},{2,0},{3,1},{4,2},{5,3},{6,4},{7,5},{8,6},{9,7},{10,... | collective-permute-start | bytes 2383880 | tf_op jit(solution)/shard_map/ppermute | solution.py:69
  244.5 37.2 %collective-permute-start.16 = (bf16[256,1552]{0,1:T(8,128)(2,1)S(1)}, bf16[256,1552]{0,1:T(8,128)(2,1)S(1)}, u32[]{:S(2)}, u32[]{:S(2)}) collective-permute-start(bf16[256,1552]{0,1:T(8,128)(2,1)S(1)} %copy-done.73), channel_id=1, source_target_pairs={{0,15},{1,14},{2,1},{3,0},{4,3},{5,2},{6,5},{7,4},{8,7},{9,6},{10,... | collective-permute-start | bytes 2383880 | tf_op jit(solution)/shard_map/ppermute | solution.py:70
  252.4 37.3 %collective-permute-start.5 = (bf16[256,1552]{0,1:T(8,128)(2,1)S(1)}, bf16[256,1552]{0,1:T(8,128)(2,1)S(1)}, u32[]{:S(2)}, u32[]{:S(2)}) collective-permute-start(bf16[256,1552]{0,1:T(8,128)(2,1)S(1)} %get-tuple-element.17), channel_id=1, source_target_pairs={{0,4},{1,5},{2,6},{3,7},{4,8},{5,9},{6,10},{7,11},{8,12},{9,13},{1... | collective-permute-start | bytes 2383880 | tf_op jit(solution)/shard_map/ppermute | solution.py:69
  253.2 36.5 %collective-permute-start.6 = (bf16[256,1552]{0,1:T(8,128)(2,1)S(1)}, bf16[256,1552]{0,1:T(8,128)(2,1)S(1)}, u32[]{:S(2)}, u32[]{:S(2)}) collective-permute-start(bf16[256,1552]{0,1:T(8,128)(2,1)S(1)} %get-tuple-element.18), channel_id=1, source_target_pairs={{0,5},{1,4},{2,7},{3,6},{4,9},{5,8},{6,11},{7,10},{8,13},{9,12},{1... | collective-permute-start | bytes 2383880 | tf_op jit(solution)/shard_map/ppermute | solution.py:70
  281.8 135.4 %copy-start.12 = (bf16[256,1552]{0,1:T(8,128)(2,1)}, bf16[256,1552]{0,1:T(8,128)(2,1)S(1)}, u32[]{:S(2)}) copy-start(bf16[256,1552]{0,1:T(8,128)(2,1)S(1)} %get-tuple-element.125) | copy-start | bytes 2383876
  281.9 135.4 %copy-start.14 = (bf16[256,1552]{0,1:T(8,128)(2,1)}, bf16[256,1552]{0,1:T(8,128)(2,1)S(1)}, u32[]{:S(2)}) copy-start(bf16[256,1552]{0,1:T(8,128)(2,1)S(1)} %get-tuple-element.126) | copy-start | bytes 2383876
  312.1 36.8 %collective-permute-start.9 = (bf16[256,1552]{0,1:T(8,128)(2,1)S(1)}, bf16[256,1552]{0,1:T(8,128)(2,1)S(1)}, u32[]{:S(2)}, u32[]{:S(2)}) collective-permute-start(bf16[256,1552]{0,1:T(8,128)(2,1)S(1)} %copy-done.69), channel_id=1, source_target_pairs={{0,8},{1,9},{2,10},{3,11},{4,12},{5,13},{6,14},{7,15},{8,0},{9,1},... | collective-permute-start | bytes 2383880 | tf_op jit(solution)/shard_map/ppermute | solution.py:69
  312.5 36.4 %collective-permute-start.10 = (bf16[256,1552]{0,1:T(8,128)(2,1)S(1)}, bf16[256,1552]{0,1:T(8,128)(2,1)S(1)}, u32[]{:S(2)}, u32[]{:S(2)}) collective-permute-start(bf16[256,1552]{0,1:T(8,128)(2,1)S(1)} %copy-done.71), channel_id=1, source_target_pairs={{0,9},{1,8},{2,11},{3,10},{4,13},{5,12},{6,15},{7,14},{8,1},{9,0},... | collective-permute-start | bytes 2383880 | tf_op jit(solution)/shard_map/ppermute | solution.py:70
  316.7 32.3 %copy-start.123 = (f32[16]{0:T(128)S(1)}, f32[16]{0:T(128)}, u32[]{:S(2)}) copy-start(f32[16]{0:T(128)} %copy-done.119) | copy-start | bytes 196
  316.7 32.3 %copy-start.128 = (f32[16]{0:T(128)S(1)}, f32[16]{0:T(128)}, u32[]{:S(2)}) copy-start(f32[16]{0:T(128)} %copy-done.124) | copy-start | bytes 196
  367.6 35.5 %collective-permute-start.13 = (bf16[256,1552]{0,1:T(8,128)(2,1)S(1)}, bf16[256,1552]{0,1:T(8,128)(2,1)S(1)}, u32[]{:S(2)}, u32[]{:S(2)}) collective-permute-start(bf16[256,1552]{0,1:T(8,128)(2,1)S(1)} %copy-done.70), channel_id=1, source_target_pairs={{0,12},{1,13},{2,14},{3,15},{4,0},{5,1},{6,2},{7,3},{8,4},{9,5},{1... | collective-permute-start | bytes 2383880 | tf_op jit(solution)/shard_map/ppermute | solution.py:69
  368.5 34.6 %collective-permute-start.14 = (bf16[256,1552]{0,1:T(8,128)(2,1)S(1)}, bf16[256,1552]{0,1:T(8,128)(2,1)S(1)}, u32[]{:S(2)}, u32[]{:S(2)}) collective-permute-start(bf16[256,1552]{0,1:T(8,128)(2,1)S(1)} %copy-done.72), channel_id=1, source_target_pairs={{0,13},{1,12},{2,15},{3,14},{4,1},{5,0},{6,3},{7,2},{8,5},{9,4},{1... | collective-permute-start | bytes 2383880 | tf_op jit(solution)/shard_map/ppermute | solution.py:70
  370.3 37.8 %copy-start.64 = (f32[16,4,128]{2,0,1:T(8,128)S(1)}, f32[16,4,128]{2,0,1:T(8,128)}, u32[]{:S(2)}) copy-start(f32[16,4,128]{2,0,1:T(8,128)} %copy-done.63) | copy-start | bytes 98308
  (123 other events, 504.3 us)
Sparse Core Ops, SparseCore 0:
  424.4 49.1 all-gather.2

commit v3 on v1

v3 whole, which is shorter than its diff:
```python
import jax
import jax.numpy as jnp
from jax import lax
from jax.sharding import PartitionSpec as P

HEADS = 256
HEADDIM = 64
STATE = 256
GROUPS = 8
CONV = 4
SPAN = 512
CHUNKS = 4


def shifted(value, axis, by):
    size = lax.axis_size(axis)
    pairs = [(i, i + by) for i in range(size) if 0 <= i + by < size]
    return lax.ppermute(value, axis, pairs)


def convolve(local, kernel, offset):
    length = local.shape[0]
    rim = shifted(local[length - (CONV - 1) :], "ctx", 1)
    padded = jnp.concatenate([rim, local], 0)
    total = padded[0:length].astype(jnp.float32) * kernel[0]
    for k in range(1, CONV):
        total = total + padded[k : k + length].astype(jnp.float32) * kernel[k]
    return jax.nn.silu(total + offset).astype(jnp.bfloat16)


def on_device(conv_input, dt_raw, conv_weight, conv_bias, a_log, dt_bias, d_skip):
    f32 = jnp.float32
    head_count = lax.axis_size("head")
    heads_dev = HEADS // head_count
    repeat_count = head_count // GROUPS
    head_pos = lax.axis_index("head")
    group = head_pos // repeat_count
    rows = conv_input.shape[0]
    x_width = HEADS * HEADDIM
    slab = heads_dev * HEADDIM
    part_heads = heads_dev // CHUNKS
    part = part_heads * HEADDIM
    x_part = conv_input[:, :x_width].reshape(rows, head_count, slab)
    bc = conv_input[:, x_width:].reshape(rows, 2, GROUPS, STATE)
    b_part = jnp.repeat(bc[:, 0], repeat_count, axis=1)
    c_part = jnp.repeat(bc[:, 1], repeat_count, axis=1)
    step_part = dt_raw.reshape(rows, head_count, heads_dev)
    steps = lax.all_to_all(step_part, "head", split_axis=1, concat_axis=0, tiled=True)
    length = steps.shape[0]
    steps = steps.reshape(length, heads_dev)
    sends = [jnp.concatenate([b_part, c_part, x_part[:, :, :part]], axis=2)]
    for c in range(1, CHUNKS):
        sends.append(x_part[:, :, c * part : (c + 1) * part])
    arrived = []
    for s in sends:
        if arrived:
            s, _ = lax.optimization_barrier((s, arrived[-1]))
        got = lax.all_to_all(s, "head", split_axis=1, concat_axis=0, tiled=True)
        arrived.append(got.reshape(length, -1))

    taps = conv_weight.astype(f32)
    x_taps = lax.dynamic_slice_in_dim(taps, head_pos * slab, slab, 1)
    x_bias = lax.dynamic_slice_in_dim(conv_bias, head_pos * slab, slab, 0)
    bc_taps = jnp.concatenate(
        [
            lax.dynamic_slice_in_dim(taps, x_width + group * STATE, STATE, 1),
            lax.dynamic_slice_in_dim(taps, x_width + (GROUPS + group) * STATE, STATE, 1),
        ],
        1,
    )
    bc_bias = jnp.concatenate(
        [
            lax.dynamic_slice_in_dim(conv_bias, x_width + group * STATE, STATE, 0),
            lax.dynamic_slice_in_dim(conv_bias, x_width + (GROUPS + group) * STATE, STATE, 0),
        ],
        0,
    )
    rate = -jnp.exp(lax.dynamic_slice_in_dim(a_log, head_pos * heads_dev, heads_dev, 0))
    bias = lax.dynamic_slice_in_dim(dt_bias, head_pos * heads_dev, heads_dev, 0)
    skip = jnp.repeat(lax.dynamic_slice_in_dim(d_skip, head_pos * heads_dev, heads_dev, 0), HEADDIM)
    step = jax.nn.softplus(steps.astype(f32) + bias)
    blocks = length // SPAN
    step_blocks = step.reshape(blocks, SPAN, heads_dev)
    cum = jnp.cumsum((rate * step).reshape(blocks, SPAN, heads_dev), axis=1)
    tri = lax.broadcasted_iota(jnp.int32, (SPAN, SPAN), 0) >= lax.broadcasted_iota(
        jnp.int32, (SPAN, SPAN), 1
    )

    first = arrived[0]
    act0 = convolve(
        first,
        jnp.concatenate([bc_taps, x_taps[:, :part]], 1),
        jnp.concatenate([bc_bias, x_bias[:part]], 0),
    )
    b_blocks = act0[:, :STATE].reshape(blocks, SPAN, STATE)
    c_blocks = act0[:, STATE : 2 * STATE].reshape(blocks, SPAN, STATE)

    def local_block(state, inputs):
        x_now, b_now, c_now, step_now, cum_now, skip_now = inputs
        heads_now = step_now.shape[1]
        gram = jnp.dot(c_now, b_now.T, preferred_element_type=f32)
        cum_t = cum_now.T
        decay = jnp.exp(jnp.where(tri[None], cum_t[:, :, None] - cum_t[:, None, :], -jnp.inf))
        mix = (gram[None] * decay * step_now.T[:, None, :]).astype(jnp.bfloat16)
        x_heads = x_now.reshape(SPAN, heads_now, HEADDIM)
        y_block = jnp.einsum("hts,shp->thp", mix, x_heads, preferred_element_type=f32).reshape(
            SPAN, heads_now * HEADDIM
        )
        grown = jnp.repeat(jnp.exp(cum_now), HEADDIM, axis=1)
        y_state = grown * jnp.dot(
            c_now.astype(f32), state, precision=lax.Precision.HIGHEST, preferred_element_type=f32
        )
        y_now = y_block + y_state + skip_now * x_now.astype(f32)
        weight = jnp.exp(cum_now[-1][None, :] - cum_now) * step_now
        xw = (x_heads.astype(f32) * weight[:, :, None]).astype(jnp.bfloat16)
        xw = xw.reshape(SPAN, heads_now * HEADDIM)
        contrib = jnp.einsum("sn,sc->nc", b_now, xw, preferred_element_type=f32)
        fade = jnp.exp(jnp.repeat(cum_now[-1], HEADDIM))
        return (state * fade[None, :] + contrib, y_now)

    finals, ys = [], []
    for c in range(CHUNKS):
        lo, hi = c * part, (c + 1) * part
        if c == 0:
            x_act = act0[:, 2 * STATE :]
        else:
            x_act = convolve(arrived[c], x_taps[:, lo:hi], x_bias[lo:hi])
        hs = slice(c * part_heads, (c + 1) * part_heads)
        skip_c = jnp.broadcast_to(skip[lo:hi], (blocks, part))
        final, y_blocks = lax.scan(
            local_block,
            jnp.zeros((STATE, part), f32),
            (
                x_act.reshape(blocks, SPAN, part),
                b_blocks,
                c_blocks,
                step_blocks[:, :, hs],
                cum[:, :, hs],
                skip_c,
            ),
        )
        finals.append(final)
        ys.append(y_blocks)
    final = jnp.concatenate(finals, 1)
    y_blocks = jnp.concatenate(ys, 2)

    block_totals = cum[:, -1, :]
    totals = jnp.sum(block_totals, axis=0)
    tail = jnp.broadcast_to(jnp.repeat(totals, HEADDIM)[None, :], (8, slab))
    gathered = lax.all_gather(jnp.concatenate([final, tail], 0), "ctx")
    shards = gathered.shape[0]
    position = lax.axis_index("ctx")
    finals = gathered[:, :STATE]
    shard_totals = gathered[:, STATE]
    before_shard = jnp.cumsum(shard_totals, axis=0) - shard_totals
    reach = jnp.sum(jnp.where(jnp.arange(shards)[:, None] < position, shard_totals, 0.0), axis=0)
    after_own = before_shard + shard_totals
    live = jnp.arange(shards)[:, None] < position
    weights = jnp.where(live, jnp.exp(jnp.where(live, reach[None] - after_own, 0.0)), 0.0)
    incoming = jnp.sum(weights[:, None, :] * finals, axis=0)
    before = jnp.concatenate(
        [jnp.zeros((1, heads_dev), f32), jnp.cumsum(block_totals, axis=0)[:-1]], 0
    )
    lifted = jnp.exp(jnp.repeat(cum + before[:, None, :], HEADDIM, axis=2))
    y_in = lifted * jnp.einsum(
        "bqn,nc->bqc", c_blocks.astype(f32), incoming, precision=lax.Precision.HIGHEST
    )
    result = y_blocks + y_in
    return result.astype(jnp.bfloat16).reshape(length, slab)


def solution(mesh):
    placed = (P(("ctx", "head"), None), P(("ctx", "head"), None), P(), P(), P(), P(), P())
    return jax.shard_map(
        on_device, mesh=mesh, in_specs=placed, out_specs=P("ctx", "head"), check_vma=False
    )
```

time: 621 us -> 919 us (1.48)
  matrix products: 147 us -> 298 us
  local copies, waits for them, and re-layouts: 162 us -> 305 us
  waiting for transfers between devices: 195 us -> 108 us
  other arithmetic: 76.7 us -> 131 us
  starting transfers between devices: 17.8 us -> 45.8 us
    all_to_all x1 -> x4, waiting for transfers between devices: 169 us -> 76.1 us  [on_device(): got = lax.all_to_all(s, 'head', split_axis=1, concat_axis=0, tiled=True)]
    dynamic_slice x28 -> x131, local copies, waits for them, and re-layouts: 25.4 us -> 94.7 us  [the longest x128 93.2 us: on_device(): lax.scan(local_block, jnp.zeros((STATE, part), f32), (x_act.reshape(block...]
    dot_general x8 -> x32, matrix products: 56.8 us -> 109 us  [local_block(): jnp.einsum('hts,shp->thp', mix, x_heads, preferred_element_type=f32)]
    dot_general x8 -> x32, matrix products: 12.9 us -> 60.4 us  [local_block(): contrib = jnp.einsum('sn,sc->nc', b_now, xw, preferred_element_type=f32)]
    dot_general x8 -> x32, matrix products: 41.8 us -> 71.3 us  [local_block(): jnp.dot(c_now.astype(f32), state, precision=lax.Precision.HIGHEST, prefer...]
    convert_element_type x10 -> x37, other arithmetic: 38.7 us -> 65.9 us  [the longest x4 40.2 us: convolve(): return jax.nn.silu(total + offset).astype(jnp.bfloat16)]
    ge x8 -> x32, other arithmetic: 0.64 us -> 25.1 us  [on_device(): lax.broadcasted_iota(jnp.int32, (SPAN, SPAN), 0)]
    dot_general x8 -> x32, matrix products: 18.8 us -> 41 us  [local_block(): gram = jnp.dot(c_now, b_now.T, preferred_element_type=f32)]
  transfers between devices with their start and end apart: 4 -> 10, of which waited for: 3 -> 3; matrix products, arithmetic and copies ran while one was open for 15% -> 64% of each run, Pallas kernels for 0% -> 0%
where the time goes in v3:
time: 919 us; the launch traced here: 904 us
  local copies, waits for them, and re-layouts  305 us (33%)
  matrix products  298 us (32%)
  other arithmetic  131 us (14%)
  waiting for transfers between devices  108 us (12%)
  starting transfers between devices  45.8 us (5%)
  between operations  13.9 us (2%)
    dot_general x32, matrix products, local_block(): jnp.einsum('hts,shp->thp', mix, x_heads, preferred_element_type=f32)  109 us
    dynamic_slice x128, local copies, waits for them, and re-layouts, on_device(): lax.scan(local_block, jnp.zeros((STATE, part), f32), (x_act.reshape(block...  93.2 us
    all_to_all x4, waiting for transfers between devices, on_device(): got = lax.all_to_all(s, 'head', split_axis=1, concat_axis=0, tiled=True)  76.1 us
    dot_general x32, matrix products, local_block(): jnp.dot(c_now.astype(f32), state, precision=lax.Precision.HIGHEST, prefer...  71.3 us
    dot_general x32, matrix products, local_block(): contrib = jnp.einsum('sn,sc->nc', b_now, xw, preferred_element_type=f32)  60.4 us
    dot_general x32, matrix products, local_block(): gram = jnp.dot(c_now, b_now.T, preferred_element_type=f32)  41 us
    convert_element_type x4, other arithmetic, convolve(): return jax.nn.silu(total + offset).astype(jnp.bfloat16)  40.2 us
    reshape x32, local copies, waits for them, and re-layouts, local_block(): jnp.einsum('hts,shp->thp', mix, x_heads, preferred_element_type=f32)  39.5 us
  transfers between devices with their start and end apart: 10, of which 3 were waited for; matrix products, arithmetic and copies ran while one was open for 64% of the time, Pallas kernels for 0%

profile of v3, /device:TPU:30, one launch (start us, length us, event | category | flops | bytes accessed | tf_op | source)
XLA Modules:
  0.0 904.3 jit_solution(2796732227138781604)
XLA Ops:
  8.2 8.3 all-to-all-start
  16.5 7.8 slice.255
  27.5 12.0 %copy.145 = bf16[256,16384]{0,1:T(8,128)(2,1)} copy(bf16[256,16384]{1,0:T(8,128)(2,1)} %slice.255) | data formatting | bytes 16777216
  39.4 5.8 fusion.124
  45.6 5.7 pad_maximum_fusion.1
  51.3 8.6 copy.130
  60.0 7.4 all-to-all-start.1
  75.4 9.1 %reduce-window.6 = f32[8,16,4,128]{3,1,2,0:T(8,128)S(1)} reduce-window(f32[8,16,4,128]{3,1,2,0:T(8,128)S(1)} %copy.123, f32[]{:T(128)} %constant.108.clone.1), window={size=1x1x1x128 pad=0_0x0_0x0_0x127_0}, to_apply=%region_0.1 | reduce-window | flops 8323072 | bytes 524292 | tf_op jit(solution)/shard_map/reduce-window
  86.6 71.8 %all-to-all-done.1 = bf16[256,16,768]{2,0,1:T(8,128)(2,1)} async-done(((bf16[256,16,768]{2,0,1:T(8,128)(2,1)}), bf16[256,16,768]{2,0,1:T(8,128)(2,1)}, u32[]{:S(2)}, u32[]{:S(2)}) %all-to-all-start.1) | async-done | bytes 6291488 | tf_op jit(solution)/shard_map/all_to_all | solution.py:58
  165.1 6.7 all-to-all-start.2
  171.8 16.9 %multiply_convert_fusion.12 = bf16[4096,768]{1,0:T(8,128)(2,1)S(1)} fusion(bf16[4096,768]{1,0:T(8,128)(2,1)} %bitcast.14, bf16[3,768]{1,0:T(4,128)(2,1)S(1)} %collective-permute-done, f32[768]{0:T(1024)S(1)} %copy-done.18, f32[768]{0:T(1024)S(1)} %get-tuple-element.542, f32[768]{0:T(1024)S(1)} %copy-done.16, f32[768]{0:T(1024)S(1)} %copy-done.17, ...), kind=kLoop, calls=%fused_computation.162 | loop fusion | flops 81788928 | bytes 12602880 | tf_op jit(solution)/shard_map/convert_element_type | solution.py:28
  191.1 4.3 all-to-all-done.2
  196.7 3.9 copy.134
  200.6 8.1 all-to-all-start.3
  213.9 152.6 %while.52 = (s32[]{:T(128)}, f32[256,256]{1,0:T(8,128)}, f32[8,512,256]{2,1,0:T(8,128)}, f32[8,512,4]{1,2,0:T(4,128)}, bf16[8,512,256]{2,1,0:T(8,128)(2,1)}, /*i...) while((s32[]{:T(128)}, f32[256,256]{1,0:T(8,128)}, ...), condition=%wide.region_3.4_spmd.clone, body=%wide.region_2.3_spmd.clone.sunk | while | flops 745017344 | bytes 12715879 | solution.py:130
  262.0 3.5 fusion.189
  300.1 3.5 fusion.189
  319.2 3.5 fusion.189
  338.3 3.5 fusion.189
  366.5 7.8 multiply_convert_fusion.15
  375.5 3.9 copy.136
  379.5 7.3 all-to-all-start.4
  391.7 152.7 %while.53 = (s32[]{:T(128)}, f32[256,256]{1,0:T(8,128)}, f32[8,512,256]{2,1,0:T(8,128)}, f32[8,512,4]{1,2,0:T(4,128)}, bf16[8,512,256]{2,1,0:T(8,128)(2,1)}, /*i...) while((s32[]{:T(128)}, f32[256,256]{1,0:T(8,128)}, ...), condition=%wide.region_5.6_spmd.clone, body=%wide.region_4.5_spmd.clone.sunk | while | flops 745017344 | bytes 12715879 | solution.py:130
  544.4 7.9 multiply_convert_fusion.14
  558.7 135.7 %while.54 = (s32[]{:T(128)}, f32[256,256]{1,0:T(8,128)}, f32[8,512,256]{2,1,0:T(8,128)}, f32[8,512,4]{1,2,0:T(4,128)S(1)}, bf16[8,512,256]{2,1,0:T(8,128)(2,1)},...) while((s32[]{:T(128)}, f32[256,256]{1,0:T(8,128)}, ...), condition=%wide.region_7.8_spmd.clone, body=%wide.region_6.7_spmd.clone.sunk | while | flops 745017344 | bytes 12715879 | solution.py:130
  694.3 7.6 multiply_convert_fusion.13
  704.3 109.3 %while.55 = (s32[]{:T(128)}, f32[256,256]{1,0:T(8,128)S(1)}, f32[8,512,256]{2,1,0:T(8,128)}, f32[8,512,4]{1,2,0:T(4,128)S(1)}, bf16[8,512,256]{2,1,0:T(8,128)(2,...) while((s32[]{:T(128)}, f32[256,256]{1,0:T(8,128)S(1)}, ...), condition=%wide.region_9.10_spmd.clone, body=%wide.region_8.9_spmd.clone.sunk | while | flops 745017344 | bytes 12707631 | solution.py:130
  817.1 7.9 broadcast_in_dim.190
  825.0 16.9 %copy.138 = f32[8,512,1024]{2,1,0:T(8,128)} copy(f32[8,512,1024]{1,2,0:T(8,128)} %bitcast.378) | data formatting | bytes 33554432 | tf_op jit(solution)/shard_map/exp | solution.py:164
  841.9 32.1 %all-gather.3.cloned.1.call-done = f32[2112,1024]{1,0:T(8,128)} async-done(((f32[264,1024]{1,0:T(8,128)}), f32[2112,1024]{1,0:T(8,128)}) %all-gather.3.cloned.1.call-update) | async-done | bytes 8650768 | tf_op jit(solution)/shard_map/all_gather | solution.py:150
  876.3 4.6 fusion.105
  880.9 16.5 %fusion.104 = bf16[8,512,1024]{2,1,0:T(8,128)(2,1)} fusion(f32[8,512,256]{2,1,0:T(8,128)} %get-tuple-element.226, f32[8,512,256]{2,1,0:T(8,128)} %get-tuple-element.224, f32[8,512,256]{2,1,0:T(8,128)} %get-tuple-element.222, f32[8,512,256]{2,1,0:T(8,128)} %get-tuple-element.220, f32[8,512,1024]{2,1,0:T(8,128)} %copy.138, ...), kind=kOutput, calls=%fused_computation.161 | convolution fusion | flops 12910067712 | bytes 45088768 | tf_op jit(solution)/shard_map/bqn,nc->bqc/dot_general | solution.py:165
  (887 shorter events, 584.9 us)
Async XLA Ops:
  8.2 51.8 %all-to-all-start = ((bf16[256,16,16]{0,2,1:T(8,128)(2,1)}), bf16[256,16,16]{0,2,1:T(8,128)(2,1)S(1)}, u32[]{:S(2)}, u32[]{:S(2)}) async-start(bf16[256,16,16]{0,2,1:T(8,128)(2,1)} %bitcast), calls=%async_computation | async-start | bytes 262144 | tf_op jit(solution)/shard_map/all_to_all | solution.py:48
  16.5 7.8 slice-start
  60.0 7.5 copy-start.25
  60.0 7.6 copy-start.26
  60.0 11.3 %copy-start.7 = (bf16[4,20480]{1,0:T(4,128)(2,1)S(1)}, bf16[4,20480]{1,0:T(4,128)(2,1)}, u32[]{:S(2)}) copy-start(bf16[4,20480]{1,0:T(4,128)(2,1)} %param.17) | copy-start | bytes 491524
  60.0 11.3 %copy-start.27 = (f32[256]{0:T(256)S(1)}, f32[256]{0:T(256)}, u32[]{:S(2)}) copy-start(f32[256]{0:T(256)} %param.19) | copy-start | bytes 3076
  60.0 98.4 %all-to-all-start.1 = ((bf16[256,16,768]{2,0,1:T(8,128)(2,1)}), bf16[256,16,768]{2,0,1:T(8,128)(2,1)}, u32[]{:S(2)}, u32[]{:S(2)}) async-start(bf16[256,16,768]{2,0,1:T(8,128)(2,1)} %copy.130), calls=%async_computation.1 | async-start | bytes 12582912 | tf_op jit(solution)/shard_map/all_to_all | solution.py:58
  67.3 95.2 %copy-start.4 = (bf16[256,16,256]{0,2,1:T(8,128)(2,1)S(1)}, bf16[256,16,256]{0,2,1:T(8,128)(2,1)}, u32[]{:S(2)}) copy-start(bf16[256,16,256]{0,2,1:T(8,128)(2,1)} %get-tuple-element.221) | copy-start | bytes 6291460
  84.5 80.6 %copy-start.6 = (f32[8,16,4,128]{3,1,2,0:T(8,128)}, f32[8,16,4,128]{3,1,2,0:T(8,128)S(1)}, u32[]{:S(2)}) copy-start(f32[8,16,4,128]{3,1,2,0:T(8,128)S(1)} %reduce-window.6) | copy-start | bytes 786436
  85.0 80.1 %copy-start.8 = (f32[8,16,4]{1,2,0:T(4,128)}, f32[8,16,4]{1,2,0:T(4,128)S(1)}, u32[]{:S(2)}) copy-start(f32[8,16,4]{1,2,0:T(4,128)S(1)} %copy.125) | copy-start | bytes 6148
  159.1 12.7 %collective-permute-start = (bf16[3,768]{1,0:T(4,128)(2,1)S(1)}, bf16[3,768]{1,0:T(4,128)(2,1)S(1)}, u32[]{:S(2)}, u32[]{:S(2)}) collective-permute-start(bf16[3,768]{1,0:T(4,128)(2,1)S(1)} %slice.329), channel_id=1, source_target_pairs={{0,16},{16,32},{32,48},{48,64},{64,80},{80,96},{96,112},{1,17},{17... | collective-permute-start | bytes 13832 | tf_op jit(solution)/shard_map/ppermute | solution.py:18
  162.6 9.2 %copy-start.16 = (f32[768]{0:T(1024)S(1)}, f32[768]{0:T(1024)}, u32[]{:S(2)}) copy-start(f32[768]{0:T(1024)} %get-tuple-element.543) | copy-start | bytes 9220
  162.6 9.2 %copy-start.17 = (f32[768]{0:T(1024)S(1)}, f32[768]{0:T(1024)}, u32[]{:S(2)}) copy-start(f32[768]{0:T(1024)} %get-tuple-element.544) | copy-start | bytes 9220
  162.6 9.2 %copy-start.18 = (f32[768]{0:T(1024)S(1)}, f32[768]{0:T(1024)}, u32[]{:S(2)}) copy-start(f32[768]{0:T(1024)} %pad_maximum_fusion.7) | copy-start | bytes 9220
  165.1 30.4 %all-to-all-start.2 = ((bf16[256,16,256]{2,0,1:T(8,128)(2,1)}), bf16[256,16,256]{2,0,1:T(8,128)(2,1)}, u32[]{:S(2)}, u32[]{:S(2)}) async-start(bf16[256,16,256]{2,0,1:T(8,128)(2,1)} %copy.132), calls=%async_computation.2 | async-start | bytes 4194304 | tf_op jit(solution)/shard_map/all_to_all | solution.py:58
  196.7 14.2 %copy-start.24 = (f32[256]{0:T(256)S(1)}, f32[256]{0:T(256)}, u32[]{:S(2)}) copy-start(f32[256]{0:T(256)} %slice.272) | copy-start | bytes 3076
  200.6 173.6 %all-to-all-start.3 = ((bf16[256,16,256]{2,0,1:T(8,128)(2,1)}), bf16[256,16,256]{2,0,1:T(8,128)(2,1)}, u32[]{:S(2)}, u32[]{:S(2)}) async-start(bf16[256,16,256]{2,0,1:T(8,128)(2,1)} %copy.134), calls=%async_computation.3 | async-start | bytes 4194304 | tf_op jit(solution)/shard_map/all_to_all | solution.py:58
  208.8 157.7 %collective-permute-start.1 = (bf16[3,256]{1,0:T(4,128)(2,1)}, bf16[3,256]{1,0:T(4,128)(2,1)}, u32[]{:S(2)}, u32[]{:S(2)}) collective-permute-start(bf16[3,256]{1,0:T(4,128)(2,1)} %slice.344), channel_id=1, source_target_pairs={{0,16},{16,32},{32,48},{48,64},{64,80},{80,96},{96,112},{1,17},{17... | collective-permute-start | bytes 4616 | tf_op jit(solution)/shard_map/ppermute | solution.py:18
  338.3 7.0 copy-start.13
  357.4 7.0 copy-start.13
  375.5 13.2 %copy-start.23 = (f32[256]{0:T(256)S(1)}, f32[256]{0:T(256)}, u32[]{:S(2)}) copy-start(f32[256]{0:T(256)} %slice.286) | copy-start | bytes 3076
  379.5 172.8 %all-to-all-start.4 = ((bf16[256,16,256]{2,0,1:T(8,128)(2,1)}), bf16[256,16,256]{2,0,1:T(8,128)(2,1)}, u32[]{:S(2)}, u32[]{:S(2)}) async-start(bf16[256,16,256]{2,0,1:T(8,128)(2,1)} %copy.136), calls=%async_computation.4 | async-start | bytes 4194304 | tf_op jit(solution)/shard_map/all_to_all | solution.py:58
  386.8 487.3 %all-gather.3.cloned.1.call-start = ((), (), s32[]{:S(2)}) async-start(), calls=%async_computation.5 | async-start | bytes 9732096 | tf_op jit(solution)/shard_map/all_gather | solution.py:150
  386.8 157.6 %collective-permute-start.2 = (bf16[3,256]{1,0:T(4,128)(2,1)}, bf16[3,256]{1,0:T(4,128)(2,1)}, u32[]{:S(2)}, u32[]{:S(2)}) collective-permute-start(bf16[3,256]{1,0:T(4,128)(2,1)} %slice.352), channel_id=1, source_target_pairs={{0,16},{16,32},{32,48},{48,64},{64,80},{80,96},{96,112},{1,17},{17... | collective-permute-start | bytes 4616 | tf_op jit(solution)/shard_map/ppermute | solution.py:18
  420.7 7.0 copy-start.14
  439.8 7.0 copy-start.14
  544.4 11.3 %copy-start.22 = (f32[256]{0:T(256)S(1)}, f32[256]{0:T(256)}, u32[]{:S(2)}) copy-start(f32[256]{0:T(256)} %slice.300) | copy-start | bytes 3076
  553.6 140.8 %collective-permute-start.3 = (bf16[3,256]{1,0:T(4,128)(2,1)}, bf16[3,256]{1,0:T(4,128)(2,1)}, u32[]{:S(2)}, u32[]{:S(2)}) collective-permute-start(bf16[3,256]{1,0:T(4,128)(2,1)} %slice.360), channel_id=1, source_target_pairs={{0,16},{16,32},{32,48},{48,64},{64,80},{80,96},{96,112},{1,17},{17... | collective-permute-start | bytes 4616 | tf_op jit(solution)/shard_map/ppermute | solution.py:18
  694.3 7.6 copy-start.21
  704.3 109.4 %copy-start.19 = (f32[1024]{0:T(1024)S(1)}, f32[1024]{0:T(1024)}, u32[]{:S(2)}) copy-start(f32[1024]{0:T(1024)} %broadcast_in_dim.194) | copy-start | bytes 12292
  704.3 111.6 %copy-start.20 = (f32[8,16]{1,0:T(8,128)S(1)}, f32[8,16]{1,0:T(8,128)}, u32[]{:S(2)}) copy-start(f32[8,16]{1,0:T(8,128)} %get-tuple-element.540) | copy-start | bytes 1540
  704.3 111.7 %copy-start.9 = (f32[8,16,4]{1,2,0:T(4,128)S(1)}, f32[8,16,4]{1,2,0:T(4,128)}, u32[]{:S(2)}) copy-start(f32[8,16,4]{1,2,0:T(4,128)} %copy-done.8) | copy-start | bytes 6148
  (77 other events, 310.6 us)
Sparse Core Ops, SparseCore 0:
  816.1 57.8 all-gather.2

commit v4 on v3

--- a/solution.py
+++ b/solution.py
@@ -95,10 +95,11 @@
     b_blocks = act0[:, :STATE].reshape(blocks, SPAN, STATE)
     c_blocks = act0[:, STATE : 2 * STATE].reshape(blocks, SPAN, STATE)
 
+    grams = jnp.einsum("bqn,bsn->bqs", c_blocks, b_blocks, preferred_element_type=f32)
+
     def local_block(state, inputs):
-        x_now, b_now, c_now, step_now, cum_now, skip_now = inputs
+        x_now, b_now, gram, step_now, cum_now, skip_now = inputs
         heads_now = step_now.shape[1]
-        gram = jnp.dot(c_now, b_now.T, preferred_element_type=f32)
         cum_t = cum_now.T
         decay = jnp.exp(jnp.where(tri[None], cum_t[:, :, None] - cum_t[:, None, :], -jnp.inf))
         mix = (gram[None] * decay * step_now.T[:, None, :]).astype(jnp.bfloat16)
@@ -106,19 +107,15 @@
         y_block = jnp.einsum("hts,shp->thp", mix, x_heads, preferred_element_type=f32).reshape(
             SPAN, heads_now * HEADDIM
         )
-        grown = jnp.repeat(jnp.exp(cum_now), HEADDIM, axis=1)
-        y_state = grown * jnp.dot(
-            c_now.astype(f32), state, precision=lax.Precision.HIGHEST, preferred_element_type=f32
-        )
-        y_now = y_block + y_state + skip_now * x_now.astype(f32)
+        y_now = y_block + skip_now * x_now.astype(f32)
         weight = jnp.exp(cum_now[-1][None, :] - cum_now) * step_now
         xw = (x_heads.astype(f32) * weight[:, :, None]).astype(jnp.bfloat16)
         xw = xw.reshape(SPAN, heads_now * HEADDIM)
         contrib = jnp.einsum("sn,sc->nc", b_now, xw, preferred_element_type=f32)
         fade = jnp.exp(jnp.repeat(cum_now[-1], HEADDIM))
-        return (state * fade[None, :] + contrib, y_now)
+        return (state * fade[None, :] + contrib, (y_now, state))
 
-    finals, ys = [], []
+    finals, ys, states = [], [], []
     for c in range(CHUNKS):
         lo, hi = c * part, (c + 1) * part
         if c == 0:
@@ -127,13 +124,13 @@
             x_act = convolve(arrived[c], x_taps[:, lo:hi], x_bias[lo:hi])
         hs = slice(c * part_heads, (c + 1) * part_heads)
         skip_c = jnp.broadcast_to(skip[lo:hi], (blocks, part))
-        final, y_blocks = lax.scan(
+        final, (y_blocks, entering) = lax.scan(
             local_block,
             jnp.zeros((STATE, part), f32),
             (
                 x_act.reshape(blocks, SPAN, part),
                 b_blocks,
-                c_blocks,
+                grams,
                 step_blocks[:, :, hs],
                 cum[:, :, hs],
                 skip_c,
@@ -141,8 +138,10 @@
         )
         finals.append(final)
         ys.append(y_blocks)
+        states.append(entering)
     final = jnp.concatenate(finals, 1)
     y_blocks = jnp.concatenate(ys, 2)
+    entering = jnp.concatenate(states, 2)
 
     block_totals = cum[:, -1, :]
     totals = jnp.sum(block_totals, axis=0)
@@ -161,11 +160,13 @@
     before = jnp.concatenate(
         [jnp.zeros((1, heads_dev), f32), jnp.cumsum(block_totals, axis=0)[:-1]], 0
     )
-    lifted = jnp.exp(jnp.repeat(cum + before[:, None, :], HEADDIM, axis=2))
-    y_in = lifted * jnp.einsum(
-        "bqn,nc->bqc", c_blocks.astype(f32), incoming, precision=lax.Precision.HIGHEST
+    carried = jnp.exp(jnp.repeat(before, HEADDIM, axis=1))[:, None, :] * incoming[None]
+    full_state = entering + carried
+    grown = jnp.exp(jnp.repeat(cum, HEADDIM, axis=2))
+    y_state = grown * jnp.einsum(
+        "bqn,bnc->bqc", c_blocks.astype(f32), full_state, precision=lax.Precision.HIGHEST
     )
-    result = y_blocks + y_in
+    result = y_blocks + y_state
     return result.astype(jnp.bfloat16).reshape(length, slab)
 
 

time: 919 us -> 786 us (0.86)
  matrix products: 298 us -> 130 us
  other arithmetic: 131 us -> 152 us
  local copies, waits for them, and re-layouts: 305 us -> 326 us
    dot_general x65 -> x2, matrix products: 129 us -> 23.6 us  [the longest x1 18.9 us: on_device(): jnp.einsum('bqn,bnc->bqc', c_blocks.astype(f32), full_state, precision=la...]
    dot_general x32, matrix products: 109 us -> 48.3 us  [local_block(): jnp.einsum('hts,shp->thp', mix, x_heads, preferred_element_type=f32)]
    reshape x65 -> x1, local copies, waits for them, and re-layouts: 46 us -> 0.16 us  [the longest x32 39.5 us: local_block(): jnp.einsum('hts,shp->thp', mix, x_heads, preferred_element_type=f32)]
    dynamic_update_slice x0 -> x32, other arithmetic: none -> 43.3 us  [on_device(): lax.scan(local_block, jnp.zeros((STATE, part), f32), (x_act.reshape(block...]
    mul x0 -> x32, local copies, waits for them, and re-layouts: none -> 41.6 us  [local_block(): mix = (gram[None] * decay * step_now.T[:, None, :]).astype(jnp.bfloat16)]
    dynamic_update_slice x0 -> x64, local copies, waits for them, and re-layouts: none -> 33 us  [on_device(): lax.scan(local_block, jnp.zeros((STATE, part), f32), (x_act.reshape(block...]
    ge x32, other arithmetic: 25.1 us -> 2.54 us  [on_device(): lax.broadcasted_iota(jnp.int32, (SPAN, SPAN), 0)]
    all_to_all x0 -> x4, local copies, waits for them, and re-layouts: none -> 20.3 us  [on_device(): got = lax.all_to_all(s, 'head', split_axis=1, concat_axis=0, tiled=True)]
  transfers between devices with their start and end apart: 10 -> 10, of which waited for: 3 -> 2; matrix products, arithmetic and copies ran while one was open for 64% -> 60% of each run, Pallas kernels for 0% -> 0%
where the time goes in v4:
time: 786 us; the launch traced here: 773 us
  local copies, waits for them, and re-layouts  326 us (41%)
  other arithmetic  152 us (19%)
  matrix products  130 us (17%)
  waiting for transfers between devices  105 us (13%)
  starting transfers between devices  44.9 us (6%)
  between operations  13.8 us (2%)
    dynamic_slice x128, local copies, waits for them, and re-layouts, on_device(): lax.scan(local_block, jnp.zeros((STATE, part), f32), (x_act.reshape(block...  93.6 us
    all_to_all x4, waiting for transfers between devices, on_device(): got = lax.all_to_all(s, 'head', split_axis=1, concat_axis=0, tiled=True)  73 us
    dot_general x32, matrix products, local_block(): contrib = jnp.einsum('sn,sc->nc', b_now, xw, preferred_element_type=f32)  58 us
    dot_general x32, matrix products, local_block(): jnp.einsum('hts,shp->thp', mix, x_heads, preferred_element_type=f32)  48.3 us
    dynamic_update_slice x32, other arithmetic, on_device(): lax.scan(local_block, jnp.zeros((STATE, part), f32), (x_act.reshape(block...  43.3 us
    mul x32, local copies, waits for them, and re-layouts, local_block(): mix = (gram[None] * decay * step_now.T[:, None, :]).astype(jnp.bfloat16)  41.6 us
    convert_element_type x4, other arithmetic, convolve(): return jax.nn.silu(total + offset).astype(jnp.bfloat16)  39.3 us
    dynamic_update_slice x64, local copies, waits for them, and re-layouts, on_device(): lax.scan(local_block, jnp.zeros((STATE, part), f32), (x_act.reshape(block...  33 us
  transfers between devices with their start and end apart: 10, of which 2 were waited for; matrix products, arithmetic and copies ran while one was open for 60% of the time, Pallas kernels for 0%

profile of v4, /device:TPU:30, one launch (start us, length us, event | category | flops | bytes accessed | tf_op | source)
XLA Modules:
  0.0 773.3 jit_solution(16205989175280064088)
XLA Ops:
  8.2 8.3 %all-to-all-start = ((bf16[256,16,16]{0,2,1:T(8,128)(2,1)}), bf16[256,16,16]{0,2,1:T(8,128)(2,1)S(1)}, u32[]{:S(2)}, u32[]{:S(2)}) async-start(bf16[256,16,16]{0,2,1:T(8,128)(2,1)} %bitcast), calls=%async_computation | async-start | bytes 262144 | tf_op jit(solution)/shard_map/all_to_all | solution.py:48
  16.5 7.8 %slice.255 = bf16[256,16384]{1,0:T(8,128)(2,1)} slice(bf16[256,20480]{1,0:T(8,128)(2,1)} %param.15), slice={[0:256], [0:16384]} | slice | bytes 16777216 | tf_op jit(solution)/shard_map/slice | solution.py:43
  27.4 12.0 %copy.109 = bf16[256,16384]{0,1:T(8,128)(2,1)} copy(bf16[256,16384]{1,0:T(8,128)(2,1)} %slice.255) | data formatting | bytes 16777216
  39.4 5.8 fusion.70
  45.6 5.7 pad_maximum_fusion.1
  51.4 7.4 all-to-all-start.1
  65.6 9.1 %reduce-window.6 = f32[8,16,4,128]{3,1,2,0:T(8,128)S(1)} reduce-window(f32[8,16,4,128]{3,1,2,0:T(8,128)S(1)} %copy.67, f32[]{:T(128)} %constant.115.clone.1), window={size=1x1x1x128 pad=0_0x0_0x0_0x127_0}, to_apply=%region_0.1 | reduce-window | flops 8323072 | bytes 524292 | tf_op jit(solution)/shard_map/reduce-window
  76.8 73.0 %all-to-all-done.1 = bf16[256,16,768]{0,2,1:T(8,128)(2,1)} async-done(((bf16[256,16,768]{0,2,1:T(8,128)(2,1)}), bf16[256,16,768]{0,2,1:T(8,128)(2,1)}, u32[]{:S(2)}, u32[]{:S(2)}) %all-to-all-start.1) | async-done | bytes 6291488 | tf_op jit(solution)/shard_map/all_to_all | solution.py:58
  149.8 8.6 %copy.74 = bf16[16,256,1,768]{3,1,0,2:T(8,128)(2,1)} copy(bf16[16,256,1,768]{1,3,0,2:T(8,128)(2,1)} %bitcast.13) | data formatting | bytes 12582912 | tf_op jit(solution)/shard_map/all_to_all | solution.py:58
  162.5 6.7 all-to-all-start.2
  169.2 16.8 %multiply_convert_fusion.12 = bf16[4096,768]{1,0:T(8,128)(2,1)S(1)} fusion(bf16[4096,768]{1,0:T(8,128)(2,1)} %bitcast.320, bf16[3,768]{1,0:T(4,128)(2,1)S(1)} %collective-permute-done, f32[768]{0:T(1024)S(1)} %pad_maximum_fusion.7, f32[768]{0:T(1024)S(1)} %get-tuple-element.562, f32[768]{0:T(1024)S(1)} %get-tuple-element.563, ...), kind=kLoop, calls=%fused_computation.102 | loop fusion | flops 81788928 | bytes 12602880 | tf_op jit(solution)/shard_map/convert_element_type | solution.py:28
  189.1 4.7 fusion.78
  193.8 3.9 copy.77
  199.0 7.4 all-to-all-start.3
  210.4 2.4 broadcast.146.clone2.3
  212.8 117.8 %while.60 = (s32[]{:T(128)}, f32[256,256]{1,0:T(8,128)}, f32[8,512,256]{2,1,0:T(8,128)}, f32[8,256,256]{2,1,0:T(8,128)}, f32[8,512,4]{1,2,0:T(4,128)}, /*index=5...) while((s32[]{:T(128)}, f32[256,256]{1,0:T(8,128)}, ...), condition=%wide.region_3.4_spmd.clone, body=%wide.region_2.3_spmd.clone.sunk | while | flops 207884288 | bytes 11119940 | solution.py:127
  330.6 7.6 multiply_convert_fusion.15
  338.2 3.9 copy.80
  343.4 7.3 all-to-all-start.4
  354.7 2.3 broadcast.146.clone2.2
  357.0 117.8 %while.61 = (s32[]{:T(128)}, f32[256,256]{1,0:T(8,128)}, f32[8,512,256]{2,1,0:T(8,128)}, f32[8,256,256]{2,1,0:T(8,128)}, f32[8,512,4]{1,2,0:T(4,128)}, /*index=5...) while((s32[]{:T(128)}, f32[256,256]{1,0:T(8,128)}, ...), condition=%wide.region_5.6_spmd.clone, body=%wide.region_4.5_spmd.clone.sunk | while | flops 207884288 | bytes 11119940 | solution.py:127
  474.9 7.3 multiply_convert_fusion.14
  482.2 3.9 copy.83
  493.9 101.2 %while.62 = (s32[]{:T(128)}, f32[256,256]{1,0:T(8,128)}, f32[8,512,256]{2,1,0:T(8,128)}, f32[8,256,256]{2,1,0:T(8,128)}, f32[8,512,4]{1,2,0:T(4,128)S(1)}, /*ind...) while((s32[]{:T(128)}, f32[256,256]{1,0:T(8,128)}, ...), condition=%wide.region_7.8_spmd.clone, body=%wide.region_6.7_spmd.clone.sunk | while | flops 207884288 | bytes 11119940 | solution.py:127
  595.1 7.6 multiply_convert_fusion.13
  604.3 2.3 broadcast.146.clone2
  606.6 73.6 %while.63 = (s32[]{:T(128)}, f32[256,256]{1,0:T(8,128)S(1)}, f32[8,512,256]{2,1,0:T(8,128)}, f32[8,256,256]{2,1,0:T(8,128)}, f32[8,512,4]{1,2,0:T(4,128)S(1)}, /...) while((s32[]{:T(128)}, f32[256,256]{1,0:T(8,128)S(1)}, ...), condition=%wide.region_9.10_spmd.clone, body=%wide.region_8.9_spmd.clone.sunk | while | flops 207884288 | bytes 11115816 | solution.py:127
  683.8 7.9 %broadcast_in_dim.187 = f32[8,512,16,64]{1,3,2,0:T(8,128)} broadcast(f32[8,512,16]{1,2,0:T(8,128)S(1)} %fusion.68), dimensions={0,1,2} | broadcast | bytes 17039360 | tf_op jit(solution)/shard_map/broadcast_in_dim | solution.py:165
  691.7 17.0 %copy.90 = f32[8,512,1024]{2,1,0:T(8,128)} copy(f32[8,512,1024]{1,2,0:T(8,128)} %bitcast.303) | data formatting | bytes 33554432 | tf_op jit(solution)/shard_map/exp | solution.py:165
  708.7 31.8 %all-gather.3.cloned.1.call-done = f32[2112,1024]{1,0:T(8,128)} async-done(((f32[264,1024]{1,0:T(8,128)}), f32[2112,1024]{1,0:T(8,128)}) %all-gather.3.cloned.1.call-update) | async-done | bytes 8650768 | tf_op jit(solution)/shard_map/all_gather | solution.py:149
  742.8 4.7 fusion.41
  747.5 18.9 %fusion.40 = bf16[8,512,1024]{2,1,0:T(8,128)(2,1)} fusion(f32[8,512,256]{2,1,0:T(8,128)} %get-tuple-element.250, f32[8,512,256]{2,1,0:T(8,128)} %get-tuple-element.248, f32[8,512,256]{2,1,0:T(8,128)} %get-tuple-element.246, f32[8,512,256]{2,1,0:T(8,128)} %get-tuple-element.244, f32[8,512,1024]{2,1,0:T(8,128)} %copy.90, ...), kind=kOutput, calls=%fused_computation.101 | convolution fusion | flops 12920553472 | bytes 53510144 | tf_op jit(solution)/shard_map/bqn,bnc->bqc/dot_general | solution.py:166
  (774 shorter events, 455.6 us)
Async XLA Ops:
  8.2 43.2 %all-to-all-start = ((bf16[256,16,16]{0,2,1:T(8,128)(2,1)}), bf16[256,16,16]{0,2,1:T(8,128)(2,1)S(1)}, u32[]{:S(2)}, u32[]{:S(2)}) async-start(bf16[256,16,16]{0,2,1:T(8,128)(2,1)} %bitcast), calls=%async_computation | async-start | bytes 262144 | tf_op jit(solution)/shard_map/all_to_all | solution.py:48
  16.5 7.8 %slice-start = ((bf16[256,20480]{1,0:T(8,128)(2,1)}), bf16[256,4096]{1,0:T(8,128)(2,1)S(1)}, s32[]{:S(2)}) async-start(bf16[256,20480]{1,0:T(8,128)(2,1)} %param.15), calls=%async_computation.6 | async-start | bytes 4194304 | tf_op jit(solution)/shard_map/slice | solution.py:44
  39.4 6.0 copy-start.2
  51.3 7.4 copy-start.14
  51.3 7.5 copy-start.15
  51.3 11.3 %copy-start.4 = (bf16[4,20480]{1,0:T(4,128)(2,1)S(1)}, bf16[4,20480]{1,0:T(4,128)(2,1)}, u32[]{:S(2)}) copy-start(bf16[4,20480]{1,0:T(4,128)(2,1)} %param.17) | copy-start | bytes 491524
  51.3 11.3 %copy-start.16 = (f32[256]{0:T(256)S(1)}, f32[256]{0:T(256)}, u32[]{:S(2)}) copy-start(f32[256]{0:T(256)} %param.19) | copy-start | bytes 3076
  51.4 98.4 %all-to-all-start.1 = ((bf16[256,16,768]{0,2,1:T(8,128)(2,1)}), bf16[256,16,768]{0,2,1:T(8,128)(2,1)}, u32[]{:S(2)}, u32[]{:S(2)}) async-start(bf16[256,16,768]{0,2,1:T(8,128)(2,1)} %pad_maximum_fusion.1), calls=%async_computation.1 | async-start | bytes 12582912 | tf_op jit(solution)/shard_map/all_to_all | solution.py:58
  74.7 83.7 %copy-start.3 = (f32[8,16,4,128]{3,1,2,0:T(8,128)}, f32[8,16,4,128]{3,1,2,0:T(8,128)S(1)}, u32[]{:S(2)}) copy-start(f32[8,16,4,128]{3,1,2,0:T(8,128)S(1)} %reduce-window.6) | copy-start | bytes 786436
  159.1 10.1 %collective-permute-start = (bf16[3,768]{1,0:T(4,128)(2,1)S(1)}, bf16[3,768]{1,0:T(4,128)(2,1)S(1)}, u32[]{:S(2)}, u32[]{:S(2)}) collective-permute-start(bf16[3,768]{1,0:T(4,128)(2,1)S(1)} %slice.329), channel_id=1, source_target_pairs={{0,16},{16,32},{32,48},{48,64},{64,80},{80,96},{96,112},{1,17},{17... | collective-permute-start | bytes 13832 | tf_op jit(solution)/shard_map/ppermute | solution.py:18
  162.5 31.3 %all-to-all-start.2 = ((bf16[256,16,256]{0,2,1:T(8,128)(2,1)}), bf16[256,16,256]{0,2,1:T(8,128)(2,1)}, u32[]{:S(2)}, u32[]{:S(2)}) async-start(bf16[256,16,256]{0,2,1:T(8,128)(2,1)} %get-tuple-element.245), calls=%async_computation.2 | async-start | bytes 4194304 | tf_op jit(solution)/shard_map/all_to_all | solution.py:58
  193.8 14.5 %copy-start.13 = (f32[256]{0:T(256)S(1)}, f32[256]{0:T(256)}, u32[]{:S(2)}) copy-start(f32[256]{0:T(256)} %slice.272) | copy-start | bytes 3076
  199.0 139.2 %all-to-all-start.3 = ((bf16[256,16,256]{0,2,1:T(8,128)(2,1)}), bf16[256,16,256]{0,2,1:T(8,128)(2,1)}, u32[]{:S(2)}, u32[]{:S(2)}) async-start(bf16[256,16,256]{0,2,1:T(8,128)(2,1)} %get-tuple-element.247), calls=%async_computation.3 | async-start | bytes 4194304 | tf_op jit(solution)/shard_map/all_to_all | solution.py:58
  206.4 124.2 %collective-permute-start.1 = (bf16[3,256]{1,0:T(4,128)(2,1)}, bf16[3,256]{1,0:T(4,128)(2,1)}, u32[]{:S(2)}, u32[]{:S(2)}) collective-permute-start(bf16[3,256]{1,0:T(4,128)(2,1)} %slice.344), channel_id=1, source_target_pairs={{0,16},{16,32},{32,48},{48,64},{64,80},{80,96},{96,112},{1,17},{17... | collective-permute-start | bytes 4616 | tf_op jit(solution)/shard_map/ppermute | solution.py:18
  220.0 2.8 copy-start.5
  233.8 2.8 copy-start.5
  248.6 2.8 copy-start.5
  338.2 14.4 %copy-start.12 = (f32[256]{0:T(256)S(1)}, f32[256]{0:T(256)}, u32[]{:S(2)}) copy-start(f32[256]{0:T(256)} %slice.286) | copy-start | bytes 3076
  343.4 138.8 %all-to-all-start.4 = ((bf16[256,16,256]{0,2,1:T(8,128)(2,1)}), bf16[256,16,256]{0,2,1:T(8,128)(2,1)}, u32[]{:S(2)}, u32[]{:S(2)}) async-start(bf16[256,16,256]{0,2,1:T(8,128)(2,1)} %get-tuple-element.249), calls=%async_computation.4 | async-start | bytes 4194304 | tf_op jit(solution)/shard_map/all_to_all | solution.py:58
  350.6 389.9 %all-gather.3.cloned.1.call-start = ((), (), s32[]{:S(2)}) async-start(), calls=%async_computation.5 | async-start | bytes 9732096 | tf_op jit(solution)/shard_map/all_gather | solution.py:149
  350.7 124.2 %collective-permute-start.2 = (bf16[3,256]{1,0:T(4,128)(2,1)}, bf16[3,256]{1,0:T(4,128)(2,1)}, u32[]{:S(2)}, u32[]{:S(2)}) collective-permute-start(bf16[3,256]{1,0:T(4,128)(2,1)} %slice.352), channel_id=1, source_target_pairs={{0,16},{16,32},{32,48},{48,64},{64,80},{80,96},{96,112},{1,17},{17... | collective-permute-start | bytes 4616 | tf_op jit(solution)/shard_map/ppermute | solution.py:18
  437.4 2.8 copy-start.6
  452.3 2.8 copy-start.6
  474.9 14.6 %copy-start.11 = (f32[256]{0:T(256)S(1)}, f32[256]{0:T(256)}, u32[]{:S(2)}) copy-start(f32[256]{0:T(256)} %slice.300) | copy-start | bytes 3076
  487.3 107.7 %collective-permute-start.3 = (bf16[3,256]{1,0:T(4,128)(2,1)}, bf16[3,256]{1,0:T(4,128)(2,1)}, u32[]{:S(2)}, u32[]{:S(2)}) collective-permute-start(bf16[3,256]{1,0:T(4,128)(2,1)} %slice.360), channel_id=1, source_target_pairs={{0,16},{16,32},{32,48},{48,64},{64,80},{80,96},{96,112},{1,17},{17... | collective-permute-start | bytes 4616 | tf_op jit(solution)/shard_map/ppermute | solution.py:18
  499.0 2.8 copy-start.7
  510.7 2.8 copy-start.7
  536.3 2.8 copy-start.7
  595.1 7.6 copy-start.10
  606.6 73.6 %copy-start.8 = (f32[1024]{0:T(1024)S(1)}, f32[1024]{0:T(1024)}, u32[]{:S(2)}) copy-start(f32[1024]{0:T(1024)} %broadcast_in_dim.192) | copy-start | bytes 12292
  606.6 75.9 %copy-start.9 = (f32[8,16]{1,0:T(8,128)S(1)}, f32[8,16]{1,0:T(8,128)}, u32[]{:S(2)}) copy-start(f32[8,16]{1,0:T(8,128)} %get-tuple-element.559) | copy-start | bytes 1540
  742.8 4.7 copy-start.1
  (17 other events, 46.5 us)
Sparse Core Ops, SparseCore 0:
  682.6 57.8 all-gather.2

commit v5 on v2

--- a/solution.py
+++ b/solution.py
@@ -58,11 +58,19 @@
     cum_acc = jnp.zeros((blocks, SPAN, heads_dev), f32)
     contrib_acc = jnp.zeros((blocks, STATE, slab), f32)
     done = []
-    for m in range(blocks):
-        same = [(i, 2 * ((i // 2 + m) % pairs) + i % 2) for i in range(head_count)]
-        other = [(i, 2 * ((i // 2 + m) % pairs) + 1 - i % 2) for i in range(head_count)]
-        t_same = 2 * ((head_pos // 2 + m) % pairs) + parity
-        t_other = 2 * ((head_pos // 2 + m) % pairs) + 1 - parity
+    rings = 4
+    across = pairs // rings
+    order = [(0, 0), (1, 0), (rings - 1, 0)] + [(d, 1) for d in (0, 1, rings - 1)]
+    order = order + [(2, 0), (2, 1)]
+
+    def moved(p, dz, dx):
+        return ((p // across + dz) % rings) * across + (p % across + dx) % across
+
+    for m, (dz, dx) in enumerate(order):
+        same = [(i, 2 * moved(i // 2, dz, dx) + i % 2) for i in range(head_count)]
+        other = [(i, 2 * moved(i // 2, dz, dx) + 1 - i % 2) for i in range(head_count)]
+        t_same = 2 * moved(head_pos // 2, dz, dx) + parity
+        t_other = 2 * moved(head_pos // 2, dz, dx) + 1 - parity
         p_same, p_other = payload(t_same), payload(t_other)
         if m >= 2:
             p_same, p_other, _ = lax.optimization_barrier((p_same, p_other, done[m - 2]))
@@ -71,7 +79,7 @@
         first = jnp.where(parity == 0, r_same, r_other)
         second = jnp.where(parity == 0, r_other, r_same)
         blk = jnp.concatenate([first, second], 0)
-        k = (head_pos // 2 - m) % pairs
+        k = moved(head_pos // 2, rings - dz, across - dx)
         x_now = blk[:, :slab]
         b_now = blk[:, slab : slab + STATE]
         c_now = blk[:, slab + STATE : slab + 2 * STATE]

time: 592 us -> 619 us (1.046)
  waiting for transfers between devices: 181 us -> 208 us
    ppermute x8, waiting for transfers between devices: 115 us -> 144 us  [on_device(): r_same = lax.ppermute(p_same, 'head', same)]
  transfers between devices with their start and end apart: 18 -> 18, of which waited for: 11 -> 11; matrix products, arithmetic and copies ran while one was open for 32% -> 30% of each run, Pallas kernels for 0% -> 0%
where the time goes in v5:
time: 619 us; the launch traced here: 611 us
  waiting for transfers between devices  208 us (34%)
  local copies, waits for them, and re-layouts  139 us (22%)
  other arithmetic  123 us (20%)
  matrix products  86.7 us (14%)
  starting transfers between devices  37.6 us (6%)
  between operations  15.9 us (3%)
    ppermute x8, waiting for transfers between devices, on_device(): r_same = lax.ppermute(p_same, 'head', same)  144 us
    ppermute x8, waiting for transfers between devices, on_device(): r_other = lax.ppermute(p_other, 'head', other)  64.6 us
    dot_general x8, matrix products, on_device(): jnp.einsum('hts,shp->thp', mix, x_heads, preferred_element_type=f32)  39.7 us
    convert_element_type x1, other arithmetic, on_device(): act = jax.nn.silu(total + conv_bias).astype(jnp.bfloat16)  36.7 us
    unnamed x293, local copies, waits for them, and re-layouts  27.1 us
    dot_general x1, matrix products, on_device(): jnp.einsum('bqn,bnc->bqc', c_acc.astype(f32), full_state, precision=lax.P...  24 us
    broadcast_in_dim x8, local copies, waits for them, and re-layouts, on_device(): y_acc = lax.dynamic_update_index_in_dim(y_acc, y_now, k, 0)  22.9 us
    ppermute x8, starting transfers between devices, on_device(): r_same = lax.ppermute(p_same, 'head', same)  21.2 us
  transfers between devices with their start and end apart: 18, of which 11 were waited for; matrix products, arithmetic and copies ran while one was open for 30% of the time, Pallas kernels for 0%

profile of v5, /device:TPU:30, one launch (start us, length us, event | category | flops | bytes accessed | tf_op | source)
XLA Modules:
  0.0 610.6 jit_solution(18297912828620384963)
XLA Ops:
  7.6 3.7 collective-permute-start
  11.7 13.8 %copy.474 = bf16[256,20480]{0,1:T(8,128)(2,1)} copy(bf16[256,20480]{1,0:T(8,128)(2,1)} %param.7) | data formatting | bytes 20971520 | tf_op args[0]
  33.6 3.6 copy.473
  37.3 36.7 %multiply_convert_fusion = bf16[256,20480]{0,1:T(8,128)(2,1)S(1)} fusion(bf16[256,20480]{0,1:T(8,128)(2,1)} %copy.474, bf16[3,20480]{0,1:T(8,128)(2,1)} %copy.473, f32[20480]{0:T(1024)S(1)} %copy-done.103, f32[20480]{0:T(1024)S(1)} %bitcast.409, f32[20480]{0:T(1024)S(1)} %bitcast.408, f32[20480]{0:T(1024)S(1)} %bitcast.407, f32[20480]{0:T(1024)S(1)} %bitcast.406), kind=kLoop, calls=%fused_computation | loop fusion | flops 136314880 | bytes 21504000 | tf_op jit(solution)/shard_map/convert_element_type | solution.py:33
  82.0 7.2 %collective-permute-start.1 = (bf16[256,1552]{0,1:T(8,128)(2,1)}, bf16[256,1552]{0,1:T(8,128)(2,1)}, u32[]{:S(2)}, u32[]{:S(2)}) collective-permute-start(bf16[256,1552]{0,1:T(8,128)(2,1)} %pad_maximum_fusion.2), channel_id=1, source_target_pairs={{0,0},{1,1},{2,2},{3,3},{4,4},{5,5},{6,6},{7,7},{8,8},{9,9},{10,10... | collective-permute-start | bytes 2383880 | tf_op jit(solution)/shard_map/ppermute | solution.py:77
  93.0 21.4 %collective-permute-done.3 = bf16[256,1552]{0,1:T(8,128)(2,1)S(1)} collective-permute-done((bf16[256,1552]{0,1:T(8,128)(2,1)S(1)}, bf16[256,1552]{0,1:T(8,128)(2,1)S(1)}, u32[]{:S(2)}, u32[]{:S(2)}) %collective-permute-start.3) | collective-permute-done | bytes 794656 | tf_op jit(solution)/shard_map/ppermute | solution.py:77
  119.6 4.9 fusion.6
  134.0 14.4 %collective-permute-done.7 = bf16[256,1552]{0,1:T(8,128)(2,1)S(1)} collective-permute-done((bf16[256,1552]{0,1:T(8,128)(2,1)S(1)}, bf16[256,1552]{0,1:T(8,128)(2,1)S(1)}, u32[]{:S(2)}, u32[]{:S(2)}) %collective-permute-start.7) | collective-permute-done | bytes 794656 | tf_op jit(solution)/shard_map/ppermute | solution.py:77
  148.4 14.7 %collective-permute-done.8 = bf16[256,1552]{0,1:T(8,128)(2,1)S(1)} collective-permute-done((bf16[256,1552]{0,1:T(8,128)(2,1)S(1)}, bf16[256,1552]{0,1:T(8,128)(2,1)S(1)}, u32[]{:S(2)}, u32[]{:S(2)}) %collective-permute-start.8) | collective-permute-done | bytes 794656 | tf_op jit(solution)/shard_map/ppermute | solution.py:78
  167.2 4.9 fusion.8
  184.1 13.3 %collective-permute-done.11 = bf16[256,1552]{0,1:T(8,128)(2,1)S(1)} collective-permute-done((bf16[256,1552]{0,1:T(8,128)(2,1)S(1)}, bf16[256,1552]{0,1:T(8,128)(2,1)S(1)}, u32[]{:S(2)}, u32[]{:S(2)}) %collective-permute-start.11) | collective-permute-done | bytes 794656 | tf_op jit(solution)/shard_map/ppermute | solution.py:77
  197.4 16.9 %collective-permute-done.12 = bf16[256,1552]{0,1:T(8,128)(2,1)S(1)} collective-permute-done((bf16[256,1552]{0,1:T(8,128)(2,1)S(1)}, bf16[256,1552]{0,1:T(8,128)(2,1)S(1)}, u32[]{:S(2)}, u32[]{:S(2)}) %collective-permute-start.12) | collective-permute-done | bytes 794656 | tf_op jit(solution)/shard_map/ppermute | solution.py:78
  224.6 5.0 fusion.10
  229.6 5.0 fusion.5
  242.2 4.5 broadcast_in_dim.348
  252.6 9.1 %collective-permute-done.15 = bf16[256,1552]{0,1:T(8,128)(2,1)S(1)} collective-permute-done((bf16[256,1552]{0,1:T(8,128)(2,1)S(1)}, bf16[256,1552]{0,1:T(8,128)(2,1)S(1)}, u32[]{:S(2)}, u32[]{:S(2)}) %collective-permute-start.15) | collective-permute-done | bytes 794656 | tf_op jit(solution)/shard_map/ppermute | solution.py:77
  261.7 16.0 %collective-permute-done.16 = bf16[256,1552]{0,1:T(8,128)(2,1)S(1)} collective-permute-done((bf16[256,1552]{0,1:T(8,128)(2,1)S(1)}, bf16[256,1552]{0,1:T(8,128)(2,1)S(1)}, u32[]{:S(2)}, u32[]{:S(2)}) %collective-permute-start.16) | collective-permute-done | bytes 794656 | tf_op jit(solution)/shard_map/ppermute | solution.py:78
  279.4 32.4 %collective-permute-done.5 = bf16[256,1552]{0,1:T(8,128)(2,1)S(1)} collective-permute-done((bf16[256,1552]{0,1:T(8,128)(2,1)S(1)}, bf16[256,1552]{0,1:T(8,128)(2,1)S(1)}, u32[]{:S(2)}, u32[]{:S(2)}) %collective-permute-start.5) | collective-permute-done | bytes 794656 | tf_op jit(solution)/shard_map/ppermute | solution.py:77
  320.5 5.0 fusion.12
  325.5 5.0 fusion.7
  338.8 19.2 %collective-permute-done.9 = bf16[256,1552]{0,1:T(8,128)(2,1)S(1)} collective-permute-done((bf16[256,1552]{0,1:T(8,128)(2,1)S(1)}, bf16[256,1552]{0,1:T(8,128)(2,1)S(1)}, u32[]{:S(2)}, u32[]{:S(2)}) %collective-permute-start.9) | collective-permute-done | bytes 794656 | tf_op jit(solution)/shard_map/ppermute | solution.py:77
  357.9 16.9 %collective-permute-done.10 = bf16[256,1552]{0,1:T(8,128)(2,1)S(1)} collective-permute-done((bf16[256,1552]{0,1:T(8,128)(2,1)S(1)}, bf16[256,1552]{0,1:T(8,128)(2,1)S(1)}, u32[]{:S(2)}, u32[]{:S(2)}) %collective-permute-start.10) | collective-permute-done | bytes 794656 | tf_op jit(solution)/shard_map/ppermute | solution.py:78
  385.4 4.9 fusion.9
  397.8 34.0 %collective-permute-done.13 = bf16[256,1552]{0,1:T(8,128)(2,1)S(1)} collective-permute-done((bf16[256,1552]{0,1:T(8,128)(2,1)S(1)}, bf16[256,1552]{0,1:T(8,128)(2,1)S(1)}, u32[]{:S(2)}, u32[]{:S(2)}) %collective-permute-start.13) | collective-permute-done | bytes 794656 | tf_op jit(solution)/shard_map/ppermute | solution.py:77
  447.4 4.4 fusion.56
  476.1 8.1 %broadcast_in_dim.315 = f32[8,512,1024]{2,1,0:T(8,128)} broadcast(f32[]{:T(128)} %constant.552.clone.1), dimensions={} | broadcast | bytes 16777220 | tf_op jit(solution)/shard_map/broadcast_in_dim | solution.py:56
  497.4 3.5 constant_dynamic-update-slice_fusion.13
  514.0 4.9 fusion.11
  523.5 8.0 %broadcast_in_dim.336 = f32[8,512,16,64]{1,3,2,0:T(8,128)} broadcast(f32[8,512,16]{1,2,0:T(8,128)S(1)} %exp.234), dimensions={0,1,2} | broadcast | bytes 17039360 | tf_op jit(solution)/shard_map/broadcast_in_dim | solution.py:133
  531.4 16.4 %copy.524 = f32[8,512,1024]{2,1,0:T(8,128)} copy(f32[8,512,1024]{1,2,0:T(8,128)} %bitcast.388) | data formatting | bytes 33554432 | tf_op jit(solution)/shard_map/exp | solution.py:133
  574.7 4.6 fusion.2
  579.3 24.0 %add_convert_fusion = bf16[8,512,1024]{2,1,0:T(8,128)(2,1)} fusion(f32[8,512,1024]{2,1,0:T(8,128)} %constant_dynamic-update-slice_fusion.8, f32[8,512,1024]{2,1,0:T(8,128)} %copy.524, bf16[8,512,256]{2,1,0:T(8,128)(2,1)} %constant_dynamic-update-slice_fusion, f32[8,256,1024]{2,1,0:T(8,128)} %add_dynamic-update-slice_fusion, f32[256,1024]{1,0:T(8,128)S(1)} %fusion.2, ...), kind=kOutput, calls=%fused_computation.3 | convolution fusion | flops 12901679104 | bytes 53510144 | tf_op jit(solution)/shard_map/bqn,bnc->bqc/dot_general | solution.py:134
  (536 shorter events, 208.1 us)
Async XLA Ops:
  6.5 565.9 %all-gather.3.cloned.1.call-start = ((), (), s32[]{:S(2)}) async-start(), calls=%async_computation | async-start | bytes 9732096 | tf_op jit(solution)/shard_map/all_gather | solution.py:117
  7.6 26.0 %collective-permute-start = (bf16[3,20480]{1,0:T(4,128)(2,1)S(1)}, bf16[3,20480]{1,0:T(4,128)(2,1)S(1)}, u32[]{:S(2)}, u32[]{:S(2)}) collective-permute-start(bf16[3,20480]{1,0:T(4,128)(2,1)S(1)} %slice.268), channel_id=1, source_target_pairs={{0,1},{1,2},{2,3},{3,4},{4,5},{5,6},{6,7},{7,8},{8,9},{9,10},{10,1... | collective-permute-start | bytes 368648 | tf_op jit(solution)/shard_map/ppermute | solution.py:25
  25.5 90.5 %copy-start.119 = (f32[16]{0:T(128)}, f32[16]{0:T(128)S(1)}, u32[]{:S(2)}) copy-start(f32[16]{0:T(128)S(1)} %exponential_negate_fusion) | copy-start | bytes 196
  25.6 90.4 %copy-start.124 = (f32[16]{0:T(128)}, f32[16]{0:T(128)S(1)}, u32[]{:S(2)}) copy-start(f32[16]{0:T(128)S(1)} %dynamic_slice.210) | copy-start | bytes 196
  76.9 37.5 %collective-permute-start.3 = (bf16[256,1552]{0,1:T(8,128)(2,1)S(1)}, bf16[256,1552]{0,1:T(8,128)(2,1)S(1)}, u32[]{:S(2)}, u32[]{:S(2)}) collective-permute-start(bf16[256,1552]{0,1:T(8,128)(2,1)S(1)} %pad_maximum_fusion.4), channel_id=1, source_target_pairs={{0,4},{1,5},{2,6},{3,7},{4,8},{5,9},{6,10},{7,11},{8,12},{9,13},{1... | collective-permute-start | bytes 2383880 | tf_op jit(solution)/shard_map/ppermute | solution.py:77
  78.9 35.4 %collective-permute-start.4 = (bf16[256,1552]{0,1:T(8,128)(2,1)S(1)}, bf16[256,1552]{0,1:T(8,128)(2,1)S(1)}, u32[]{:S(2)}, u32[]{:S(2)}) collective-permute-start(bf16[256,1552]{0,1:T(8,128)(2,1)S(1)} %pad_maximum_fusion.5), channel_id=1, source_target_pairs={{0,5},{1,4},{2,7},{3,6},{4,9},{5,8},{6,11},{7,10},{8,13},{9,12},{1... | collective-permute-start | bytes 2383880 | tf_op jit(solution)/shard_map/ppermute | solution.py:78
  82.0 99.1 %collective-permute-start.1 = (bf16[256,1552]{0,1:T(8,128)(2,1)}, bf16[256,1552]{0,1:T(8,128)(2,1)}, u32[]{:S(2)}, u32[]{:S(2)}) collective-permute-start(bf16[256,1552]{0,1:T(8,128)(2,1)} %pad_maximum_fusion.2), channel_id=1, source_target_pairs={{0,0},{1,1},{2,2},{3,3},{4,4},{5,5},{6,6},{7,7},{8,8},{9,9},{10,10... | collective-permute-start | bytes 2383880 | tf_op jit(solution)/shard_map/ppermute | solution.py:77
  126.3 22.1 %collective-permute-start.7 = (bf16[256,1552]{0,1:T(8,128)(2,1)S(1)}, bf16[256,1552]{0,1:T(8,128)(2,1)S(1)}, u32[]{:S(2)}, u32[]{:S(2)}) collective-permute-start(bf16[256,1552]{0,1:T(8,128)(2,1)S(1)} %copy-done.75), channel_id=1, source_target_pairs={{0,2},{1,3},{2,0},{3,1},{4,6},{5,7},{6,4},{7,5},{8,10},{9,11},{10,... | collective-permute-start | bytes 2383880 | tf_op jit(solution)/shard_map/ppermute | solution.py:77
  128.4 34.7 %collective-permute-start.8 = (bf16[256,1552]{0,1:T(8,128)(2,1)S(1)}, bf16[256,1552]{0,1:T(8,128)(2,1)S(1)}, u32[]{:S(2)}, u32[]{:S(2)}) collective-permute-start(bf16[256,1552]{0,1:T(8,128)(2,1)S(1)} %copy-done.77), channel_id=1, source_target_pairs={{0,3},{1,2},{2,1},{3,0},{4,7},{5,6},{6,5},{7,4},{8,11},{9,10},{10,... | collective-permute-start | bytes 2383880 | tf_op jit(solution)/shard_map/ppermute | solution.py:78
  131.2 49.9 %collective-permute-start.2 = (bf16[256,1552]{0,1:T(8,128)(2,1)}, bf16[256,1552]{0,1:T(8,128)(2,1)}, u32[]{:S(2)}, u32[]{:S(2)}) collective-permute-start(bf16[256,1552]{0,1:T(8,128)(2,1)} %pad_maximum_fusion.3), channel_id=1, source_target_pairs={{0,1},{1,0},{2,3},{3,2},{4,5},{5,4},{6,7},{7,6},{8,9},{9,8},{10,11... | collective-permute-start | bytes 2383880 | tf_op jit(solution)/shard_map/ppermute | solution.py:78
  134.0 29.2 %copy-start.125 = (f32[16]{0:T(128)S(1)}, f32[16]{0:T(128)}, u32[]{:S(2)}) copy-start(f32[16]{0:T(128)} %copy-done.124) | copy-start | bytes 196
  175.3 22.1 %collective-permute-start.11 = (bf16[256,1552]{0,1:T(8,128)(2,1)S(1)}, bf16[256,1552]{0,1:T(8,128)(2,1)S(1)}, u32[]{:S(2)}, u32[]{:S(2)}) collective-permute-start(bf16[256,1552]{0,1:T(8,128)(2,1)S(1)} %copy-done.76), channel_id=1, source_target_pairs={{0,14},{1,15},{2,12},{3,13},{4,2},{5,3},{6,0},{7,1},{8,6},{9,7},{1... | collective-permute-start | bytes 2383880 | tf_op jit(solution)/shard_map/ppermute | solution.py:77
  177.9 36.5 %collective-permute-start.12 = (bf16[256,1552]{0,1:T(8,128)(2,1)S(1)}, bf16[256,1552]{0,1:T(8,128)(2,1)S(1)}, u32[]{:S(2)}, u32[]{:S(2)}) collective-permute-start(bf16[256,1552]{0,1:T(8,128)(2,1)S(1)} %copy-done.78), channel_id=1, source_target_pairs={{0,15},{1,14},{2,13},{3,12},{4,3},{5,2},{6,1},{7,0},{8,7},{9,6},{1... | collective-permute-start | bytes 2383880 | tf_op jit(solution)/shard_map/ppermute | solution.py:78
  182.6 31.9 %copy-start.8 = (bf16[256,1552]{0,1:T(8,128)(2,1)}, bf16[256,1552]{0,1:T(8,128)(2,1)S(1)}, u32[]{:S(2)}) copy-start(bf16[256,1552]{0,1:T(8,128)(2,1)S(1)} %get-tuple-element.139) | copy-start | bytes 2383876
  182.6 31.9 %copy-start.10 = (bf16[256,1552]{0,1:T(8,128)(2,1)}, bf16[256,1552]{0,1:T(8,128)(2,1)S(1)}, u32[]{:S(2)}) copy-start(bf16[256,1552]{0,1:T(8,128)(2,1)S(1)} %get-tuple-element.140) | copy-start | bytes 2383876
  184.1 30.4 %copy-start.121 = (f32[16]{0:T(128)S(1)}, f32[16]{0:T(128)}, u32[]{:S(2)}) copy-start(f32[16]{0:T(128)} %copy-done.119) | copy-start | bytes 196
  184.1 30.4 %copy-start.126 = (f32[16]{0:T(128)S(1)}, f32[16]{0:T(128)}, u32[]{:S(2)}) copy-start(f32[16]{0:T(128)} %copy-done.124) | copy-start | bytes 196
  237.2 24.5 %collective-permute-start.15 = (bf16[256,1552]{0,1:T(8,128)(2,1)S(1)}, bf16[256,1552]{0,1:T(8,128)(2,1)S(1)}, u32[]{:S(2)}, u32[]{:S(2)}) collective-permute-start(bf16[256,1552]{0,1:T(8,128)(2,1)S(1)} %copy-done.74), channel_id=1, source_target_pairs={{0,10},{1,11},{2,8},{3,9},{4,14},{5,15},{6,12},{7,13},{8,2},{9,3},... | collective-permute-start | bytes 2383880 | tf_op jit(solution)/shard_map/ppermute | solution.py:77
  240.4 37.4 %collective-permute-start.16 = (bf16[256,1552]{0,1:T(8,128)(2,1)S(1)}, bf16[256,1552]{0,1:T(8,128)(2,1)S(1)}, u32[]{:S(2)}, u32[]{:S(2)}) collective-permute-start(bf16[256,1552]{0,1:T(8,128)(2,1)S(1)} %copy-done.73), channel_id=1, source_target_pairs={{0,11},{1,10},{2,9},{3,8},{4,15},{5,14},{6,13},{7,12},{8,3},{9,2},... | collective-permute-start | bytes 2383880 | tf_op jit(solution)/shard_map/ppermute | solution.py:78
  248.1 63.7 %collective-permute-start.5 = (bf16[256,1552]{0,1:T(8,128)(2,1)S(1)}, bf16[256,1552]{0,1:T(8,128)(2,1)S(1)}, u32[]{:S(2)}, u32[]{:S(2)}) collective-permute-start(bf16[256,1552]{0,1:T(8,128)(2,1)S(1)} %get-tuple-element.17), channel_id=1, source_target_pairs={{0,12},{1,13},{2,14},{3,15},{4,0},{5,1},{6,2},{7,3},{8,4},{9,5},{1... | collective-permute-start | bytes 2383880 | tf_op jit(solution)/shard_map/ppermute | solution.py:77
  250.8 61.0 %collective-permute-start.6 = (bf16[256,1552]{0,1:T(8,128)(2,1)S(1)}, bf16[256,1552]{0,1:T(8,128)(2,1)S(1)}, u32[]{:S(2)}, u32[]{:S(2)}) collective-permute-start(bf16[256,1552]{0,1:T(8,128)(2,1)S(1)} %get-tuple-element.18), channel_id=1, source_target_pairs={{0,13},{1,12},{2,15},{3,14},{4,1},{5,0},{6,3},{7,2},{8,5},{9,4},{1... | collective-permute-start | bytes 2383880 | tf_op jit(solution)/shard_map/ppermute | solution.py:78
  277.9 168.1 %copy-start.12 = (bf16[256,1552]{0,1:T(8,128)(2,1)}, bf16[256,1552]{0,1:T(8,128)(2,1)S(1)}, u32[]{:S(2)}) copy-start(bf16[256,1552]{0,1:T(8,128)(2,1)S(1)} %get-tuple-element.125) | copy-start | bytes 2383876
  277.9 168.1 %copy-start.14 = (bf16[256,1552]{0,1:T(8,128)(2,1)}, bf16[256,1552]{0,1:T(8,128)(2,1)S(1)}, u32[]{:S(2)}) copy-start(bf16[256,1552]{0,1:T(8,128)(2,1)S(1)} %get-tuple-element.126) | copy-start | bytes 2383876
  279.4 32.5 %copy-start.122 = (f32[16]{0:T(128)S(1)}, f32[16]{0:T(128)}, u32[]{:S(2)}) copy-start(f32[16]{0:T(128)} %copy-done.119) | copy-start | bytes 196
  279.4 32.5 %copy-start.127 = (f32[16]{0:T(128)S(1)}, f32[16]{0:T(128)}, u32[]{:S(2)}) copy-start(f32[16]{0:T(128)} %copy-done.124) | copy-start | bytes 196
  334.6 23.4 %collective-permute-start.9 = (bf16[256,1552]{0,1:T(8,128)(2,1)S(1)}, bf16[256,1552]{0,1:T(8,128)(2,1)S(1)}, u32[]{:S(2)}, u32[]{:S(2)}) collective-permute-start(bf16[256,1552]{0,1:T(8,128)(2,1)S(1)} %copy-done.69), channel_id=1, source_target_pairs={{0,6},{1,7},{2,4},{3,5},{4,10},{5,11},{6,8},{7,9},{8,14},{9,15},{1... | collective-permute-start | bytes 2383880 | tf_op jit(solution)/shard_map/ppermute | solution.py:77
  335.9 39.0 %collective-permute-start.10 = (bf16[256,1552]{0,1:T(8,128)(2,1)S(1)}, bf16[256,1552]{0,1:T(8,128)(2,1)S(1)}, u32[]{:S(2)}, u32[]{:S(2)}) collective-permute-start(bf16[256,1552]{0,1:T(8,128)(2,1)S(1)} %copy-done.71), channel_id=1, source_target_pairs={{0,7},{1,6},{2,5},{3,4},{4,11},{5,10},{6,9},{7,8},{8,15},{9,14},{1... | collective-permute-start | bytes 2383880 | tf_op jit(solution)/shard_map/ppermute | solution.py:78
  338.8 36.2 %copy-start.123 = (f32[16]{0:T(128)S(1)}, f32[16]{0:T(128)}, u32[]{:S(2)}) copy-start(f32[16]{0:T(128)} %copy-done.119) | copy-start | bytes 196
  338.8 36.2 %copy-start.128 = (f32[16]{0:T(128)S(1)}, f32[16]{0:T(128)}, u32[]{:S(2)}) copy-start(f32[16]{0:T(128)} %copy-done.124) | copy-start | bytes 196
  393.6 38.2 %collective-permute-start.13 = (bf16[256,1552]{0,1:T(8,128)(2,1)S(1)}, bf16[256,1552]{0,1:T(8,128)(2,1)S(1)}, u32[]{:S(2)}, u32[]{:S(2)}) collective-permute-start(bf16[256,1552]{0,1:T(8,128)(2,1)S(1)} %copy-done.70), channel_id=1, source_target_pairs={{0,8},{1,9},{2,10},{3,11},{4,12},{5,13},{6,14},{7,15},{8,0},{9,1},... | collective-permute-start | bytes 2383880 | tf_op jit(solution)/shard_map/ppermute | solution.py:77
  393.8 38.0 %collective-permute-start.14 = (bf16[256,1552]{0,1:T(8,128)(2,1)S(1)}, bf16[256,1552]{0,1:T(8,128)(2,1)S(1)}, u32[]{:S(2)}, u32[]{:S(2)}) collective-permute-start(bf16[256,1552]{0,1:T(8,128)(2,1)S(1)} %copy-done.72), channel_id=1, source_target_pairs={{0,9},{1,8},{2,11},{3,10},{4,13},{5,12},{6,15},{7,14},{8,1},{9,0},... | collective-permute-start | bytes 2383880 | tf_op jit(solution)/shard_map/ppermute | solution.py:78
  397.8 39.0 %copy-start.64 = (f32[16,4,128]{2,0,1:T(8,128)S(1)}, f32[16,4,128]{2,0,1:T(8,128)}, u32[]{:S(2)}) copy-start(f32[16,4,128]{2,0,1:T(8,128)} %copy-done.63) | copy-start | bytes 98308
  (123 other events, 518.0 us)
Sparse Core Ops, SparseCore 0:
  453.1 48.6 all-gather.2

commit v6 on v2

--- a/solution.py
+++ b/solution.py
@@ -27,22 +27,30 @@
     )
     padded = jnp.concatenate([rim, conv_input], 0)
     taps = conv_weight.astype(f32)
-    total = padded[0:rows].astype(f32) * taps[0]
-    for k in range(1, CONV):
-        total = total + padded[k : k + rows].astype(f32) * taps[k]
-    act = jax.nn.silu(total + conv_bias).astype(jnp.bfloat16)
 
     def payload(target):
         group = target // repeat_count
-        return jnp.concatenate(
-            [
-                lax.dynamic_slice_in_dim(act, target * slab, slab, 1),
-                lax.dynamic_slice_in_dim(act, x_width + group * STATE, STATE, 1),
-                lax.dynamic_slice_in_dim(act, x_width + (GROUPS + group) * STATE, STATE, 1),
-                lax.dynamic_slice_in_dim(dt_raw, target * heads_dev, heads_dev, 1),
-            ],
-            1,
-        )
+
+        def pick(table):
+            last = table.ndim - 1
+            return jnp.concatenate(
+                [
+                    lax.dynamic_slice_in_dim(table, target * slab, slab, last),
+                    lax.dynamic_slice_in_dim(table, x_width + group * STATE, STATE, last),
+                    lax.dynamic_slice_in_dim(
+                        table, x_width + (GROUPS + group) * STATE, STATE, last
+                    ),
+                ],
+                last,
+            )
+
+        window, kernel = pick(padded), pick(taps)
+        total = window[0:rows].astype(f32) * kernel[0]
+        for k in range(1, CONV):
+            total = total + window[k : k + rows].astype(f32) * kernel[k]
+        act = jax.nn.silu(total + pick(conv_bias)).astype(jnp.bfloat16)
+        steps = lax.dynamic_slice_in_dim(dt_raw, target * heads_dev, heads_dev, 1)
+        return jnp.concatenate([act, steps], 1)
 
     rate = -jnp.exp(lax.dynamic_slice_in_dim(a_log, head_pos * heads_dev, heads_dev, 0))
     bias = lax.dynamic_slice_in_dim(dt_bias, head_pos * heads_dev, heads_dev, 0)

time: 592 us -> 595 us (level)
  waiting for transfers between devices: 181 us -> 158 us
  other arithmetic: 123 us -> 145 us
    concatenate x10 -> x49, other arithmetic: 8.44 us -> 26.9 us  [the longest x16 13.5 us: payload(): return jnp.concatenate([act, steps], 1)]
    ppermute x8, waiting for transfers between devices: 65.9 us -> 49.9 us  [on_device(): r_other = lax.ppermute(p_other, 'head', other)]
    unnamed x293 -> x283, local copies, waits for them, and re-layouts: 27.1 us -> 34.7 us
    ppermute x8, waiting for transfers between devices: 115 us -> 108 us  [on_device(): r_same = lax.ppermute(p_same, 'head', same)]
    unnamed x12 -> x13, other arithmetic: 16.9 us -> 18.2 us
    convert_element_type x1 -> x17, other arithmetic: 36.7 us -> 37.1 us  [the longest x16 37.1 us: payload(): act = jax.nn.silu(total + pick(conv_bias)).astype(jnp.bfloat16)]
  transfers between devices with their start and end apart: 18 -> 18, of which waited for: 11 -> 9; matrix products, arithmetic and copies ran while one was open for 32% -> 39% of each run, Pallas kernels for 0% -> 0%
where the time goes in v6:
time: 595 us; the launch traced here: 585 us
  waiting for transfers between devices  158 us (27%)
  other arithmetic  145 us (24%)
  local copies, waits for them, and re-layouts  144 us (24%)
  matrix products  84.7 us (14%)
  starting transfers between devices  36.4 us (6%)
  between operations  17.2 us (3%)
    ppermute x8, waiting for transfers between devices, on_device(): r_same = lax.ppermute(p_same, 'head', same)  108 us
    ppermute x8, waiting for transfers between devices, on_device(): r_other = lax.ppermute(p_other, 'head', other)  49.9 us
    dot_general x8, matrix products, on_device(): jnp.einsum('hts,shp->thp', mix, x_heads, preferred_element_type=f32)  39.9 us
    convert_element_type x16, other arithmetic, payload(): act = jax.nn.silu(total + pick(conv_bias)).astype(jnp.bfloat16)  37.1 us
    unnamed x283, local copies, waits for them, and re-layouts  34.7 us
    dot_general x1, matrix products, on_device(): jnp.einsum('bqn,bnc->bqc', c_acc.astype(f32), full_state, precision=lax.P...  24 us
    broadcast_in_dim x8, local copies, waits for them, and re-layouts, on_device(): y_acc = lax.dynamic_update_index_in_dim(y_acc, y_now, k, 0)  19.9 us
    another operation x24, other arithmetic  19.2 us
  transfers between devices with their start and end apart: 18, of which 9 were waited for; matrix products, arithmetic and copies ran while one was open for 39% of the time, Pallas kernels for 0%

profile of v6, /device:TPU:30, one launch (start us, length us, event | category | flops | bytes accessed | tf_op | source)
XLA Modules:
  0.0 584.8 jit_solution(2949844651595493871)
XLA Ops:
  7.6 3.7 collective-permute-start
  18.0 13.9 %copy.471 = bf16[256,20480]{0,1:T(8,128)(2,1)} copy(bf16[256,20480]{1,0:T(8,128)(2,1)} %param.7) | data formatting | bytes 20971520 | tf_op args[0]
  37.8 3.6 copy.470
  62.7 7.2 %collective-permute-start.1 = (bf16[256,1552]{0,1:T(8,128)(2,1)}, bf16[256,1552]{0,1:T(8,128)(2,1)}, u32[]{:S(2)}, u32[]{:S(2)}) collective-permute-start(bf16[256,1552]{0,1:T(8,128)(2,1)} %pad_maximum_fusion.17), channel_id=1, source_target_pairs={{0,0},{1,1},{2,2},{3,3},{4,4},{5,5},{6,6},{7,7},{8,8},{9,9},{10,10... | collective-permute-start | bytes 2383880 | tf_op jit(solution)/shard_map/ppermute | solution.py:77
  118.9 3.6 reduce-window.56
  129.6 4.9 fusion.4
  136.2 4.2 collective-permute-start.7
  144.9 13.4 %collective-permute-done.7 = bf16[256,1552]{0,1:T(8,128)(2,1)S(1)} collective-permute-done((bf16[256,1552]{0,1:T(8,128)(2,1)S(1)}, bf16[256,1552]{0,1:T(8,128)(2,1)S(1)}, u32[]{:S(2)}, u32[]{:S(2)}) %collective-permute-start.7) | collective-permute-done | bytes 794656 | tf_op jit(solution)/shard_map/ppermute | solution.py:77
  158.3 16.9 %collective-permute-done.8 = bf16[256,1552]{0,1:T(8,128)(2,1)S(1)} collective-permute-done((bf16[256,1552]{0,1:T(8,128)(2,1)S(1)}, bf16[256,1552]{0,1:T(8,128)(2,1)S(1)}, u32[]{:S(2)}, u32[]{:S(2)}) %collective-permute-start.8) | collective-permute-done | bytes 794656 | tf_op jit(solution)/shard_map/ppermute | solution.py:78
  178.5 5.0 fusion.6
  195.2 15.0 %collective-permute-done.11 = bf16[256,1552]{0,1:T(8,128)(2,1)S(1)} collective-permute-done((bf16[256,1552]{0,1:T(8,128)(2,1)S(1)}, bf16[256,1552]{0,1:T(8,128)(2,1)S(1)}, u32[]{:S(2)}, u32[]{:S(2)}) %collective-permute-start.11) | collective-permute-done | bytes 794656 | tf_op jit(solution)/shard_map/ppermute | solution.py:77
  210.2 16.9 %collective-permute-done.12 = bf16[256,1552]{0,1:T(8,128)(2,1)S(1)} collective-permute-done((bf16[256,1552]{0,1:T(8,128)(2,1)S(1)}, bf16[256,1552]{0,1:T(8,128)(2,1)S(1)}, u32[]{:S(2)}, u32[]{:S(2)}) %collective-permute-start.12) | collective-permute-done | bytes 794656 | tf_op jit(solution)/shard_map/ppermute | solution.py:78
  235.5 5.0 fusion.8
  240.6 5.0 fusion.3
  252.0 4.5 broadcast_in_dim.363
  261.2 10.0 %collective-permute-done.15 = bf16[256,1552]{0,1:T(8,128)(2,1)S(1)} collective-permute-done((bf16[256,1552]{0,1:T(8,128)(2,1)S(1)}, bf16[256,1552]{0,1:T(8,128)(2,1)S(1)}, u32[]{:S(2)}, u32[]{:S(2)}) %collective-permute-start.15) | collective-permute-done | bytes 794656 | tf_op jit(solution)/shard_map/ppermute | solution.py:77
  271.1 16.0 %collective-permute-done.16 = bf16[256,1552]{0,1:T(8,128)(2,1)S(1)} collective-permute-done((bf16[256,1552]{0,1:T(8,128)(2,1)S(1)}, bf16[256,1552]{0,1:T(8,128)(2,1)S(1)}, u32[]{:S(2)}, u32[]{:S(2)}) %collective-permute-start.16) | collective-permute-done | bytes 794656 | tf_op jit(solution)/shard_map/ppermute | solution.py:78
  288.8 6.4 %collective-permute-done.5 = bf16[256,1552]{0,1:T(8,128)(2,1)S(1)} collective-permute-done((bf16[256,1552]{0,1:T(8,128)(2,1)S(1)}, bf16[256,1552]{0,1:T(8,128)(2,1)S(1)}, u32[]{:S(2)}, u32[]{:S(2)}) %collective-permute-start.5) | collective-permute-done | bytes 794656 | tf_op jit(solution)/shard_map/ppermute | solution.py:77
  304.3 5.0 fusion.10
  309.3 5.0 fusion.5
  323.2 31.8 %collective-permute-done.9 = bf16[256,1552]{0,1:T(8,128)(2,1)S(1)} collective-permute-done((bf16[256,1552]{0,1:T(8,128)(2,1)S(1)}, bf16[256,1552]{0,1:T(8,128)(2,1)S(1)}, u32[]{:S(2)}, u32[]{:S(2)}) %collective-permute-start.9) | collective-permute-done | bytes 794656 | tf_op jit(solution)/shard_map/ppermute | solution.py:77
  368.0 4.9 fusion.7
  379.3 31.5 %collective-permute-done.13 = bf16[256,1552]{0,1:T(8,128)(2,1)S(1)} collective-permute-done((bf16[256,1552]{0,1:T(8,128)(2,1)S(1)}, bf16[256,1552]{0,1:T(8,128)(2,1)S(1)}, u32[]{:S(2)}, u32[]{:S(2)}) %collective-permute-start.13) | collective-permute-done | bytes 794656 | tf_op jit(solution)/shard_map/ppermute | solution.py:77
  426.7 4.4 fusion.54
  453.0 8.1 %broadcast_in_dim.330 = f32[8,512,1024]{2,1,0:T(8,128)} broadcast(f32[]{:T(128)} %constant.440.clone.1), dimensions={} | broadcast | bytes 16777220 | tf_op jit(solution)/shard_map/broadcast_in_dim | solution.py:64
  473.4 3.3 constant_dynamic-update-slice_fusion.21
  483.7 3.3 constant_dynamic-update-slice_fusion.19
  490.6 4.9 fusion.9
  499.1 7.9 %broadcast_in_dim.351 = f32[8,512,16,64]{1,3,2,0:T(8,128)} broadcast(f32[8,512,16]{1,2,0:T(8,128)S(1)} %exp.294), dimensions={0,1,2} | broadcast | bytes 17039360 | tf_op jit(solution)/shard_map/broadcast_in_dim | solution.py:133
  506.9 16.4 %copy.520 = f32[8,512,1024]{2,1,0:T(8,128)} copy(f32[8,512,1024]{1,2,0:T(8,128)} %bitcast.386) | data formatting | bytes 33554432 | tf_op jit(solution)/shard_map/exp | solution.py:133
  548.9 4.6 fusion
  553.5 24.0 %add_convert_fusion = bf16[8,512,1024]{2,1,0:T(8,128)(2,1)} fusion(f32[8,512,1024]{2,1,0:T(8,128)} %constant_dynamic-update-slice_fusion.16, f32[8,512,1024]{2,1,0:T(8,128)} %copy.520, bf16[8,512,256]{2,1,0:T(8,128)(2,1)} %constant_dynamic-update-slice_fusion, f32[8,256,1024]{2,1,0:T(8,128)} %add_dynamic-update-slice_fusion, f32[256,1024]{1,0:T(8,128)S(1)} %fusion, ...), kind=kOutput, calls=%fused_computation.96 | convolution fusion | flops 12901679104 | bytes 53510144 | tf_op jit(solution)/shard_map/bqn,bnc->bqc/dot_general | solution.py:134
  (600 shorter events, 257.1 us)
Async XLA Ops:
  6.5 540.1 %all-gather.3.cloned.1.call-start = ((), (), s32[]{:S(2)}) async-start(), calls=%async_computation | async-start | bytes 9732096 | tf_op jit(solution)/shard_map/all_gather | solution.py:117
  7.6 30.2 %collective-permute-start = (bf16[3,20480]{1,0:T(4,128)(2,1)S(1)}, bf16[3,20480]{1,0:T(4,128)(2,1)S(1)}, u32[]{:S(2)}, u32[]{:S(2)}) collective-permute-start(bf16[3,20480]{1,0:T(4,128)(2,1)S(1)} %slice.631), channel_id=1, source_target_pairs={{0,1},{1,2},{2,3},{3,4},{4,5},{5,6},{6,7},{7,8},{8,9},{9,10},{10,1... | collective-permute-start | bytes 368648 | tf_op jit(solution)/shard_map/ppermute | solution.py:25
  17.9 13.9 %copy-start.127 = (f32[256]{0:T(256)S(1)}, f32[256]{0:T(256)}, u32[]{:S(2)}) copy-start(f32[256]{0:T(256)} %param.12) | copy-start | bytes 3076
  17.9 14.6 %copy-start.128 = (f32[256]{0:T(256)S(1)}, f32[256]{0:T(256)}, u32[]{:S(2)}) copy-start(f32[256]{0:T(256)} %param.13) | copy-start | bytes 3076
  59.4 132.9 %collective-permute-start.2 = (bf16[256,1552]{0,1:T(8,128)(2,1)}, bf16[256,1552]{0,1:T(8,128)(2,1)}, u32[]{:S(2)}, u32[]{:S(2)}) collective-permute-start(bf16[256,1552]{0,1:T(8,128)(2,1)} %pad_maximum_fusion.18), channel_id=1, source_target_pairs={{0,1},{1,0},{2,3},{3,2},{4,5},{5,4},{6,7},{7,6},{8,9},{9,8},{10,11... | collective-permute-start | bytes 2383880 | tf_op jit(solution)/shard_map/ppermute | solution.py:78
  62.7 129.6 %collective-permute-start.1 = (bf16[256,1552]{0,1:T(8,128)(2,1)}, bf16[256,1552]{0,1:T(8,128)(2,1)}, u32[]{:S(2)}, u32[]{:S(2)}) collective-permute-start(bf16[256,1552]{0,1:T(8,128)(2,1)} %pad_maximum_fusion.17), channel_id=1, source_target_pairs={{0,0},{1,1},{2,2},{3,3},{4,4},{5,5},{6,6},{7,7},{8,8},{9,9},{10,10... | collective-permute-start | bytes 2383880 | tf_op jit(solution)/shard_map/ppermute | solution.py:77
  72.4 43.6 %collective-permute-start.4 = (bf16[256,1552]{0,1:T(8,128)(2,1)S(1)}, bf16[256,1552]{0,1:T(8,128)(2,1)S(1)}, u32[]{:S(2)}, u32[]{:S(2)}) collective-permute-start(bf16[256,1552]{0,1:T(8,128)(2,1)S(1)} %pad_maximum_fusion.20), channel_id=1, source_target_pairs={{0,3},{1,2},{2,5},{3,4},{4,7},{5,6},{6,9},{7,8},{8,11},{9,10},{10,... | collective-permute-start | bytes 2383880 | tf_op jit(solution)/shard_map/ppermute | solution.py:78
  77.7 38.2 %collective-permute-start.3 = (bf16[256,1552]{0,1:T(8,128)(2,1)S(1)}, bf16[256,1552]{0,1:T(8,128)(2,1)S(1)}, u32[]{:S(2)}, u32[]{:S(2)}) collective-permute-start(bf16[256,1552]{0,1:T(8,128)(2,1)S(1)} %pad_maximum_fusion.19), channel_id=1, source_target_pairs={{0,2},{1,3},{2,4},{3,5},{4,6},{5,7},{6,8},{7,9},{8,10},{9,11},{10,... | collective-permute-start | bytes 2383880 | tf_op jit(solution)/shard_map/ppermute | solution.py:77
  116.1 12.0 %copy-start.1 = (bf16[256,1552]{0,1:T(8,128)(2,1)}, bf16[256,1552]{0,1:T(8,128)(2,1)S(1)}, u32[]{:S(2)}) copy-start(bf16[256,1552]{0,1:T(8,128)(2,1)S(1)} %get-tuple-element.201) | copy-start | bytes 2383876
  116.1 12.0 %copy-start.3 = (bf16[256,1552]{0,1:T(8,128)(2,1)}, bf16[256,1552]{0,1:T(8,128)(2,1)S(1)}, u32[]{:S(2)}) copy-start(bf16[256,1552]{0,1:T(8,128)(2,1)S(1)} %get-tuple-element.202) | copy-start | bytes 2383876
  136.2 22.1 %collective-permute-start.7 = (bf16[256,1552]{0,1:T(8,128)(2,1)S(1)}, bf16[256,1552]{0,1:T(8,128)(2,1)S(1)}, u32[]{:S(2)}, u32[]{:S(2)}) collective-permute-start(bf16[256,1552]{0,1:T(8,128)(2,1)S(1)} %copy-done.75), channel_id=1, source_target_pairs={{0,6},{1,7},{2,8},{3,9},{4,10},{5,11},{6,12},{7,13},{8,14},{9,15},... | collective-permute-start | bytes 2383880 | tf_op jit(solution)/shard_map/ppermute | solution.py:77
  140.4 34.9 %collective-permute-start.8 = (bf16[256,1552]{0,1:T(8,128)(2,1)S(1)}, bf16[256,1552]{0,1:T(8,128)(2,1)S(1)}, u32[]{:S(2)}, u32[]{:S(2)}) collective-permute-start(bf16[256,1552]{0,1:T(8,128)(2,1)S(1)} %copy-done.73), channel_id=1, source_target_pairs={{0,7},{1,6},{2,9},{3,8},{4,11},{5,10},{6,13},{7,12},{8,15},{9,14},... | collective-permute-start | bytes 2383880 | tf_op jit(solution)/shard_map/ppermute | solution.py:78
  144.9 30.4 %copy-start.115 = (f32[16]{0:T(128)S(1)}, f32[16]{0:T(128)}, u32[]{:S(2)}) copy-start(f32[16]{0:T(128)} %exponential_negate_fusion) | copy-start | bytes 196
  144.9 30.4 %copy-start.119 = (f32[16]{0:T(128)S(1)}, f32[16]{0:T(128)}, u32[]{:S(2)}) copy-start(f32[16]{0:T(128)} %dynamic_slice.510) | copy-start | bytes 196
  186.6 23.6 %collective-permute-start.11 = (bf16[256,1552]{0,1:T(8,128)(2,1)S(1)}, bf16[256,1552]{0,1:T(8,128)(2,1)S(1)}, u32[]{:S(2)}, u32[]{:S(2)}) collective-permute-start(bf16[256,1552]{0,1:T(8,128)(2,1)S(1)} %copy-done.69), channel_id=1, source_target_pairs={{0,10},{1,11},{2,12},{3,13},{4,14},{5,15},{6,0},{7,1},{8,2},{9,3},... | collective-permute-start | bytes 2383880 | tf_op jit(solution)/shard_map/ppermute | solution.py:77
  189.0 38.2 %collective-permute-start.12 = (bf16[256,1552]{0,1:T(8,128)(2,1)S(1)}, bf16[256,1552]{0,1:T(8,128)(2,1)S(1)}, u32[]{:S(2)}, u32[]{:S(2)}) collective-permute-start(bf16[256,1552]{0,1:T(8,128)(2,1)S(1)} %copy-done.70), channel_id=1, source_target_pairs={{0,11},{1,10},{2,13},{3,12},{4,15},{5,14},{6,1},{7,0},{8,3},{9,2},... | collective-permute-start | bytes 2383880 | tf_op jit(solution)/shard_map/ppermute | solution.py:78
  193.7 33.6 %copy-start.9 = (bf16[256,1552]{0,1:T(8,128)(2,1)}, bf16[256,1552]{0,1:T(8,128)(2,1)S(1)}, u32[]{:S(2)}) copy-start(bf16[256,1552]{0,1:T(8,128)(2,1)S(1)} %get-tuple-element.203) | copy-start | bytes 2383876
  193.7 33.6 %copy-start.11 = (bf16[256,1552]{0,1:T(8,128)(2,1)}, bf16[256,1552]{0,1:T(8,128)(2,1)S(1)}, u32[]{:S(2)}) copy-start(bf16[256,1552]{0,1:T(8,128)(2,1)S(1)} %get-tuple-element.204) | copy-start | bytes 2383876
  248.1 23.0 %collective-permute-start.15 = (bf16[256,1552]{0,1:T(8,128)(2,1)S(1)}, bf16[256,1552]{0,1:T(8,128)(2,1)S(1)}, u32[]{:S(2)}, u32[]{:S(2)}) collective-permute-start(bf16[256,1552]{0,1:T(8,128)(2,1)S(1)} %copy-done.68), channel_id=1, source_target_pairs={{0,14},{1,15},{2,0},{3,1},{4,2},{5,3},{6,4},{7,5},{8,6},{9,7},{10,... | collective-permute-start | bytes 2383880 | tf_op jit(solution)/shard_map/ppermute | solution.py:77
  248.1 39.1 %collective-permute-start.16 = (bf16[256,1552]{0,1:T(8,128)(2,1)S(1)}, bf16[256,1552]{0,1:T(8,128)(2,1)S(1)}, u32[]{:S(2)}, u32[]{:S(2)}) collective-permute-start(bf16[256,1552]{0,1:T(8,128)(2,1)S(1)} %copy-done.67), channel_id=1, source_target_pairs={{0,15},{1,14},{2,1},{3,0},{4,3},{5,2},{6,5},{7,4},{8,7},{9,6},{10,... | collective-permute-start | bytes 2383880 | tf_op jit(solution)/shard_map/ppermute | solution.py:78
  257.9 37.3 %collective-permute-start.5 = (bf16[256,1552]{0,1:T(8,128)(2,1)S(1)}, bf16[256,1552]{0,1:T(8,128)(2,1)S(1)}, u32[]{:S(2)}, u32[]{:S(2)}) collective-permute-start(bf16[256,1552]{0,1:T(8,128)(2,1)S(1)} %copy-done.66), channel_id=1, source_target_pairs={{0,4},{1,5},{2,6},{3,7},{4,8},{5,9},{6,10},{7,11},{8,12},{9,13},{1... | collective-permute-start | bytes 2383880 | tf_op jit(solution)/shard_map/ppermute | solution.py:77
  259.7 35.5 %collective-permute-start.6 = (bf16[256,1552]{0,1:T(8,128)(2,1)S(1)}, bf16[256,1552]{0,1:T(8,128)(2,1)S(1)}, u32[]{:S(2)}, u32[]{:S(2)}) collective-permute-start(bf16[256,1552]{0,1:T(8,128)(2,1)S(1)} %copy-done.72), channel_id=1, source_target_pairs={{0,5},{1,4},{2,7},{3,6},{4,9},{5,8},{6,11},{7,10},{8,13},{9,12},{1... | collective-permute-start | bytes 2383880 | tf_op jit(solution)/shard_map/ppermute | solution.py:78
  287.3 138.0 %copy-start.13 = (bf16[256,1552]{0,1:T(8,128)(2,1)}, bf16[256,1552]{0,1:T(8,128)(2,1)S(1)}, u32[]{:S(2)}) copy-start(bf16[256,1552]{0,1:T(8,128)(2,1)S(1)} %get-tuple-element.189) | copy-start | bytes 2383876
  287.3 138.0 %copy-start.15 = (bf16[256,1552]{0,1:T(8,128)(2,1)}, bf16[256,1552]{0,1:T(8,128)(2,1)S(1)}, u32[]{:S(2)}) copy-start(bf16[256,1552]{0,1:T(8,128)(2,1)S(1)} %get-tuple-element.190) | copy-start | bytes 2383876
  318.3 36.8 %collective-permute-start.9 = (bf16[256,1552]{0,1:T(8,128)(2,1)S(1)}, bf16[256,1552]{0,1:T(8,128)(2,1)S(1)}, u32[]{:S(2)}, u32[]{:S(2)}) collective-permute-start(bf16[256,1552]{0,1:T(8,128)(2,1)S(1)} %copy-done.71), channel_id=1, source_target_pairs={{0,8},{1,9},{2,10},{3,11},{4,12},{5,13},{6,14},{7,15},{8,0},{9,1},... | collective-permute-start | bytes 2383880 | tf_op jit(solution)/shard_map/ppermute | solution.py:77
  319.2 35.8 %collective-permute-start.10 = (bf16[256,1552]{0,1:T(8,128)(2,1)S(1)}, bf16[256,1552]{0,1:T(8,128)(2,1)S(1)}, u32[]{:S(2)}, u32[]{:S(2)}) collective-permute-start(bf16[256,1552]{0,1:T(8,128)(2,1)S(1)} %copy-done.74), channel_id=1, source_target_pairs={{0,9},{1,8},{2,11},{3,10},{4,13},{5,12},{6,15},{7,14},{8,1},{9,0},... | collective-permute-start | bytes 2383880 | tf_op jit(solution)/shard_map/ppermute | solution.py:78
  323.2 32.0 %copy-start.116 = (f32[16]{0:T(128)S(1)}, f32[16]{0:T(128)}, u32[]{:S(2)}) copy-start(f32[16]{0:T(128)} %exponential_negate_fusion) | copy-start | bytes 196
  323.2 32.0 %copy-start.121 = (f32[16]{0:T(128)S(1)}, f32[16]{0:T(128)}, u32[]{:S(2)}) copy-start(f32[16]{0:T(128)} %dynamic_slice.510) | copy-start | bytes 196
  376.2 34.6 %collective-permute-start.13 = (bf16[256,1552]{0,1:T(8,128)(2,1)S(1)}, bf16[256,1552]{0,1:T(8,128)(2,1)S(1)}, u32[]{:S(2)}, u32[]{:S(2)}) collective-permute-start(bf16[256,1552]{0,1:T(8,128)(2,1)S(1)} %copy-done.64), channel_id=1, source_target_pairs={{0,12},{1,13},{2,14},{3,15},{4,0},{5,1},{6,2},{7,3},{8,4},{9,5},{1... | collective-permute-start | bytes 2383880 | tf_op jit(solution)/shard_map/ppermute | solution.py:77
  376.3 34.6 %collective-permute-start.14 = (bf16[256,1552]{0,1:T(8,128)(2,1)S(1)}, bf16[256,1552]{0,1:T(8,128)(2,1)S(1)}, u32[]{:S(2)}, u32[]{:S(2)}) collective-permute-start(bf16[256,1552]{0,1:T(8,128)(2,1)S(1)} %copy-done.65), channel_id=1, source_target_pairs={{0,13},{1,12},{2,15},{3,14},{4,1},{5,0},{6,3},{7,2},{8,5},{9,4},{1... | collective-permute-start | bytes 2383880 | tf_op jit(solution)/shard_map/ppermute | solution.py:78
  379.3 32.5 %copy-start.117 = (f32[16]{0:T(128)S(1)}, f32[16]{0:T(128)}, u32[]{:S(2)}) copy-start(f32[16]{0:T(128)} %exponential_negate_fusion) | copy-start | bytes 196
  379.3 32.5 %copy-start.122 = (f32[16]{0:T(128)S(1)}, f32[16]{0:T(128)}, u32[]{:S(2)}) copy-start(f32[16]{0:T(128)} %dynamic_slice.510) | copy-start | bytes 196
  (118 other events, 353.1 us)
Sparse Core Ops, SparseCore 0:
  432.4 49.1 all-gather.2

commit v7 on v2

--- a/solution.py
+++ b/solution.py
@@ -64,8 +64,8 @@
         t_same = 2 * ((head_pos // 2 + m) % pairs) + parity
         t_other = 2 * ((head_pos // 2 + m) % pairs) + 1 - parity
         p_same, p_other = payload(t_same), payload(t_other)
-        if m >= 2:
-            p_same, p_other, _ = lax.optimization_barrier((p_same, p_other, done[m - 2]))
+        if m >= 4:
+            p_same, p_other, _ = lax.optimization_barrier((p_same, p_other, done[m - 4]))
         r_same = lax.ppermute(p_same, "head", same)
         r_other = lax.ppermute(p_other, "head", other)
         first = jnp.where(parity == 0, r_same, r_other)

time: 592 us -> 578 us (0.976)
  waiting for transfers between devices: 181 us -> 105 us
  starting transfers between devices: 36.8 us -> 78.4 us
  other arithmetic: 123 us -> 149 us
    ppermute x8, waiting for transfers between devices: 115 us -> 65.2 us  [on_device(): r_same = lax.ppermute(p_same, 'head', same)]
    ppermute x8, waiting for transfers between devices: 65.9 us -> 39.5 us  [on_device(): r_other = lax.ppermute(p_other, 'head', other)]
    ppermute x8, starting transfers between devices: 22.3 us -> 43.9 us  [on_device(): r_same = lax.ppermute(p_same, 'head', same)]
    ppermute x8, starting transfers between devices: 10.8 us -> 30.7 us  [on_device(): r_other = lax.ppermute(p_other, 'head', other)]
    another operation x24, other arithmetic: 14.5 us -> 30 us
    another operation x22, local copies, waits for them, and re-layouts: 3.71 us -> 10.9 us
    unnamed x293 -> x247, local copies, waits for them, and re-layouts: 27.1 us -> 26.3 us
    unnamed x12 -> x9, other arithmetic: 16.9 us -> 17.5 us
  transfers between devices with their start and end apart: 18 -> 18, of which waited for: 11 -> 4; matrix products, arithmetic and copies ran while one was open for 32% -> 33% of each run, Pallas kernels for 0% -> 0%
where the time goes in v7:
time: 578 us; the launch traced here: 572 us
  other arithmetic  149 us (26%)
  local copies, waits for them, and re-layouts  138 us (24%)
  waiting for transfers between devices  105 us (18%)
  matrix products  87.2 us (15%)
  starting transfers between devices  78.4 us (14%)
  between operations  15.7 us (3%)
    ppermute x8, waiting for transfers between devices, on_device(): r_same = lax.ppermute(p_same, 'head', same)  65.2 us
    ppermute x8, starting transfers between devices, on_device(): r_same = lax.ppermute(p_same, 'head', same)  43.9 us
    dot_general x8, matrix products, on_device(): jnp.einsum('hts,shp->thp', mix, x_heads, preferred_element_type=f32)  41.6 us
    ppermute x8, waiting for transfers between devices, on_device(): r_other = lax.ppermute(p_other, 'head', other)  39.5 us
    convert_element_type x1, other arithmetic, on_device(): act = jax.nn.silu(total + conv_bias).astype(jnp.bfloat16)  36.6 us
    ppermute x8, starting transfers between devices, on_device(): r_other = lax.ppermute(p_other, 'head', other)  30.7 us
    another operation x24, other arithmetic  30 us
    unnamed x247, local copies, waits for them, and re-layouts  26.3 us
  transfers between devices with their start and end apart: 18, of which 4 were waited for; matrix products, arithmetic and copies ran while one was open for 33% of the time, Pallas kernels for 0%

profile of v7, /device:TPU:30, one launch (start us, length us, event | category | flops | bytes accessed | tf_op | source)
XLA Modules:
  0.0 572.5 jit_solution(16078004299729561000)
XLA Ops:
  7.6 3.7 collective-permute-start
  11.7 13.7 %copy.474 = bf16[256,20480]{0,1:T(8,128)(2,1)} copy(bf16[256,20480]{1,0:T(8,128)(2,1)} %param.7) | data formatting | bytes 20971520 | tf_op args[0]
  28.5 3.6 copy.473
  32.2 36.6 %multiply_convert_fusion = bf16[256,20480]{0,1:T(8,128)(2,1)S(1)} fusion(bf16[256,20480]{0,1:T(8,128)(2,1)} %copy.474, bf16[3,20480]{0,1:T(8,128)(2,1)} %copy.473, f32[20480]{0:T(1024)S(1)} %copy-done.89, f32[20480]{0:T(1024)S(1)} %bitcast.411, f32[20480]{0:T(1024)S(1)} %bitcast.410, f32[20480]{0:T(1024)S(1)} %bitcast.409, f32[20480]{0:T(1024)S(1)} %bitcast.408), kind=kLoop, calls=%fused_computation | loop fusion | flops 136314880 | bytes 21504000 | tf_op jit(solution)/shard_map/convert_element_type | solution.py:33
  70.0 4.4 collective-permute-start.7
  87.2 7.1 %collective-permute-done.7 = bf16[256,1552]{0,1:T(8,128)(2,1)S(1)} collective-permute-done((bf16[256,1552]{0,1:T(8,128)(2,1)S(1)}, bf16[256,1552]{0,1:T(8,128)(2,1)S(1)}, u32[]{:S(2)}, u32[]{:S(2)}) %collective-permute-start.7) | collective-permute-done | bytes 794656 | tf_op jit(solution)/shard_map/ppermute | solution.py:69
  96.1 15.3 %collective-permute-done.8 = bf16[256,1552]{0,1:T(8,128)(2,1)S(1)} collective-permute-done((bf16[256,1552]{0,1:T(8,128)(2,1)S(1)}, bf16[256,1552]{0,1:T(8,128)(2,1)S(1)}, u32[]{:S(2)}, u32[]{:S(2)}) %collective-permute-start.8) | collective-permute-done | bytes 794656 | tf_op jit(solution)/shard_map/ppermute | solution.py:70
  126.5 5.0 fusion.8
  131.5 5.0 fusion.5
  140.4 14.3 %collective-permute-start.15 = (bf16[256,1552]{0,1:T(8,128)(2,1)S(1)}, bf16[256,1552]{0,1:T(8,128)(2,1)S(1)}, u32[]{:S(2)}, u32[]{:S(2)}) collective-permute-start(bf16[256,1552]{0,1:T(8,128)(2,1)S(1)} %copy-done.71), channel_id=1, source_target_pairs={{0,14},{1,15},{2,0},{3,1},{4,2},{5,3},{6,4},{7,5},{8,6},{9,7},{10,... | collective-permute-start | bytes 2383880 | tf_op jit(solution)/shard_map/ppermute | solution.py:69
  154.7 4.5 broadcast_in_dim.348
  166.5 14.6 %collective-permute-start.10 = (bf16[256,1552]{0,1:T(8,128)(2,1)S(1)}, bf16[256,1552]{0,1:T(8,128)(2,1)S(1)}, u32[]{:S(2)}, u32[]{:S(2)}) collective-permute-start(bf16[256,1552]{0,1:T(8,128)(2,1)S(1)} %copy-done.68), channel_id=1, source_target_pairs={{0,9},{1,8},{2,11},{3,10},{4,13},{5,12},{6,15},{7,14},{8,1},{9,0},... | collective-permute-start | bytes 2383880 | tf_op jit(solution)/shard_map/ppermute | solution.py:70
  184.0 24.2 %collective-permute-done.16 = bf16[256,1552]{0,1:T(8,128)(2,1)S(1)} collective-permute-done((bf16[256,1552]{0,1:T(8,128)(2,1)S(1)}, bf16[256,1552]{0,1:T(8,128)(2,1)S(1)}, u32[]{:S(2)}, u32[]{:S(2)}) %collective-permute-start.16) | collective-permute-done | bytes 794656 | tf_op jit(solution)/shard_map/ppermute | solution.py:70
  255.1 4.9 fusion.12
  260.2 4.9 fusion.6
  265.2 6.0 %fusion.7 = f32[16,64,512]{2,1,0:T(8,128)} fusion(bf16[512,16,64]{0,2,1:T(8,128)(2,1)S(1)} %bitcast.404, f32[16,512]{1,0:T(8,128)S(1)} %bitcast.415, f32[16,512]{1,0:T(8,128)S(1)} %copy-done.94, f32[512,512]{1,0:T(8,128)S(1)} %copy-done.61, pred[512,512]{1,0:T(8,128)(4,1)S(1)} %copy-done.74), kind=kOutput, calls=%fused_computation.23 | convolution fusion | flops 557842432 | bytes 4521984 | tf_op jit(solution)/shard_map/hts,shp->thp/dot_general | solution.py:85
  271.1 5.7 fusion.9
  276.8 6.8 %fusion.41 = (f32[1,512,1024]{1,2,0:T(8,128)}, f32[512,1024]{0,1:T(8,128)}, f32[512,1024]{0,1:T(8,128)}, f32[1,512,1024]{1,2,0:T(8,128)}) fusion(bf16[512,1024]{0,1:T(8,128)(2,1)S(1)} %copy-done.46, f32[16,64,512]{2,1,0:T(8,128)S(1)} %fusion.12, f32[1024]{0:T(1024)S(1)} %mul.778, bf16[512,1024]{0,1:T(8,128)(2,1)S(1)} %copy-done.47, ...), kind=kLoop, calls=%fused_computation.73 | loop fusion | flops 6291456 | bytes 20975616 | tf_op jit(solution)/shard_map/jit(dynamic_update_index_in_dim)/broadcast_in_dim | solution.py:92
  283.6 23.6 %collective-permute-start.13 = (bf16[256,1552]{0,1:T(8,128)(2,1)}, bf16[256,1552]{0,1:T(8,128)(2,1)S(1)}, u32[]{:S(2)}, u32[]{:S(2)}) collective-permute-start(bf16[256,1552]{0,1:T(8,128)(2,1)} %get-tuple-element.17), channel_id=1, source_target_pairs={{0,12},{1,13},{2,14},{3,15},{4,0},{5,1},{6,2},{7,3},{8,4},{9,5},{1... | collective-permute-start | bytes 2383880 | tf_op jit(solution)/shard_map/ppermute | solution.py:69
  307.2 7.7 %collective-permute-start.12 = (bf16[256,1552]{0,1:T(8,128)(2,1)}, bf16[256,1552]{0,1:T(8,128)(2,1)S(1)}, u32[]{:S(2)}, u32[]{:S(2)}) collective-permute-start(bf16[256,1552]{0,1:T(8,128)(2,1)} %get-tuple-element.16), channel_id=1, source_target_pairs={{0,11},{1,10},{2,13},{3,12},{4,15},{5,14},{6,1},{7,0},{8,3},{9,2},... | collective-permute-start | bytes 2383880 | tf_op jit(solution)/shard_map/ppermute | solution.py:70
  317.7 58.0 %collective-permute-done.13 = bf16[256,1552]{0,1:T(8,128)(2,1)S(1)} collective-permute-done((bf16[256,1552]{0,1:T(8,128)(2,1)}, bf16[256,1552]{0,1:T(8,128)(2,1)S(1)}, u32[]{:S(2)}, u32[]{:S(2)}) %collective-permute-start.13) | collective-permute-done | bytes 794656 | tf_op jit(solution)/shard_map/ppermute | solution.py:69
  402.7 4.4 fusion.60
  427.8 8.1 %broadcast_in_dim.315 = f32[8,512,1024]{2,1,0:T(8,128)} broadcast(f32[]{:T(128)} %constant.425.clone.1), dimensions={} | broadcast | bytes 16777220 | tf_op jit(solution)/shard_map/broadcast_in_dim | solution.py:56
  445.1 3.2 copy.515
  451.8 3.4 constant_dynamic-update-slice_fusion.14
  464.8 5.0 fusion.11
  469.9 5.0 fusion.10
  480.4 3.2 copy.510
  483.6 7.9 %broadcast_in_dim.336 = f32[8,512,16,64]{1,3,2,0:T(8,128)} broadcast(f32[8,512,16]{1,2,0:T(8,128)S(1)} %copy-done.56), dimensions={0,1,2} | broadcast | bytes 17039360 | tf_op jit(solution)/shard_map/broadcast_in_dim | solution.py:125
  491.5 16.4 %copy.524 = f32[8,512,1024]{2,1,0:T(8,128)} copy(f32[8,512,1024]{1,2,0:T(8,128)} %bitcast.392) | data formatting | bytes 33554432 | tf_op jit(solution)/shard_map/exp | solution.py:125
  537.1 4.6 fusion.2
  541.7 23.7 %add_convert_fusion = bf16[8,512,1024]{2,1,0:T(8,128)(2,1)} fusion(f32[8,512,1024]{2,1,0:T(8,128)} %constant_dynamic-update-slice_fusion.8, f32[8,512,1024]{2,1,0:T(8,128)} %copy.524, bf16[8,512,256]{2,1,0:T(8,128)(2,1)} %constant_dynamic-update-slice_fusion, f32[8,256,1024]{2,1,0:T(8,128)} %add_dynamic-update-slice_fusion, f32[256,1024]{1,0:T(8,128)S(1)} %fusion.2, ...), kind=kOutput, calls=%fused_computation.3 | convolution fusion | flops 12901679104 | bytes 53510144 | tf_op jit(solution)/shard_map/bqn,bnc->bqc/dot_general | solution.py:126
  (483 shorter events, 202.2 us)
Async XLA Ops:
  6.5 528.3 %all-gather.3.cloned.1.call-start = ((), (), s32[]{:S(2)}) async-start(), calls=%async_computation | async-start | bytes 9732096 | tf_op jit(solution)/shard_map/all_gather | solution.py:109
  7.6 20.9 %collective-permute-start = (bf16[3,20480]{1,0:T(4,128)(2,1)S(1)}, bf16[3,20480]{1,0:T(4,128)(2,1)S(1)}, u32[]{:S(2)}, u32[]{:S(2)}) collective-permute-start(bf16[3,20480]{1,0:T(4,128)(2,1)S(1)} %slice.268), channel_id=1, source_target_pairs={{0,1},{1,2},{2,3},{3,4},{4,5},{5,6},{6,7},{7,8},{8,9},{9,10},{10,1... | collective-permute-start | bytes 368648 | tf_op jit(solution)/shard_map/ppermute | solution.py:25
  11.6 13.8 %copy-start.112 = (f32[256]{0:T(256)S(1)}, f32[256]{0:T(256)}, u32[]{:S(2)}) copy-start(f32[256]{0:T(256)} %param.12) | copy-start | bytes 3076
  11.6 13.9 %copy-start.41 = (bf16[256,256]{1,0:T(8,128)(2,1)S(1)}, bf16[256,256]{1,0:T(8,128)(2,1)}, u32[]{:S(2)}) copy-start(bf16[256,256]{1,0:T(8,128)(2,1)} %param.8) | copy-start | bytes 393220
  25.4 91.3 %copy-start.98 = (f32[16]{0:T(128)}, f32[16]{0:T(128)S(1)}, u32[]{:S(2)}) copy-start(f32[16]{0:T(128)S(1)} %exponential_negate_fusion) | copy-start | bytes 196
  25.5 91.2 %copy-start.101 = (f32[16]{0:T(128)}, f32[16]{0:T(128)S(1)}, u32[]{:S(2)}) copy-start(f32[16]{0:T(128)S(1)} %dynamic_slice.210) | copy-start | bytes 196
  28.5 103.0 %copy-start.73 = (pred[512,512]{1,0:T(8,128)(4,1)}, pred[512,512]{1,0:T(8,128)(4,1)S(1)}, u32[]{:S(2)}) copy-start(pred[512,512]{1,0:T(8,128)(4,1)S(1)} %iota_compare_fusion) | copy-start | bytes 786436
  70.0 24.3 %collective-permute-start.7 = (bf16[256,1552]{0,1:T(8,128)(2,1)S(1)}, bf16[256,1552]{0,1:T(8,128)(2,1)S(1)}, u32[]{:S(2)}, u32[]{:S(2)}) collective-permute-start(bf16[256,1552]{0,1:T(8,128)(2,1)S(1)} %pad_maximum_fusion.8), channel_id=1, source_target_pairs={{0,6},{1,7},{2,8},{3,9},{4,10},{5,11},{6,12},{7,13},{8,14},{9,15},... | collective-permute-start | bytes 2383880 | tf_op jit(solution)/shard_map/ppermute | solution.py:69
  74.8 36.6 %collective-permute-start.8 = (bf16[256,1552]{0,1:T(8,128)(2,1)S(1)}, bf16[256,1552]{0,1:T(8,128)(2,1)S(1)}, u32[]{:S(2)}, u32[]{:S(2)}) collective-permute-start(bf16[256,1552]{0,1:T(8,128)(2,1)S(1)} %pad_maximum_fusion.9), channel_id=1, source_target_pairs={{0,7},{1,6},{2,9},{3,8},{4,11},{5,10},{6,13},{7,12},{8,15},{9,14},... | collective-permute-start | bytes 2383880 | tf_op jit(solution)/shard_map/ppermute | solution.py:70
  77.7 35.8 %collective-permute-start.1 = (bf16[256,1552]{0,1:T(8,128)(2,1)S(1)}, bf16[256,1552]{0,1:T(8,128)(2,1)S(1)}, u32[]{:S(2)}, u32[]{:S(2)}) collective-permute-start(bf16[256,1552]{0,1:T(8,128)(2,1)S(1)} %pad_maximum_fusion.2), channel_id=1, source_target_pairs={{0,0},{1,1},{2,2},{3,3},{4,4},{5,5},{6,6},{7,7},{8,8},{9,9},{10,10... | collective-permute-start | bytes 2383880 | tf_op jit(solution)/shard_map/ppermute | solution.py:69
  77.9 37.4 %collective-permute-start.2 = (bf16[256,1552]{0,1:T(8,128)(2,1)S(1)}, bf16[256,1552]{0,1:T(8,128)(2,1)S(1)}, u32[]{:S(2)}, u32[]{:S(2)}) collective-permute-start(bf16[256,1552]{0,1:T(8,128)(2,1)S(1)} %pad_maximum_fusion.3), channel_id=1, source_target_pairs={{0,1},{1,0},{2,3},{3,2},{4,5},{5,4},{6,7},{7,6},{8,9},{9,8},{10,11... | collective-permute-start | bytes 2383880 | tf_op jit(solution)/shard_map/ppermute | solution.py:70
  78.9 81.8 %collective-permute-start.3 = (bf16[256,1552]{0,1:T(8,128)(2,1)}, bf16[256,1552]{0,1:T(8,128)(2,1)}, u32[]{:S(2)}, u32[]{:S(2)}) collective-permute-start(bf16[256,1552]{0,1:T(8,128)(2,1)} %pad_maximum_fusion.4), channel_id=1, source_target_pairs={{0,2},{1,3},{2,4},{3,5},{4,6},{5,7},{6,8},{7,9},{8,10},{9,11},{10,... | collective-permute-start | bytes 2383880 | tf_op jit(solution)/shard_map/ppermute | solution.py:69
  94.3 68.3 %collective-permute-start.4 = (bf16[256,1552]{0,1:T(8,128)(2,1)}, bf16[256,1552]{0,1:T(8,128)(2,1)}, u32[]{:S(2)}, u32[]{:S(2)}) collective-permute-start(bf16[256,1552]{0,1:T(8,128)(2,1)} %pad_maximum_fusion.5), channel_id=1, source_target_pairs={{0,3},{1,2},{2,5},{3,4},{4,7},{5,6},{6,9},{7,8},{8,11},{9,10},{10,... | collective-permute-start | bytes 2383880 | tf_op jit(solution)/shard_map/ppermute | solution.py:70
  111.4 54.7 %collective-permute-start.5 = (bf16[256,1552]{0,1:T(8,128)(2,1)}, bf16[256,1552]{0,1:T(8,128)(2,1)}, u32[]{:S(2)}, u32[]{:S(2)}) collective-permute-start(bf16[256,1552]{0,1:T(8,128)(2,1)} %pad_maximum_fusion.6), channel_id=1, source_target_pairs={{0,4},{1,5},{2,6},{3,7},{4,8},{5,9},{6,10},{7,11},{8,12},{9,13},{1... | collective-permute-start | bytes 2383880 | tf_op jit(solution)/shard_map/ppermute | solution.py:69
  113.5 67.5 %collective-permute-start.6 = (bf16[256,1552]{0,1:T(8,128)(2,1)}, bf16[256,1552]{0,1:T(8,128)(2,1)}, u32[]{:S(2)}, u32[]{:S(2)}) collective-permute-start(bf16[256,1552]{0,1:T(8,128)(2,1)} %pad_maximum_fusion.7), channel_id=1, source_target_pairs={{0,5},{1,4},{2,7},{3,6},{4,9},{5,8},{6,11},{7,10},{8,13},{9,12},{1... | collective-permute-start | bytes 2383880 | tf_op jit(solution)/shard_map/ppermute | solution.py:70
  140.4 43.6 %collective-permute-start.15 = (bf16[256,1552]{0,1:T(8,128)(2,1)S(1)}, bf16[256,1552]{0,1:T(8,128)(2,1)S(1)}, u32[]{:S(2)}, u32[]{:S(2)}) collective-permute-start(bf16[256,1552]{0,1:T(8,128)(2,1)S(1)} %copy-done.71), channel_id=1, source_target_pairs={{0,14},{1,15},{2,0},{3,1},{4,2},{5,3},{6,4},{7,5},{8,6},{9,7},{10,... | collective-permute-start | bytes 2383880 | tf_op jit(solution)/shard_map/ppermute | solution.py:69
  160.7 47.5 %collective-permute-start.16 = (bf16[256,1552]{0,1:T(8,128)(2,1)S(1)}, bf16[256,1552]{0,1:T(8,128)(2,1)S(1)}, u32[]{:S(2)}, u32[]{:S(2)}) collective-permute-start(bf16[256,1552]{0,1:T(8,128)(2,1)S(1)} %copy-done.70), channel_id=1, source_target_pairs={{0,15},{1,14},{2,1},{3,0},{4,3},{5,2},{6,5},{7,4},{8,7},{9,6},{10,... | collective-permute-start | bytes 2383880 | tf_op jit(solution)/shard_map/ppermute | solution.py:70
  162.7 47.2 %collective-permute-start.9 = (bf16[256,1552]{0,1:T(8,128)(2,1)S(1)}, bf16[256,1552]{0,1:T(8,128)(2,1)S(1)}, u32[]{:S(2)}, u32[]{:S(2)}) collective-permute-start(bf16[256,1552]{0,1:T(8,128)(2,1)S(1)} %copy-done.69), channel_id=1, source_target_pairs={{0,8},{1,9},{2,10},{3,11},{4,12},{5,13},{6,14},{7,15},{8,0},{9,1},... | collective-permute-start | bytes 2383880 | tf_op jit(solution)/shard_map/ppermute | solution.py:69
  164.7 45.3 %copy-start.18 = (bf16[256,1552]{0,1:T(8,128)(2,1)}, bf16[256,1552]{0,1:T(8,128)(2,1)S(1)}, u32[]{:S(2)}) copy-start(bf16[256,1552]{0,1:T(8,128)(2,1)S(1)} %get-tuple-element.129) | copy-start | bytes 2383876
  164.7 45.3 %copy-start.20 = (bf16[256,1552]{0,1:T(8,128)(2,1)}, bf16[256,1552]{0,1:T(8,128)(2,1)S(1)}, u32[]{:S(2)}) copy-start(bf16[256,1552]{0,1:T(8,128)(2,1)S(1)} %get-tuple-element.130) | copy-start | bytes 2383876
  166.5 43.4 %collective-permute-start.10 = (bf16[256,1552]{0,1:T(8,128)(2,1)S(1)}, bf16[256,1552]{0,1:T(8,128)(2,1)S(1)}, u32[]{:S(2)}, u32[]{:S(2)}) collective-permute-start(bf16[256,1552]{0,1:T(8,128)(2,1)S(1)} %copy-done.68), channel_id=1, source_target_pairs={{0,9},{1,8},{2,11},{3,10},{4,13},{5,12},{6,15},{7,14},{8,1},{9,0},... | collective-permute-start | bytes 2383880 | tf_op jit(solution)/shard_map/ppermute | solution.py:70
  182.5 27.5 %copy-start.28 = (bf16[256,1552]{0,1:T(8,128)(2,1)}, bf16[256,1552]{0,1:T(8,128)(2,1)S(1)}, u32[]{:S(2)}) copy-start(bf16[256,1552]{0,1:T(8,128)(2,1)S(1)} %get-tuple-element.127) | copy-start | bytes 2383876
  182.5 27.5 %copy-start.31 = (bf16[256,1552]{0,1:T(8,128)(2,1)}, bf16[256,1552]{0,1:T(8,128)(2,1)S(1)}, u32[]{:S(2)}) copy-start(bf16[256,1552]{0,1:T(8,128)(2,1)S(1)} %get-tuple-element.128) | copy-start | bytes 2383876
  276.8 38.1 %copy-start.51 = (f32[256,1024]{1,0:T(8,128)S(1)}, f32[256,1024]{1,0:T(8,128)}, u32[]{:S(2)}) copy-start(f32[256,1024]{1,0:T(8,128)} %fusion.126) | copy-start | bytes 3145732
  283.6 32.4 %copy-start.66 = (f32[16,4,128]{2,0,1:T(8,128)S(1)}, f32[16,4,128]{2,0,1:T(8,128)}, u32[]{:S(2)}) copy-start(f32[16,4,128]{2,0,1:T(8,128)} %reduce-window.60) | copy-start | bytes 98308
  283.6 32.4 %copy-start.97 = (f32[16,4]{0,1:T(4,128)S(1)}, f32[16,4]{0,1:T(4,128)}, u32[]{:S(2)}) copy-start(f32[16,4]{0,1:T(4,128)} %copy-done.96) | copy-start | bytes 772
  283.6 32.5 %copy-start.23 = (bf16[256,1552]{0,1:T(8,128)(2,1)S(1)}, bf16[256,1552]{0,1:T(8,128)(2,1)}, u32[]{:S(2)}) copy-start(bf16[256,1552]{0,1:T(8,128)(2,1)} %copy-done.22) | copy-start | bytes 2383876
  283.6 32.5 %copy-start.26 = (bf16[256,1552]{0,1:T(8,128)(2,1)S(1)}, bf16[256,1552]{0,1:T(8,128)(2,1)}, u32[]{:S(2)}) copy-start(bf16[256,1552]{0,1:T(8,128)(2,1)} %copy-done.25) | copy-start | bytes 2383876
  283.6 92.1 %collective-permute-start.13 = (bf16[256,1552]{0,1:T(8,128)(2,1)}, bf16[256,1552]{0,1:T(8,128)(2,1)S(1)}, u32[]{:S(2)}, u32[]{:S(2)}) collective-permute-start(bf16[256,1552]{0,1:T(8,128)(2,1)} %get-tuple-element.17), channel_id=1, source_target_pairs={{0,12},{1,13},{2,14},{3,15},{4,0},{5,1},{6,2},{7,3},{8,4},{9,5},{1... | collective-permute-start | bytes 2383880 | tf_op jit(solution)/shard_map/ppermute | solution.py:69
  307.2 68.6 %collective-permute-start.14 = (bf16[256,1552]{0,1:T(8,128)(2,1)}, bf16[256,1552]{0,1:T(8,128)(2,1)S(1)}, u32[]{:S(2)}, u32[]{:S(2)}) collective-permute-start(bf16[256,1552]{0,1:T(8,128)(2,1)} %get-tuple-element.18), channel_id=1, source_target_pairs={{0,13},{1,12},{2,15},{3,14},{4,1},{5,0},{6,3},{7,2},{8,5},{9,4},{1... | collective-permute-start | bytes 2383880 | tf_op jit(solution)/shard_map/ppermute | solution.py:70
  307.2 68.7 %collective-permute-start.11 = (bf16[256,1552]{0,1:T(8,128)(2,1)}, bf16[256,1552]{0,1:T(8,128)(2,1)S(1)}, u32[]{:S(2)}, u32[]{:S(2)}) collective-permute-start(bf16[256,1552]{0,1:T(8,128)(2,1)} %get-tuple-element.15), channel_id=1, source_target_pairs={{0,10},{1,11},{2,12},{3,13},{4,14},{5,15},{6,0},{7,1},{8,2},{9,3},... | collective-permute-start | bytes 2383880 | tf_op jit(solution)/shard_map/ppermute | solution.py:69
  307.2 68.7 %collective-permute-start.12 = (bf16[256,1552]{0,1:T(8,128)(2,1)}, bf16[256,1552]{0,1:T(8,128)(2,1)S(1)}, u32[]{:S(2)}, u32[]{:S(2)}) collective-permute-start(bf16[256,1552]{0,1:T(8,128)(2,1)} %get-tuple-element.16), channel_id=1, source_target_pairs={{0,11},{1,10},{2,13},{3,12},{4,15},{5,14},{6,1},{7,0},{8,3},{9,2},... | collective-permute-start | bytes 2383880 | tf_op jit(solution)/shard_map/ppermute | solution.py:70
  (100 other events, 303.4 us)
Sparse Core Ops, SparseCore 0:
  408.4 50.3 all-gather.2

commit v8 on v7

--- a/solution.py
+++ b/solution.py
@@ -64,8 +64,8 @@
         t_same = 2 * ((head_pos // 2 + m) % pairs) + parity
         t_other = 2 * ((head_pos // 2 + m) % pairs) + 1 - parity
         p_same, p_other = payload(t_same), payload(t_other)
-        if m >= 4:
-            p_same, p_other, _ = lax.optimization_barrier((p_same, p_other, done[m - 4]))
+        if m >= 6:
+            p_same, p_other, _ = lax.optimization_barrier((p_same, p_other, done[m - 6]))
         r_same = lax.ppermute(p_same, "head", same)
         r_other = lax.ppermute(p_other, "head", other)
         first = jnp.where(parity == 0, r_same, r_other)

time: 578 us -> 590 us (1.021)
  starting transfers between devices: 78.4 us -> 89.6 us
    ppermute x8, starting transfers between devices: 43.9 us -> 73.8 us  [on_device(): r_same = lax.ppermute(p_same, 'head', same)]
    ppermute x8, waiting for transfers between devices: 65.2 us -> 37.7 us  [on_device(): r_same = lax.ppermute(p_same, 'head', same)]
    ppermute x8, waiting for transfers between devices: 39.5 us -> 66 us  [on_device(): r_other = lax.ppermute(p_other, 'head', other)]
    ppermute x8, starting transfers between devices: 30.7 us -> 12 us  [on_device(): r_other = lax.ppermute(p_other, 'head', other)]
    unnamed x9, other arithmetic: 17.5 us -> 8.63 us
    broadcast_in_dim x1, local copies, waits for them, and re-layouts: 8.06 us -> 2.13 us  [on_device(): y_acc = jnp.zeros((blocks, SPAN, slab), f32)]
    unnamed x247 -> x293, local copies, waits for them, and re-layouts: 26.3 us -> 32.1 us
  transfers between devices with their start and end apart: 18 -> 18, of which waited for: 4 -> 6; matrix products, arithmetic and copies ran while one was open for 33% -> 35% of each run, Pallas kernels for 0% -> 0%
where the time goes in v8:
time: 590 us; the launch traced here: 579 us
  other arithmetic  144 us (24%)
  local copies, waits for them, and re-layouts  141 us (24%)
  waiting for transfers between devices  104 us (18%)
  starting transfers between devices  89.6 us (15%)
  matrix products  85.3 us (14%)
  between operations  16 us (3%)
    ppermute x8, starting transfers between devices, on_device(): r_same = lax.ppermute(p_same, 'head', same)  73.8 us
    ppermute x8, waiting for transfers between devices, on_device(): r_other = lax.ppermute(p_other, 'head', other)  66 us
    dot_general x8, matrix products, on_device(): jnp.einsum('hts,shp->thp', mix, x_heads, preferred_element_type=f32)  41.7 us
    ppermute x8, waiting for transfers between devices, on_device(): r_same = lax.ppermute(p_same, 'head', same)  37.7 us
    convert_element_type x1, other arithmetic, on_device(): act = jax.nn.silu(total + conv_bias).astype(jnp.bfloat16)  36.6 us
    another operation x24, other arithmetic  32.6 us
    unnamed x293, local copies, waits for them, and re-layouts  32.1 us
    dot_general x1, matrix products, on_device(): jnp.einsum('bqn,bnc->bqc', c_acc.astype(f32), full_state, precision=lax.P...  23.7 us
  transfers between devices with their start and end apart: 18, of which 6 were waited for; matrix products, arithmetic and copies ran while one was open for 35% of the time, Pallas kernels for 0%

profile of v8, /device:TPU:30, one launch (start us, length us, event | category | flops | bytes accessed | tf_op | source)
XLA Modules:
  0.0 578.9 jit_solution(6771058535049529380)
XLA Ops:
  7.6 3.7 collective-permute-start
  11.7 14.1 %copy.474 = bf16[256,20480]{0,1:T(8,128)(2,1)} copy(bf16[256,20480]{1,0:T(8,128)(2,1)} %param.7) | data formatting | bytes 20971520 | tf_op args[0]
  28.9 3.6 copy.473
  32.6 36.6 %multiply_convert_fusion = bf16[256,20480]{0,1:T(8,128)(2,1)S(1)} fusion(bf16[256,20480]{0,1:T(8,128)(2,1)} %copy.474, bf16[3,20480]{0,1:T(8,128)(2,1)} %copy.473, f32[20480]{0:T(1024)S(1)} %copy-done.100, f32[20480]{0:T(1024)S(1)} %bitcast.417, f32[20480]{0:T(1024)S(1)} %bitcast.416, f32[20480]{0:T(1024)S(1)} %bitcast.415, f32[20480]{0:T(1024)S(1)} %bitcast.414), kind=kLoop, calls=%fused_computation | loop fusion | flops 136314880 | bytes 21504000 | tf_op jit(solution)/shard_map/convert_element_type | solution.py:33
  87.6 4.9 collective-permute-done.3
  94.1 14.0 %collective-permute-done.4 = bf16[256,1552]{0,1:T(8,128)(2,1)S(1)} collective-permute-done((bf16[256,1552]{0,1:T(8,128)(2,1)S(1)}, bf16[256,1552]{0,1:T(8,128)(2,1)S(1)}, u32[]{:S(2)}, u32[]{:S(2)}) %collective-permute-start.4) | collective-permute-done | bytes 794656 | tf_op jit(solution)/shard_map/ppermute | solution.py:70
  108.1 7.7 %collective-permute-start.7 = (bf16[256,1552]{0,1:T(8,128)(2,1)}, bf16[256,1552]{0,1:T(8,128)(2,1)}, u32[]{:S(2)}, u32[]{:S(2)}) collective-permute-start(bf16[256,1552]{0,1:T(8,128)(2,1)} %pad_maximum_fusion.8), channel_id=1, source_target_pairs={{0,6},{1,7},{2,8},{3,9},{4,10},{5,11},{6,12},{7,13},{8,14},{9,15},... | collective-permute-start | bytes 2383880 | tf_op jit(solution)/shard_map/ppermute | solution.py:69
  129.9 5.3 fusion.6
  135.2 5.0 fusion.5
  142.7 56.2 %collective-permute-start.11 = (bf16[256,1552]{0,1:T(8,128)(2,1)S(1)}, bf16[256,1552]{0,1:T(8,128)(2,1)S(1)}, u32[]{:S(2)}, u32[]{:S(2)}) collective-permute-start(bf16[256,1552]{0,1:T(8,128)(2,1)S(1)} %copy-done.83), channel_id=1, source_target_pairs={{0,10},{1,11},{2,12},{3,13},{4,14},{5,15},{6,0},{7,1},{8,2},{9,3},... | collective-permute-start | bytes 2383880 | tf_op jit(solution)/shard_map/ppermute | solution.py:69
  210.6 4.0 collective-permute-start.13
  216.0 18.4 %collective-permute-done.11 = bf16[256,1552]{0,1:T(8,128)(2,1)S(1)} collective-permute-done((bf16[256,1552]{0,1:T(8,128)(2,1)S(1)}, bf16[256,1552]{0,1:T(8,128)(2,1)S(1)}, u32[]{:S(2)}, u32[]{:S(2)}) %collective-permute-start.11) | collective-permute-done | bytes 794656 | tf_op jit(solution)/shard_map/ppermute | solution.py:69
  234.4 4.4 collective-permute-start.14
  238.8 42.0 %collective-permute-done.12 = bf16[256,1552]{0,1:T(8,128)(2,1)S(1)} collective-permute-done((bf16[256,1552]{0,1:T(8,128)(2,1)S(1)}, bf16[256,1552]{0,1:T(8,128)(2,1)S(1)}, u32[]{:S(2)}, u32[]{:S(2)}) %collective-permute-start.12) | collective-permute-done | bytes 794656 | tf_op jit(solution)/shard_map/ppermute | solution.py:70
  281.1 10.0 %collective-permute-done.16 = bf16[256,1552]{0,1:T(8,128)(2,1)S(1)} collective-permute-done((bf16[256,1552]{0,1:T(8,128)(2,1)S(1)}, bf16[256,1552]{0,1:T(8,128)(2,1)S(1)}, u32[]{:S(2)}, u32[]{:S(2)}) %collective-permute-start.16) | collective-permute-done | bytes 794656 | tf_op jit(solution)/shard_map/ppermute | solution.py:70
  291.3 14.3 %collective-permute-done.13 = bf16[256,1552]{0,1:T(8,128)(2,1)S(1)} collective-permute-done((bf16[256,1552]{0,1:T(8,128)(2,1)S(1)}, bf16[256,1552]{0,1:T(8,128)(2,1)S(1)}, u32[]{:S(2)}, u32[]{:S(2)}) %collective-permute-start.13) | collective-permute-done | bytes 794656 | tf_op jit(solution)/shard_map/ppermute | solution.py:69
  321.1 3.1 reduce-window.66
  331.1 3.2 reduce-window.70
  341.1 3.1 reduce-window.74
  384.0 4.4 fusion.64
  436.4 6.3 %fusion.12 = f32[16,64,512]{2,1,0:T(8,128)} fusion(bf16[512,16,64]{0,2,1:T(8,128)(2,1)S(1)} %bitcast.406, f32[16,512]{1,0:T(8,128)S(1)} %bitcast.423, f32[16,512]{1,0:T(8,128)S(1)} %copy-done.109, f32[512,512]{1,0:T(8,128)S(1)} %fusion.142, pred[512,512]{1,0:T(8,128)(4,1)S(1)} %copy-done.88), kind=kOutput, calls=%fused_computation.28 | convolution fusion | flops 557842432 | bytes 4521984 | tf_op jit(solution)/shard_map/hts,shp->thp/dot_general | solution.py:85
  442.8 5.0 fusion.7
  447.9 5.0 fusion.8
  452.9 5.1 fusion.9
  458.1 5.0 fusion.10
  463.1 5.0 fusion.11
  468.1 6.4 %fusion.43 = (f32[1,512,1024]{1,2,0:T(8,128)}, f32[1,512,1024]{1,2,0:T(8,128)}, f32[1,512,1024]{1,2,0:T(8,128)}, f32[1,512,1024]{1,2,0:T(8,128)}, f32[1,512,1024]{1,2,0:T(8,128)}, /*index=5*/f32[1,512,1024]{1,2,0:T(8,128)}) fusion(bf16[512,1024]{0,1:T(8,128)(2,1)S(1)} %copy-done.49, f32[16,64,512]{2,1,0:T(8,128)S(1)} %copy-done.62, f32[1024]{0:T(1024)S(1)} %mul.778, ...), kind=kLoop, calls=%fused_computation.75 | loop fusion | flops 9437184 | bytes 31461376 | tf_op jit(solution)/shard_map/jit(dynamic_update_index_in_dim)/broadcast_in_dim | solution.py:92
  492.2 8.0 %broadcast_in_dim.336 = f32[8,512,16,64]{1,3,2,0:T(8,128)} broadcast(f32[8,512,16]{1,2,0:T(8,128)S(1)} %copy-done.63), dimensions={0,1,2} | broadcast | bytes 17039360 | tf_op jit(solution)/shard_map/broadcast_in_dim | solution.py:125
  500.1 16.4 %copy.524 = f32[8,512,1024]{2,1,0:T(8,128)} copy(f32[8,512,1024]{1,2,0:T(8,128)} %bitcast.400) | data formatting | bytes 33554432 | tf_op jit(solution)/shard_map/exp | solution.py:125
  518.9 3.3 constant_dynamic-update-slice_fusion.13
  543.4 4.7 fusion.2
  548.1 23.7 %add_convert_fusion = bf16[8,512,1024]{2,1,0:T(8,128)(2,1)} fusion(f32[8,512,1024]{2,1,0:T(8,128)} %constant_dynamic-update-slice_fusion.8, f32[8,512,1024]{2,1,0:T(8,128)} %copy.524, bf16[8,512,256]{2,1,0:T(8,128)(2,1)S(1)} %copy-done.41, f32[8,256,1024]{2,1,0:T(8,128)} %add_dynamic-update-slice_fusion, f32[256,1024]{1,0:T(8,128)S(1)} %fusion.2, ...), kind=kOutput, calls=%fused_computation.3 | convolution fusion | flops 12901679104 | bytes 53510144 | tf_op jit(solution)/shard_map/bqn,bnc->bqc/dot_general | solution.py:126
  (529 shorter events, 210.8 us)
Async XLA Ops:
  6.5 534.5 %all-gather.3.cloned.1.call-start = ((), (), s32[]{:S(2)}) async-start(), calls=%async_computation | async-start | bytes 9732096 | tf_op jit(solution)/shard_map/all_gather | solution.py:109
  7.6 21.3 %collective-permute-start = (bf16[3,20480]{1,0:T(4,128)(2,1)S(1)}, bf16[3,20480]{1,0:T(4,128)(2,1)S(1)}, u32[]{:S(2)}, u32[]{:S(2)}) collective-permute-start(bf16[3,20480]{1,0:T(4,128)(2,1)S(1)} %slice.268), channel_id=1, source_target_pairs={{0,1},{1,2},{2,3},{3,4},{4,5},{5,6},{6,7},{7,8},{8,9},{9,10},{10,1... | collective-permute-start | bytes 368648 | tf_op jit(solution)/shard_map/ppermute | solution.py:25
  25.8 94.3 %copy-start.121 = (f32[16]{0:T(128)}, f32[16]{0:T(128)S(1)}, u32[]{:S(2)}) copy-start(f32[16]{0:T(128)S(1)} %exponential_negate_fusion) | copy-start | bytes 196
  25.9 94.2 %copy-start.123 = (f32[16]{0:T(128)}, f32[16]{0:T(128)S(1)}, u32[]{:S(2)}) copy-start(f32[16]{0:T(128)S(1)} %dynamic_slice.210) | copy-start | bytes 196
  28.9 106.3 %copy-start.87 = (pred[512,512]{1,0:T(8,128)(4,1)}, pred[512,512]{1,0:T(8,128)(4,1)S(1)}, u32[]{:S(2)}) copy-start(pred[512,512]{1,0:T(8,128)(4,1)S(1)} %iota_compare_fusion) | copy-start | bytes 786436
  70.4 22.2 %collective-permute-start.3 = (bf16[256,1552]{0,1:T(8,128)(2,1)S(1)}, bf16[256,1552]{0,1:T(8,128)(2,1)S(1)}, u32[]{:S(2)}, u32[]{:S(2)}) collective-permute-start(bf16[256,1552]{0,1:T(8,128)(2,1)S(1)} %pad_maximum_fusion.4), channel_id=1, source_target_pairs={{0,2},{1,3},{2,4},{3,5},{4,6},{5,7},{6,8},{7,9},{8,10},{9,11},{10,... | collective-permute-start | bytes 2383880 | tf_op jit(solution)/shard_map/ppermute | solution.py:69
  72.9 35.2 %collective-permute-start.4 = (bf16[256,1552]{0,1:T(8,128)(2,1)S(1)}, bf16[256,1552]{0,1:T(8,128)(2,1)S(1)}, u32[]{:S(2)}, u32[]{:S(2)}) collective-permute-start(bf16[256,1552]{0,1:T(8,128)(2,1)S(1)} %pad_maximum_fusion.5), channel_id=1, source_target_pairs={{0,3},{1,2},{2,5},{3,4},{4,7},{5,6},{6,9},{7,8},{8,11},{9,10},{10,... | collective-permute-start | bytes 2383880 | tf_op jit(solution)/shard_map/ppermute | solution.py:70
  74.8 42.6 %collective-permute-start.1 = (bf16[256,1552]{0,1:T(8,128)(2,1)S(1)}, bf16[256,1552]{0,1:T(8,128)(2,1)S(1)}, u32[]{:S(2)}, u32[]{:S(2)}) collective-permute-start(bf16[256,1552]{0,1:T(8,128)(2,1)S(1)} %pad_maximum_fusion.2), channel_id=1, source_target_pairs={{0,0},{1,1},{2,2},{3,3},{4,4},{5,5},{6,6},{7,7},{8,8},{9,9},{10,10... | collective-permute-start | bytes 2383880 | tf_op jit(solution)/shard_map/ppermute | solution.py:69
  75.0 42.5 %collective-permute-start.2 = (bf16[256,1552]{0,1:T(8,128)(2,1)S(1)}, bf16[256,1552]{0,1:T(8,128)(2,1)S(1)}, u32[]{:S(2)}, u32[]{:S(2)}) collective-permute-start(bf16[256,1552]{0,1:T(8,128)(2,1)S(1)} %pad_maximum_fusion.3), channel_id=1, source_target_pairs={{0,1},{1,0},{2,3},{3,2},{4,5},{5,4},{6,7},{7,6},{8,9},{9,8},{10,11... | collective-permute-start | bytes 2383880 | tf_op jit(solution)/shard_map/ppermute | solution.py:70
  76.6 63.6 %collective-permute-start.5 = (bf16[256,1552]{0,1:T(8,128)(2,1)}, bf16[256,1552]{0,1:T(8,128)(2,1)}, u32[]{:S(2)}, u32[]{:S(2)}) collective-permute-start(bf16[256,1552]{0,1:T(8,128)(2,1)} %pad_maximum_fusion.6), channel_id=1, source_target_pairs={{0,4},{1,5},{2,6},{3,7},{4,8},{5,9},{6,10},{7,11},{8,12},{9,13},{1... | collective-permute-start | bytes 2383880 | tf_op jit(solution)/shard_map/ppermute | solution.py:69
  92.6 50.1 %collective-permute-start.6 = (bf16[256,1552]{0,1:T(8,128)(2,1)}, bf16[256,1552]{0,1:T(8,128)(2,1)}, u32[]{:S(2)}, u32[]{:S(2)}) collective-permute-start(bf16[256,1552]{0,1:T(8,128)(2,1)} %pad_maximum_fusion.7), channel_id=1, source_target_pairs={{0,5},{1,4},{2,7},{3,6},{4,9},{5,8},{6,11},{7,10},{8,13},{9,12},{1... | collective-permute-start | bytes 2383880 | tf_op jit(solution)/shard_map/ppermute | solution.py:70
  108.1 97.1 %collective-permute-start.7 = (bf16[256,1552]{0,1:T(8,128)(2,1)}, bf16[256,1552]{0,1:T(8,128)(2,1)}, u32[]{:S(2)}, u32[]{:S(2)}) collective-permute-start(bf16[256,1552]{0,1:T(8,128)(2,1)} %pad_maximum_fusion.8), channel_id=1, source_target_pairs={{0,6},{1,7},{2,8},{3,9},{4,10},{5,11},{6,12},{7,13},{8,14},{9,15},... | collective-permute-start | bytes 2383880 | tf_op jit(solution)/shard_map/ppermute | solution.py:69
  115.9 88.8 %copy-start.34 = (bf16[256,1552]{0,1:T(8,128)(2,1)}, bf16[256,1552]{0,1:T(8,128)(2,1)S(1)}, u32[]{:S(2)}) copy-start(bf16[256,1552]{0,1:T(8,128)(2,1)S(1)} %get-tuple-element.121) | copy-start | bytes 2383876
  115.9 88.7 %copy-start.35 = (bf16[256,1552]{0,1:T(8,128)(2,1)}, bf16[256,1552]{0,1:T(8,128)(2,1)S(1)}, u32[]{:S(2)}) copy-start(bf16[256,1552]{0,1:T(8,128)(2,1)S(1)} %get-tuple-element.122) | copy-start | bytes 2383876
  117.4 88.4 %collective-permute-start.8 = (bf16[256,1552]{0,1:T(8,128)(2,1)}, bf16[256,1552]{0,1:T(8,128)(2,1)}, u32[]{:S(2)}, u32[]{:S(2)}) collective-permute-start(bf16[256,1552]{0,1:T(8,128)(2,1)} %pad_maximum_fusion.9), channel_id=1, source_target_pairs={{0,7},{1,6},{2,9},{3,8},{4,11},{5,10},{6,13},{7,12},{8,15},{9,14},... | collective-permute-start | bytes 2383880 | tf_op jit(solution)/shard_map/ppermute | solution.py:70
  117.4 92.1 %collective-permute-start.9 = (bf16[256,1552]{0,1:T(8,128)(2,1)}, bf16[256,1552]{0,1:T(8,128)(2,1)}, u32[]{:S(2)}, u32[]{:S(2)}) collective-permute-start(bf16[256,1552]{0,1:T(8,128)(2,1)} %pad_maximum_fusion.10), channel_id=1, source_target_pairs={{0,8},{1,9},{2,10},{3,11},{4,12},{5,13},{6,14},{7,15},{8,0},{9,1},... | collective-permute-start | bytes 2383880 | tf_op jit(solution)/shard_map/ppermute | solution.py:69
  140.2 70.3 %collective-permute-start.10 = (bf16[256,1552]{0,1:T(8,128)(2,1)S(1)}, bf16[256,1552]{0,1:T(8,128)(2,1)S(1)}, u32[]{:S(2)}, u32[]{:S(2)}) collective-permute-start(bf16[256,1552]{0,1:T(8,128)(2,1)S(1)} %copy-done.84), channel_id=1, source_target_pairs={{0,9},{1,8},{2,11},{3,10},{4,13},{5,12},{6,15},{7,14},{8,1},{9,0},... | collective-permute-start | bytes 2383880 | tf_op jit(solution)/shard_map/ppermute | solution.py:70
  142.7 91.7 %collective-permute-start.11 = (bf16[256,1552]{0,1:T(8,128)(2,1)S(1)}, bf16[256,1552]{0,1:T(8,128)(2,1)S(1)}, u32[]{:S(2)}, u32[]{:S(2)}) collective-permute-start(bf16[256,1552]{0,1:T(8,128)(2,1)S(1)} %copy-done.83), channel_id=1, source_target_pairs={{0,10},{1,11},{2,12},{3,13},{4,14},{5,15},{6,0},{7,1},{8,2},{9,3},... | collective-permute-start | bytes 2383880 | tf_op jit(solution)/shard_map/ppermute | solution.py:69
  205.2 86.1 %copy-start = (f32[8,256,1024]{2,1,0:T(8,128)}, f32[8,256,1024]{2,1,0:T(8,128)S(1)}, u32[]{:S(2)}) copy-start(f32[8,256,1024]{2,1,0:T(8,128)S(1)} %bitcast_dynamic-update-slice_fusion) | copy-start | bytes 25165828
  205.8 75.0 %collective-permute-start.12 = (bf16[256,1552]{0,1:T(8,128)(2,1)S(1)}, bf16[256,1552]{0,1:T(8,128)(2,1)S(1)}, u32[]{:S(2)}, u32[]{:S(2)}) collective-permute-start(bf16[256,1552]{0,1:T(8,128)(2,1)S(1)} %copy-done.85), channel_id=1, source_target_pairs={{0,11},{1,10},{2,13},{3,12},{4,15},{5,14},{6,1},{7,0},{8,3},{9,2},... | collective-permute-start | bytes 2383880 | tf_op jit(solution)/shard_map/ppermute | solution.py:70
  206.0 75.1 %collective-permute-start.15 = (bf16[256,1552]{0,1:T(8,128)(2,1)S(1)}, bf16[256,1552]{0,1:T(8,128)(2,1)S(1)}, u32[]{:S(2)}, u32[]{:S(2)}) collective-permute-start(bf16[256,1552]{0,1:T(8,128)(2,1)S(1)} %copy-done.82), channel_id=1, source_target_pairs={{0,14},{1,15},{2,0},{3,1},{4,2},{5,3},{6,4},{7,5},{8,6},{9,7},{10,... | collective-permute-start | bytes 2383880 | tf_op jit(solution)/shard_map/ppermute | solution.py:69
  209.5 96.2 %copy-start.10 = (bf16[256,1552]{0,1:T(8,128)(2,1)}, bf16[256,1552]{0,1:T(8,128)(2,1)S(1)}, u32[]{:S(2)}) copy-start(bf16[256,1552]{0,1:T(8,128)(2,1)S(1)} %get-tuple-element.117) | copy-start | bytes 2383876
  209.5 96.2 %copy-start.14 = (bf16[256,1552]{0,1:T(8,128)(2,1)}, bf16[256,1552]{0,1:T(8,128)(2,1)S(1)}, u32[]{:S(2)}) copy-start(bf16[256,1552]{0,1:T(8,128)(2,1)S(1)} %get-tuple-element.118) | copy-start | bytes 2383876
  209.5 24.8 %copy-start.79 = (bf16[256,1552]{0,1:T(8,128)(2,1)S(1)}, bf16[256,1552]{0,1:T(8,128)(2,1)}, u32[]{:S(2)}) copy-start(bf16[256,1552]{0,1:T(8,128)(2,1)} %get-tuple-element.10) | copy-start | bytes 2383876
  209.6 81.6 %collective-permute-start.16 = (bf16[256,1552]{0,1:T(8,128)(2,1)S(1)}, bf16[256,1552]{0,1:T(8,128)(2,1)S(1)}, u32[]{:S(2)}, u32[]{:S(2)}) collective-permute-start(bf16[256,1552]{0,1:T(8,128)(2,1)S(1)} %copy-done.80), channel_id=1, source_target_pairs={{0,15},{1,14},{2,1},{3,0},{4,3},{5,2},{6,5},{7,4},{8,7},{9,6},{10,... | collective-permute-start | bytes 2383880 | tf_op jit(solution)/shard_map/ppermute | solution.py:70
  210.6 95.0 %collective-permute-start.13 = (bf16[256,1552]{0,1:T(8,128)(2,1)S(1)}, bf16[256,1552]{0,1:T(8,128)(2,1)S(1)}, u32[]{:S(2)}, u32[]{:S(2)}) collective-permute-start(bf16[256,1552]{0,1:T(8,128)(2,1)S(1)} %copy-done.81), channel_id=1, source_target_pairs={{0,12},{1,13},{2,14},{3,15},{4,0},{5,1},{6,2},{7,3},{8,4},{9,5},{1... | collective-permute-start | bytes 2383880 | tf_op jit(solution)/shard_map/ppermute | solution.py:69
  216.0 89.8 %copy-start.18 = (bf16[256,1552]{0,1:T(8,128)(2,1)}, bf16[256,1552]{0,1:T(8,128)(2,1)S(1)}, u32[]{:S(2)}) copy-start(bf16[256,1552]{0,1:T(8,128)(2,1)S(1)} %get-tuple-element.115) | copy-start | bytes 2383876
  216.0 89.8 %copy-start.22 = (bf16[256,1552]{0,1:T(8,128)(2,1)}, bf16[256,1552]{0,1:T(8,128)(2,1)S(1)}, u32[]{:S(2)}) copy-start(bf16[256,1552]{0,1:T(8,128)(2,1)S(1)} %get-tuple-element.116) | copy-start | bytes 2383876
  234.4 71.2 %collective-permute-start.14 = (bf16[256,1552]{0,1:T(8,128)(2,1)S(1)}, bf16[256,1552]{0,1:T(8,128)(2,1)S(1)}, u32[]{:S(2)}, u32[]{:S(2)}) collective-permute-start(bf16[256,1552]{0,1:T(8,128)(2,1)S(1)} %copy-done.79), channel_id=1, source_target_pairs={{0,13},{1,12},{2,15},{3,14},{4,1},{5,0},{6,3},{7,2},{8,5},{9,4},{1... | collective-permute-start | bytes 2383880 | tf_op jit(solution)/shard_map/ppermute | solution.py:70
  280.9 24.9 %copy-start.26 = (bf16[256,1552]{0,1:T(8,128)(2,1)}, bf16[256,1552]{0,1:T(8,128)(2,1)S(1)}, u32[]{:S(2)}) copy-start(bf16[256,1552]{0,1:T(8,128)(2,1)S(1)} %get-tuple-element.113) | copy-start | bytes 2383876
  280.9 24.9 %copy-start.30 = (bf16[256,1552]{0,1:T(8,128)(2,1)}, bf16[256,1552]{0,1:T(8,128)(2,1)S(1)}, u32[]{:S(2)}) copy-start(bf16[256,1552]{0,1:T(8,128)(2,1)S(1)} %get-tuple-element.114) | copy-start | bytes 2383876
  291.3 14.5 %copy-start.122 = (f32[16]{0:T(128)S(1)}, f32[16]{0:T(128)}, u32[]{:S(2)}) copy-start(f32[16]{0:T(128)} %copy-done.121) | copy-start | bytes 196
  (123 other events, 491.9 us)
Sparse Core Ops, SparseCore 0:
  389.6 49.4 all-gather.2

commit v9 on v7

--- a/solution.py
+++ b/solution.py
@@ -122,10 +122,10 @@
     )
     carried = jnp.exp(jnp.repeat(before, HEADDIM, axis=1))[:, None, :] * incoming[None]
     full_state = entering + carried
-    grown = jnp.exp(jnp.repeat(cum_acc, HEADDIM, axis=2))
-    y_state = grown * jnp.einsum(
+    y_state = jnp.einsum(
         "bqn,bnc->bqc", c_acc.astype(f32), full_state, precision=lax.Precision.HIGHEST
-    )
+    ).reshape(blocks, SPAN, heads_dev, HEADDIM)
+    y_state = (jnp.exp(cum_acc)[..., None] * y_state).reshape(blocks, SPAN, slab)
     result = y_acc + y_state
     return result.astype(jnp.bfloat16).reshape(blocks * SPAN, slab)
 

time: 578 us -> 578 us (level)
    mul x0 -> x2, local copies, waits for them, and re-layouts: none -> 24.3 us  [on_device(): jnp.exp(cum_acc)[..., None] * y_state]
    exp x2 -> x1, local copies, waits for them, and re-layouts: 17.2 us -> 0.75 us  [on_device(): jnp.exp(cum_acc)[..., None] * y_state]
    broadcast_in_dim x1 -> x0, local copies, waits for them, and re-layouts: 7.92 us -> none  [on_device(): grown = jnp.exp(jnp.repeat(cum_acc, HEADDIM, axis=2))]
where the time goes in v9:
time: 578 us; the launch traced here: 572 us
  other arithmetic  149 us (26%)
  local copies, waits for them, and re-layouts  138 us (24%)
  waiting for transfers between devices  105 us (18%)
  matrix products  87.2 us (15%)
  starting transfers between devices  78.4 us (14%)
  between operations  15.7 us (3%)
    ppermute x8, waiting for transfers between devices, on_device(): r_same = lax.ppermute(p_same, 'head', same)  65.2 us
    ppermute x8, starting transfers between devices, on_device(): r_same = lax.ppermute(p_same, 'head', same)  43.9 us
    dot_general x8, matrix products, on_device(): jnp.einsum('hts,shp->thp', mix, x_heads, preferred_element_type=f32)  41.6 us
    ppermute x8, waiting for transfers between devices, on_device(): r_other = lax.ppermute(p_other, 'head', other)  39.5 us
    convert_element_type x1, other arithmetic, on_device(): act = jax.nn.silu(total + conv_bias).astype(jnp.bfloat16)  36.6 us
    ppermute x8, starting transfers between devices, on_device(): r_other = lax.ppermute(p_other, 'head', other)  30.7 us
    another operation x24, other arithmetic  30 us
    unnamed x247, local copies, waits for them, and re-layouts  26.3 us
  transfers between devices with their start and end apart: 18, of which 4 were waited for; matrix products, arithmetic and copies ran while one was open for 33% of the time, Pallas kernels for 0%

profile of v9, /device:TPU:30, one launch (start us, length us, event | category | flops | bytes accessed | tf_op | source)
XLA Modules:
  0.0 572.5 jit_solution(16078004299729561000)
XLA Ops:
  7.6 3.7 collective-permute-start
  11.7 13.7 %copy.474 = bf16[256,20480]{0,1:T(8,128)(2,1)} copy(bf16[256,20480]{1,0:T(8,128)(2,1)} %param.7) | data formatting | bytes 20971520 | tf_op args[0]
  28.5 3.6 copy.473
  32.2 36.6 %multiply_convert_fusion = bf16[256,20480]{0,1:T(8,128)(2,1)S(1)} fusion(bf16[256,20480]{0,1:T(8,128)(2,1)} %copy.474, bf16[3,20480]{0,1:T(8,128)(2,1)} %copy.473, f32[20480]{0:T(1024)S(1)} %copy-done.89, f32[20480]{0:T(1024)S(1)} %bitcast.411, f32[20480]{0:T(1024)S(1)} %bitcast.410, f32[20480]{0:T(1024)S(1)} %bitcast.409, f32[20480]{0:T(1024)S(1)} %bitcast.408), kind=kLoop, calls=%fused_computation | loop fusion | flops 136314880 | bytes 21504000 | tf_op jit(solution)/shard_map/convert_element_type | solution.py:33
  70.0 4.4 collective-permute-start.7
  87.2 7.1 %collective-permute-done.7 = bf16[256,1552]{0,1:T(8,128)(2,1)S(1)} collective-permute-done((bf16[256,1552]{0,1:T(8,128)(2,1)S(1)}, bf16[256,1552]{0,1:T(8,128)(2,1)S(1)}, u32[]{:S(2)}, u32[]{:S(2)}) %collective-permute-start.7) | collective-permute-done | bytes 794656 | tf_op jit(solution)/shard_map/ppermute | solution.py:69
  96.1 15.3 %collective-permute-done.8 = bf16[256,1552]{0,1:T(8,128)(2,1)S(1)} collective-permute-done((bf16[256,1552]{0,1:T(8,128)(2,1)S(1)}, bf16[256,1552]{0,1:T(8,128)(2,1)S(1)}, u32[]{:S(2)}, u32[]{:S(2)}) %collective-permute-start.8) | collective-permute-done | bytes 794656 | tf_op jit(solution)/shard_map/ppermute | solution.py:70
  126.5 5.0 fusion.8
  131.5 5.0 fusion.5
  140.4 14.3 %collective-permute-start.15 = (bf16[256,1552]{0,1:T(8,128)(2,1)S(1)}, bf16[256,1552]{0,1:T(8,128)(2,1)S(1)}, u32[]{:S(2)}, u32[]{:S(2)}) collective-permute-start(bf16[256,1552]{0,1:T(8,128)(2,1)S(1)} %copy-done.71), channel_id=1, source_target_pairs={{0,14},{1,15},{2,0},{3,1},{4,2},{5,3},{6,4},{7,5},{8,6},{9,7},{10,... | collective-permute-start | bytes 2383880 | tf_op jit(solution)/shard_map/ppermute | solution.py:69
  154.7 4.5 broadcast_in_dim.345
  166.5 14.6 %collective-permute-start.10 = (bf16[256,1552]{0,1:T(8,128)(2,1)S(1)}, bf16[256,1552]{0,1:T(8,128)(2,1)S(1)}, u32[]{:S(2)}, u32[]{:S(2)}) collective-permute-start(bf16[256,1552]{0,1:T(8,128)(2,1)S(1)} %copy-done.68), channel_id=1, source_target_pairs={{0,9},{1,8},{2,11},{3,10},{4,13},{5,12},{6,15},{7,14},{8,1},{9,0},... | collective-permute-start | bytes 2383880 | tf_op jit(solution)/shard_map/ppermute | solution.py:70
  184.0 24.2 %collective-permute-done.16 = bf16[256,1552]{0,1:T(8,128)(2,1)S(1)} collective-permute-done((bf16[256,1552]{0,1:T(8,128)(2,1)S(1)}, bf16[256,1552]{0,1:T(8,128)(2,1)S(1)}, u32[]{:S(2)}, u32[]{:S(2)}) %collective-permute-start.16) | collective-permute-done | bytes 794656 | tf_op jit(solution)/shard_map/ppermute | solution.py:70
  255.1 4.9 fusion.12
  260.2 4.9 fusion.6
  265.2 6.0 %fusion.7 = f32[16,64,512]{2,1,0:T(8,128)} fusion(bf16[512,16,64]{0,2,1:T(8,128)(2,1)S(1)} %bitcast.404, f32[16,512]{1,0:T(8,128)S(1)} %bitcast.415, f32[16,512]{1,0:T(8,128)S(1)} %copy-done.94, f32[512,512]{1,0:T(8,128)S(1)} %copy-done.61, pred[512,512]{1,0:T(8,128)(4,1)S(1)} %copy-done.74), kind=kOutput, calls=%fused_computation.23 | convolution fusion | flops 557842432 | bytes 4521984 | tf_op jit(solution)/shard_map/hts,shp->thp/dot_general | solution.py:85
  271.1 5.7 fusion.9
  276.8 6.8 %fusion.41 = (f32[1,512,1024]{1,2,0:T(8,128)}, f32[512,1024]{0,1:T(8,128)}, f32[512,1024]{0,1:T(8,128)}, f32[1,512,1024]{1,2,0:T(8,128)}) fusion(bf16[512,1024]{0,1:T(8,128)(2,1)S(1)} %copy-done.46, f32[16,64,512]{2,1,0:T(8,128)S(1)} %fusion.12, f32[1024]{0:T(1024)S(1)} %mul.786, bf16[512,1024]{0,1:T(8,128)(2,1)S(1)} %copy-done.47, ...), kind=kLoop, calls=%fused_computation.73 | loop fusion | flops 6291456 | bytes 20975616 | tf_op jit(solution)/shard_map/jit(dynamic_update_index_in_dim)/broadcast_in_dim | solution.py:92
  283.6 23.6 %collective-permute-start.13 = (bf16[256,1552]{0,1:T(8,128)(2,1)}, bf16[256,1552]{0,1:T(8,128)(2,1)S(1)}, u32[]{:S(2)}, u32[]{:S(2)}) collective-permute-start(bf16[256,1552]{0,1:T(8,128)(2,1)} %get-tuple-element.17), channel_id=1, source_target_pairs={{0,12},{1,13},{2,14},{3,15},{4,0},{5,1},{6,2},{7,3},{8,4},{9,5},{1... | collective-permute-start | bytes 2383880 | tf_op jit(solution)/shard_map/ppermute | solution.py:69
  307.2 7.7 %collective-permute-start.12 = (bf16[256,1552]{0,1:T(8,128)(2,1)}, bf16[256,1552]{0,1:T(8,128)(2,1)S(1)}, u32[]{:S(2)}, u32[]{:S(2)}) collective-permute-start(bf16[256,1552]{0,1:T(8,128)(2,1)} %get-tuple-element.16), channel_id=1, source_target_pairs={{0,11},{1,10},{2,13},{3,12},{4,15},{5,14},{6,1},{7,0},{8,3},{9,2},... | collective-permute-start | bytes 2383880 | tf_op jit(solution)/shard_map/ppermute | solution.py:70
  317.7 58.0 %collective-permute-done.13 = bf16[256,1552]{0,1:T(8,128)(2,1)S(1)} collective-permute-done((bf16[256,1552]{0,1:T(8,128)(2,1)}, bf16[256,1552]{0,1:T(8,128)(2,1)S(1)}, u32[]{:S(2)}, u32[]{:S(2)}) %collective-permute-start.13) | collective-permute-done | bytes 794656 | tf_op jit(solution)/shard_map/ppermute | solution.py:69
  402.7 4.4 fusion.60
  427.8 8.1 %broadcast_in_dim.313 = f32[8,512,1024]{2,1,0:T(8,128)} broadcast(f32[]{:T(128)} %constant.425.clone.1), dimensions={} | broadcast | bytes 16777220 | tf_op jit(solution)/shard_map/broadcast_in_dim | solution.py:56
  445.1 3.2 copy.515
  451.8 3.4 constant_dynamic-update-slice_fusion.14
  464.8 5.0 fusion.11
  469.9 5.0 fusion.10
  480.4 3.2 copy.510
  483.6 7.9 %mul.910 = f32[8,512,16,64]{1,3,2,0:T(8,128)} broadcast(f32[8,512,16]{1,2,0:T(8,128)S(1)} %copy-done.56), dimensions={0,1,2} | broadcast | bytes 17039360 | tf_op jit(solution)/shard_map/mul | solution.py:128
  491.5 16.4 %copy.524 = f32[8,512,1024]{2,1,0:T(8,128)} copy(f32[8,512,1024]{1,2,0:T(8,128)} %bitcast.392) | data formatting | bytes 33554432 | tf_op jit(solution)/shard_map/mul | solution.py:128
  537.1 4.6 fusion.2
  541.7 23.7 %add_convert_fusion = bf16[8,512,1024]{2,1,0:T(8,128)(2,1)} fusion(f32[8,512,1024]{2,1,0:T(8,128)} %constant_dynamic-update-slice_fusion.8, f32[8,512,1024]{2,1,0:T(8,128)} %copy.524, bf16[8,512,256]{2,1,0:T(8,128)(2,1)} %constant_dynamic-update-slice_fusion, f32[8,256,1024]{2,1,0:T(8,128)} %add_dynamic-update-slice_fusion, f32[256,1024]{1,0:T(8,128)S(1)} %fusion.2, ...), kind=kOutput, calls=%fused_computation.3 | convolution fusion | flops 12901679104 | bytes 53510144 | tf_op jit(solution)/shard_map/bqn,bnc->bqc/dot_general | solution.py:125
  (483 shorter events, 202.2 us)
Async XLA Ops:
  6.5 528.3 %all-gather.3.cloned.1.call-start = ((), (), s32[]{:S(2)}) async-start(), calls=%async_computation | async-start | bytes 9732096 | tf_op jit(solution)/shard_map/all_gather | solution.py:109
  7.6 20.9 %collective-permute-start = (bf16[3,20480]{1,0:T(4,128)(2,1)S(1)}, bf16[3,20480]{1,0:T(4,128)(2,1)S(1)}, u32[]{:S(2)}, u32[]{:S(2)}) collective-permute-start(bf16[3,20480]{1,0:T(4,128)(2,1)S(1)} %slice.268), channel_id=1, source_target_pairs={{0,1},{1,2},{2,3},{3,4},{4,5},{5,6},{6,7},{7,8},{8,9},{9,10},{10,1... | collective-permute-start | bytes 368648 | tf_op jit(solution)/shard_map/ppermute | solution.py:25
  11.6 13.8 %copy-start.112 = (f32[256]{0:T(256)S(1)}, f32[256]{0:T(256)}, u32[]{:S(2)}) copy-start(f32[256]{0:T(256)} %param.12) | copy-start | bytes 3076
  11.6 13.9 %copy-start.41 = (bf16[256,256]{1,0:T(8,128)(2,1)S(1)}, bf16[256,256]{1,0:T(8,128)(2,1)}, u32[]{:S(2)}) copy-start(bf16[256,256]{1,0:T(8,128)(2,1)} %param.8) | copy-start | bytes 393220
  25.4 91.3 %copy-start.98 = (f32[16]{0:T(128)}, f32[16]{0:T(128)S(1)}, u32[]{:S(2)}) copy-start(f32[16]{0:T(128)S(1)} %exponential_negate_fusion) | copy-start | bytes 196
  25.5 91.2 %copy-start.101 = (f32[16]{0:T(128)}, f32[16]{0:T(128)S(1)}, u32[]{:S(2)}) copy-start(f32[16]{0:T(128)S(1)} %dynamic_slice.210) | copy-start | bytes 196
  28.5 103.0 %copy-start.73 = (pred[512,512]{1,0:T(8,128)(4,1)}, pred[512,512]{1,0:T(8,128)(4,1)S(1)}, u32[]{:S(2)}) copy-start(pred[512,512]{1,0:T(8,128)(4,1)S(1)} %iota_compare_fusion) | copy-start | bytes 786436
  70.0 24.3 %collective-permute-start.7 = (bf16[256,1552]{0,1:T(8,128)(2,1)S(1)}, bf16[256,1552]{0,1:T(8,128)(2,1)S(1)}, u32[]{:S(2)}, u32[]{:S(2)}) collective-permute-start(bf16[256,1552]{0,1:T(8,128)(2,1)S(1)} %pad_maximum_fusion.8), channel_id=1, source_target_pairs={{0,6},{1,7},{2,8},{3,9},{4,10},{5,11},{6,12},{7,13},{8,14},{9,15},... | collective-permute-start | bytes 2383880 | tf_op jit(solution)/shard_map/ppermute | solution.py:69
  74.8 36.6 %collective-permute-start.8 = (bf16[256,1552]{0,1:T(8,128)(2,1)S(1)}, bf16[256,1552]{0,1:T(8,128)(2,1)S(1)}, u32[]{:S(2)}, u32[]{:S(2)}) collective-permute-start(bf16[256,1552]{0,1:T(8,128)(2,1)S(1)} %pad_maximum_fusion.9), channel_id=1, source_target_pairs={{0,7},{1,6},{2,9},{3,8},{4,11},{5,10},{6,13},{7,12},{8,15},{9,14},... | collective-permute-start | bytes 2383880 | tf_op jit(solution)/shard_map/ppermute | solution.py:70
  77.7 35.8 %collective-permute-start.1 = (bf16[256,1552]{0,1:T(8,128)(2,1)S(1)}, bf16[256,1552]{0,1:T(8,128)(2,1)S(1)}, u32[]{:S(2)}, u32[]{:S(2)}) collective-permute-start(bf16[256,1552]{0,1:T(8,128)(2,1)S(1)} %pad_maximum_fusion.2), channel_id=1, source_target_pairs={{0,0},{1,1},{2,2},{3,3},{4,4},{5,5},{6,6},{7,7},{8,8},{9,9},{10,10... | collective-permute-start | bytes 2383880 | tf_op jit(solution)/shard_map/ppermute | solution.py:69
  77.9 37.4 %collective-permute-start.2 = (bf16[256,1552]{0,1:T(8,128)(2,1)S(1)}, bf16[256,1552]{0,1:T(8,128)(2,1)S(1)}, u32[]{:S(2)}, u32[]{:S(2)}) collective-permute-start(bf16[256,1552]{0,1:T(8,128)(2,1)S(1)} %pad_maximum_fusion.3), channel_id=1, source_target_pairs={{0,1},{1,0},{2,3},{3,2},{4,5},{5,4},{6,7},{7,6},{8,9},{9,8},{10,11... | collective-permute-start | bytes 2383880 | tf_op jit(solution)/shard_map/ppermute | solution.py:70
  78.9 81.8 %collective-permute-start.3 = (bf16[256,1552]{0,1:T(8,128)(2,1)}, bf16[256,1552]{0,1:T(8,128)(2,1)}, u32[]{:S(2)}, u32[]{:S(2)}) collective-permute-start(bf16[256,1552]{0,1:T(8,128)(2,1)} %pad_maximum_fusion.4), channel_id=1, source_target_pairs={{0,2},{1,3},{2,4},{3,5},{4,6},{5,7},{6,8},{7,9},{8,10},{9,11},{10,... | collective-permute-start | bytes 2383880 | tf_op jit(solution)/shard_map/ppermute | solution.py:69
  94.3 68.3 %collective-permute-start.4 = (bf16[256,1552]{0,1:T(8,128)(2,1)}, bf16[256,1552]{0,1:T(8,128)(2,1)}, u32[]{:S(2)}, u32[]{:S(2)}) collective-permute-start(bf16[256,1552]{0,1:T(8,128)(2,1)} %pad_maximum_fusion.5), channel_id=1, source_target_pairs={{0,3},{1,2},{2,5},{3,4},{4,7},{5,6},{6,9},{7,8},{8,11},{9,10},{10,... | collective-permute-start | bytes 2383880 | tf_op jit(solution)/shard_map/ppermute | solution.py:70
  111.4 54.7 %collective-permute-start.5 = (bf16[256,1552]{0,1:T(8,128)(2,1)}, bf16[256,1552]{0,1:T(8,128)(2,1)}, u32[]{:S(2)}, u32[]{:S(2)}) collective-permute-start(bf16[256,1552]{0,1:T(8,128)(2,1)} %pad_maximum_fusion.6), channel_id=1, source_target_pairs={{0,4},{1,5},{2,6},{3,7},{4,8},{5,9},{6,10},{7,11},{8,12},{9,13},{1... | collective-permute-start | bytes 2383880 | tf_op jit(solution)/shard_map/ppermute | solution.py:69
  113.5 67.5 %collective-permute-start.6 = (bf16[256,1552]{0,1:T(8,128)(2,1)}, bf16[256,1552]{0,1:T(8,128)(2,1)}, u32[]{:S(2)}, u32[]{:S(2)}) collective-permute-start(bf16[256,1552]{0,1:T(8,128)(2,1)} %pad_maximum_fusion.7), channel_id=1, source_target_pairs={{0,5},{1,4},{2,7},{3,6},{4,9},{5,8},{6,11},{7,10},{8,13},{9,12},{1... | collective-permute-start | bytes 2383880 | tf_op jit(solution)/shard_map/ppermute | solution.py:70
  140.4 43.6 %collective-permute-start.15 = (bf16[256,1552]{0,1:T(8,128)(2,1)S(1)}, bf16[256,1552]{0,1:T(8,128)(2,1)S(1)}, u32[]{:S(2)}, u32[]{:S(2)}) collective-permute-start(bf16[256,1552]{0,1:T(8,128)(2,1)S(1)} %copy-done.71), channel_id=1, source_target_pairs={{0,14},{1,15},{2,0},{3,1},{4,2},{5,3},{6,4},{7,5},{8,6},{9,7},{10,... | collective-permute-start | bytes 2383880 | tf_op jit(solution)/shard_map/ppermute | solution.py:69
  160.7 47.5 %collective-permute-start.16 = (bf16[256,1552]{0,1:T(8,128)(2,1)S(1)}, bf16[256,1552]{0,1:T(8,128)(2,1)S(1)}, u32[]{:S(2)}, u32[]{:S(2)}) collective-permute-start(bf16[256,1552]{0,1:T(8,128)(2,1)S(1)} %copy-done.70), channel_id=1, source_target_pairs={{0,15},{1,14},{2,1},{3,0},{4,3},{5,2},{6,5},{7,4},{8,7},{9,6},{10,... | collective-permute-start | bytes 2383880 | tf_op jit(solution)/shard_map/ppermute | solution.py:70
  162.7 47.2 %collective-permute-start.9 = (bf16[256,1552]{0,1:T(8,128)(2,1)S(1)}, bf16[256,1552]{0,1:T(8,128)(2,1)S(1)}, u32[]{:S(2)}, u32[]{:S(2)}) collective-permute-start(bf16[256,1552]{0,1:T(8,128)(2,1)S(1)} %copy-done.69), channel_id=1, source_target_pairs={{0,8},{1,9},{2,10},{3,11},{4,12},{5,13},{6,14},{7,15},{8,0},{9,1},... | collective-permute-start | bytes 2383880 | tf_op jit(solution)/shard_map/ppermute | solution.py:69
  164.7 45.3 %copy-start.18 = (bf16[256,1552]{0,1:T(8,128)(2,1)}, bf16[256,1552]{0,1:T(8,128)(2,1)S(1)}, u32[]{:S(2)}) copy-start(bf16[256,1552]{0,1:T(8,128)(2,1)S(1)} %get-tuple-element.129) | copy-start | bytes 2383876
  164.7 45.3 %copy-start.20 = (bf16[256,1552]{0,1:T(8,128)(2,1)}, bf16[256,1552]{0,1:T(8,128)(2,1)S(1)}, u32[]{:S(2)}) copy-start(bf16[256,1552]{0,1:T(8,128)(2,1)S(1)} %get-tuple-element.130) | copy-start | bytes 2383876
  166.5 43.4 %collective-permute-start.10 = (bf16[256,1552]{0,1:T(8,128)(2,1)S(1)}, bf16[256,1552]{0,1:T(8,128)(2,1)S(1)}, u32[]{:S(2)}, u32[]{:S(2)}) collective-permute-start(bf16[256,1552]{0,1:T(8,128)(2,1)S(1)} %copy-done.68), channel_id=1, source_target_pairs={{0,9},{1,8},{2,11},{3,10},{4,13},{5,12},{6,15},{7,14},{8,1},{9,0},... | collective-permute-start | bytes 2383880 | tf_op jit(solution)/shard_map/ppermute | solution.py:70
  182.5 27.5 %copy-start.28 = (bf16[256,1552]{0,1:T(8,128)(2,1)}, bf16[256,1552]{0,1:T(8,128)(2,1)S(1)}, u32[]{:S(2)}) copy-start(bf16[256,1552]{0,1:T(8,128)(2,1)S(1)} %get-tuple-element.127) | copy-start | bytes 2383876
  182.5 27.5 %copy-start.31 = (bf16[256,1552]{0,1:T(8,128)(2,1)}, bf16[256,1552]{0,1:T(8,128)(2,1)S(1)}, u32[]{:S(2)}) copy-start(bf16[256,1552]{0,1:T(8,128)(2,1)S(1)} %get-tuple-element.128) | copy-start | bytes 2383876
  276.8 38.1 %copy-start.51 = (f32[256,1024]{1,0:T(8,128)S(1)}, f32[256,1024]{1,0:T(8,128)}, u32[]{:S(2)}) copy-start(f32[256,1024]{1,0:T(8,128)} %fusion.126) | copy-start | bytes 3145732
  283.6 32.4 %copy-start.66 = (f32[16,4,128]{2,0,1:T(8,128)S(1)}, f32[16,4,128]{2,0,1:T(8,128)}, u32[]{:S(2)}) copy-start(f32[16,4,128]{2,0,1:T(8,128)} %reduce-window.60) | copy-start | bytes 98308
  283.6 32.4 %copy-start.97 = (f32[16,4]{0,1:T(4,128)S(1)}, f32[16,4]{0,1:T(4,128)}, u32[]{:S(2)}) copy-start(f32[16,4]{0,1:T(4,128)} %copy-done.96) | copy-start | bytes 772
  283.6 32.5 %copy-start.23 = (bf16[256,1552]{0,1:T(8,128)(2,1)S(1)}, bf16[256,1552]{0,1:T(8,128)(2,1)}, u32[]{:S(2)}) copy-start(bf16[256,1552]{0,1:T(8,128)(2,1)} %copy-done.22) | copy-start | bytes 2383876
  283.6 32.5 %copy-start.26 = (bf16[256,1552]{0,1:T(8,128)(2,1)S(1)}, bf16[256,1552]{0,1:T(8,128)(2,1)}, u32[]{:S(2)}) copy-start(bf16[256,1552]{0,1:T(8,128)(2,1)} %copy-done.25) | copy-start | bytes 2383876
  283.6 92.1 %collective-permute-start.13 = (bf16[256,1552]{0,1:T(8,128)(2,1)}, bf16[256,1552]{0,1:T(8,128)(2,1)S(1)}, u32[]{:S(2)}, u32[]{:S(2)}) collective-permute-start(bf16[256,1552]{0,1:T(8,128)(2,1)} %get-tuple-element.17), channel_id=1, source_target_pairs={{0,12},{1,13},{2,14},{3,15},{4,0},{5,1},{6,2},{7,3},{8,4},{9,5},{1... | collective-permute-start | bytes 2383880 | tf_op jit(solution)/shard_map/ppermute | solution.py:69
  307.2 68.6 %collective-permute-start.14 = (bf16[256,1552]{0,1:T(8,128)(2,1)}, bf16[256,1552]{0,1:T(8,128)(2,1)S(1)}, u32[]{:S(2)}, u32[]{:S(2)}) collective-permute-start(bf16[256,1552]{0,1:T(8,128)(2,1)} %get-tuple-element.18), channel_id=1, source_target_pairs={{0,13},{1,12},{2,15},{3,14},{4,1},{5,0},{6,3},{7,2},{8,5},{9,4},{1... | collective-permute-start | bytes 2383880 | tf_op jit(solution)/shard_map/ppermute | solution.py:70
  307.2 68.7 %collective-permute-start.11 = (bf16[256,1552]{0,1:T(8,128)(2,1)}, bf16[256,1552]{0,1:T(8,128)(2,1)S(1)}, u32[]{:S(2)}, u32[]{:S(2)}) collective-permute-start(bf16[256,1552]{0,1:T(8,128)(2,1)} %get-tuple-element.15), channel_id=1, source_target_pairs={{0,10},{1,11},{2,12},{3,13},{4,14},{5,15},{6,0},{7,1},{8,2},{9,3},... | collective-permute-start | bytes 2383880 | tf_op jit(solution)/shard_map/ppermute | solution.py:69
  307.2 68.7 %collective-permute-start.12 = (bf16[256,1552]{0,1:T(8,128)(2,1)}, bf16[256,1552]{0,1:T(8,128)(2,1)S(1)}, u32[]{:S(2)}, u32[]{:S(2)}) collective-permute-start(bf16[256,1552]{0,1:T(8,128)(2,1)} %get-tuple-element.16), channel_id=1, source_target_pairs={{0,11},{1,10},{2,13},{3,12},{4,15},{5,14},{6,1},{7,0},{8,3},{9,2},... | collective-permute-start | bytes 2383880 | tf_op jit(solution)/shard_map/ppermute | solution.py:70
  (100 other events, 303.4 us)
Sparse Core Ops, SparseCore 0:
  408.4 50.3 all-gather.2

commit v10 on v6

--- a/solution.py
+++ b/solution.py
@@ -72,8 +72,8 @@
         t_same = 2 * ((head_pos // 2 + m) % pairs) + parity
         t_other = 2 * ((head_pos // 2 + m) % pairs) + 1 - parity
         p_same, p_other = payload(t_same), payload(t_other)
-        if m >= 2:
-            p_same, p_other, _ = lax.optimization_barrier((p_same, p_other, done[m - 2]))
+        if m >= 4:
+            p_same, p_other, _ = lax.optimization_barrier((p_same, p_other, done[m - 4]))
         r_same = lax.ppermute(p_same, "head", same)
         r_other = lax.ppermute(p_other, "head", other)
         first = jnp.where(parity == 0, r_same, r_other)

time: 595 us -> 570 us (0.958)
  waiting for transfers between devices: 158 us -> 101 us
  local copies, waits for them, and re-layouts: 144 us -> 160 us
  starting transfers between devices: 36.4 us -> 50.1 us
    ppermute x8, waiting for transfers between devices: 108 us -> 71.2 us  [on_device(): r_same = lax.ppermute(p_same, 'head', same)]
    ppermute x8, waiting for transfers between devices: 49.9 us -> 29.5 us  [on_device(): r_other = lax.ppermute(p_other, 'head', other)]
    ppermute x8, starting transfers between devices: 13.5 us -> 21.4 us  [on_device(): r_other = lax.ppermute(p_other, 'head', other)]
    broadcast_in_dim x8, local copies, waits for them, and re-layouts: 1.86 us -> 9.09 us  [on_device(): fade = jnp.exp(jnp.repeat(block_totals[k], HEADDIM))]
    exp x7, local copies, waits for them, and re-layouts: 1.1 us -> 8.32 us  [on_device(): fade = jnp.exp(jnp.repeat(block_totals[k], HEADDIM))]
    unnamed x283 -> x235, local copies, waits for them, and re-layouts: 34.7 us -> 31.2 us
    unnamed x13 -> x10, other arithmetic: 18.2 us -> 17.9 us
  transfers between devices with their start and end apart: 18 -> 18, of which waited for: 9 -> 4; matrix products, arithmetic and copies ran while one was open for 39% -> 39% of each run, Pallas kernels for 0% -> 0%
where the time goes in v10:
time: 570 us; the launch traced here: 563 us
  local copies, waits for them, and re-layouts  160 us (28%)
  other arithmetic  148 us (26%)
  waiting for transfers between devices  101 us (18%)
  matrix products  87.5 us (15%)
  starting transfers between devices  50.1 us (9%)
  between operations  17 us (3%)
    ppermute x8, waiting for transfers between devices, on_device(): r_same = lax.ppermute(p_same, 'head', same)  71.2 us
    dot_general x8, matrix products, on_device(): jnp.einsum('hts,shp->thp', mix, x_heads, preferred_element_type=f32)  43.1 us
    convert_element_type x16, other arithmetic, payload(): act = jax.nn.silu(total + pick(conv_bias)).astype(jnp.bfloat16)  35.6 us
    unnamed x235, local copies, waits for them, and re-layouts  31.2 us
    ppermute x8, waiting for transfers between devices, on_device(): r_other = lax.ppermute(p_other, 'head', other)  29.5 us
    ppermute x8, starting transfers between devices, on_device(): r_same = lax.ppermute(p_same, 'head', same)  24.9 us
    another operation x24, other arithmetic  24.6 us
    dot_general x1, matrix products, on_device(): jnp.einsum('bqn,bnc->bqc', c_acc.astype(f32), full_state, precision=lax.P...  23.7 us
  transfers between devices with their start and end apart: 18, of which 4 were waited for; matrix products, arithmetic and copies ran while one was open for 39% of the time, Pallas kernels for 0%

profile of v10, /device:TPU:30, one launch (start us, length us, event | category | flops | bytes accessed | tf_op | source)
XLA Modules:
  0.0 563.0 jit_solution(6233954487041454951)
XLA Ops:
  7.6 3.7 collective-permute-start
  15.7 13.9 %copy.471 = bf16[256,20480]{0,1:T(8,128)(2,1)} copy(bf16[256,20480]{1,0:T(8,128)(2,1)} %param.7) | data formatting | bytes 20971520 | tf_op args[0]
  31.9 3.6 copy.470
  58.5 3.8 collective-permute-start.8
  112.9 4.3 collective-permute-start.4
  127.7 4.5 broadcast_in_dim.363
  133.6 5.0 fusion.6
  138.7 5.0 fusion.3
  150.8 4.1 collective-permute-start.16
  161.3 13.7 %collective-permute-done.15 = bf16[256,1552]{0,1:T(8,128)(2,1)S(1)} collective-permute-done((bf16[256,1552]{0,1:T(8,128)(2,1)S(1)}, bf16[256,1552]{0,1:T(8,128)(2,1)S(1)}, u32[]{:S(2)}, u32[]{:S(2)}) %collective-permute-start.15) | collective-permute-done | bytes 794656 | tf_op jit(solution)/shard_map/ppermute | solution.py:77
  175.0 27.9 %collective-permute-done.16 = bf16[256,1552]{0,1:T(8,128)(2,1)S(1)} collective-permute-done((bf16[256,1552]{0,1:T(8,128)(2,1)S(1)}, bf16[256,1552]{0,1:T(8,128)(2,1)S(1)}, u32[]{:S(2)}, u32[]{:S(2)}) %collective-permute-start.16) | collective-permute-done | bytes 794656 | tf_op jit(solution)/shard_map/ppermute | solution.py:78
  237.1 5.7 %fusion.10 = f32[16,64,512]{2,1,0:T(8,128)} fusion(bf16[512,16,64]{0,2,1:T(8,128)(2,1)S(1)} %bitcast.402, f32[16,512]{1,0:T(8,128)S(1)} %bitcast.413, f32[16,512]{1,0:T(8,128)S(1)} %get-tuple-element.309, f32[512,512]{1,0:T(8,128)S(1)} %copy-done.55, pred[512,512]{1,0:T(8,128)(4,1)S(1)} %copy-done.71), kind=kOutput, calls=%fused_computation.116 | convolution fusion | flops 557842432 | bytes 4521984 | tf_op jit(solution)/shard_map/hts,shp->thp/dot_general | solution.py:93
  242.8 5.7 %fusion.4 = f32[16,64,512]{2,1,0:T(8,128)} fusion(bf16[512,16,64]{0,2,1:T(8,128)(2,1)S(1)} %bitcast.403, f32[16,512]{1,0:T(8,128)S(1)} %bitcast.412, f32[16,512]{1,0:T(8,128)S(1)} %get-tuple-element.321, f32[512,512]{1,0:T(8,128)S(1)} %copy-done.53, pred[512,512]{1,0:T(8,128)(4,1)S(1)} %copy-done.71), kind=kOutput, calls=%fused_computation.110 | convolution fusion | flops 557842432 | bytes 4521984 | tf_op jit(solution)/shard_map/hts,shp->thp/dot_general | solution.py:93
  248.5 5.8 %fusion.5 = f32[16,64,512]{2,1,0:T(8,128)} fusion(bf16[512,16,64]{0,2,1:T(8,128)(2,1)S(1)} %bitcast.404, f32[16,512]{1,0:T(8,128)S(1)} %bitcast.411, f32[16,512]{1,0:T(8,128)S(1)} %get-tuple-element.319, f32[512,512]{1,0:T(8,128)S(1)} %copy-done.54, pred[512,512]{1,0:T(8,128)(4,1)S(1)} %copy-done.71), kind=kOutput, calls=%fused_computation.111 | convolution fusion | flops 557842432 | bytes 4521984 | tf_op jit(solution)/shard_map/hts,shp->thp/dot_general | solution.py:93
  254.3 5.9 %fusion.7 = f32[16,64,512]{2,1,0:T(8,128)} fusion(bf16[512,16,64]{0,2,1:T(8,128)(2,1)S(1)} %bitcast.405, f32[16,512]{1,0:T(8,128)S(1)} %bitcast.410, f32[16,512]{1,0:T(8,128)S(1)} %get-tuple-element.315, f32[512,512]{1,0:T(8,128)S(1)} %copy-done.56, pred[512,512]{1,0:T(8,128)(4,1)S(1)} %copy-done.71), kind=kOutput, calls=%fused_computation.113 | convolution fusion | flops 557842432 | bytes 4521984 | tf_op jit(solution)/shard_map/hts,shp->thp/dot_general | solution.py:93
  260.2 7.6 %fusion.39 = (f32[1,512,1024]{1,2,0:T(8,128)}, f32[512,1024]{0,1:T(8,128)}, f32[512,1024]{0,1:T(8,128)}, f32[1,512,1024]{1,2,0:T(8,128)}) fusion(bf16[512,1024]{0,1:T(8,128)(2,1)S(1)} %get-tuple-element.102, f32[16,64,512]{2,1,0:T(8,128)} %fusion.10, f32[1024]{0:T(1024)S(1)} %mul.1532, bf16[512,1024]{0,1:T(8,128)(2,1)S(1)} %get-tuple-element.120, ...), kind=kLoop, calls=%fused_computation.161 | loop fusion | flops 6291456 | bytes 20975616 | tf_op jit(solution)/shard_map/jit(dynamic_update_index_in_dim)/broadcast_in_dim | solution.py:100
  269.4 17.1 %collective-permute-start.13 = (bf16[256,1552]{0,1:T(8,128)(2,1)S(1)}, bf16[256,1552]{0,1:T(8,128)(2,1)S(1)}, u32[]{:S(2)}, u32[]{:S(2)}) collective-permute-start(bf16[256,1552]{0,1:T(8,128)(2,1)S(1)} %copy-done.63), channel_id=1, source_target_pairs={{0,12},{1,13},{2,14},{3,15},{4,0},{5,1},{6,2},{7,3},{8,4},{9,5},{1... | collective-permute-start | bytes 2383880 | tf_op jit(solution)/shard_map/ppermute | solution.py:77
  286.5 7.6 %collective-permute-start.12 = (bf16[256,1552]{0,1:T(8,128)(2,1)}, bf16[256,1552]{0,1:T(8,128)(2,1)S(1)}, u32[]{:S(2)}, u32[]{:S(2)}) collective-permute-start(bf16[256,1552]{0,1:T(8,128)(2,1)} %pad_maximum_fusion.28), channel_id=1, source_target_pairs={{0,11},{1,10},{2,13},{3,12},{4,15},{5,14},{6,1},{7,0},{8,3},{9,2},... | collective-permute-start | bytes 2383880 | tf_op jit(solution)/shard_map/ppermute | solution.py:78
  296.8 57.5 %collective-permute-done.13 = bf16[256,1552]{0,1:T(8,128)(2,1)S(1)} collective-permute-done((bf16[256,1552]{0,1:T(8,128)(2,1)S(1)}, bf16[256,1552]{0,1:T(8,128)(2,1)S(1)}, u32[]{:S(2)}, u32[]{:S(2)}) %collective-permute-start.13) | collective-permute-done | bytes 794656 | tf_op jit(solution)/shard_map/ppermute | solution.py:77
  398.6 4.4 fusion.58
  411.1 3.1 copy.476
  420.4 8.1 %broadcast_in_dim.330 = f32[8,512,1024]{2,1,0:T(8,128)} broadcast(f32[]{:T(128)} %constant.440.clone.1), dimensions={} | broadcast | bytes 16777220 | tf_op jit(solution)/shard_map/broadcast_in_dim | solution.py:64
  432.9 3.1 copy.511
  439.8 3.1 copy.481
  443.6 3.3 constant_dynamic-update-slice_fusion.22
  457.4 5.0 fusion.9
  462.5 5.0 fusion.8
  469.3 2.9 copy.506
  474.3 7.9 %broadcast_in_dim.351 = f32[8,512,16,64]{1,3,2,0:T(8,128)} broadcast(f32[8,512,16]{1,2,0:T(8,128)S(1)} %copy-done.48), dimensions={0,1,2} | broadcast | bytes 17039360 | tf_op jit(solution)/shard_map/broadcast_in_dim | solution.py:133
  482.2 16.6 %copy.520 = f32[8,512,1024]{2,1,0:T(8,128)} copy(f32[8,512,1024]{1,2,0:T(8,128)} %bitcast.392) | data formatting | bytes 33554432 | tf_op jit(solution)/shard_map/exp | solution.py:133
  527.4 4.6 fusion
  532.0 23.7 %add_convert_fusion = bf16[8,512,1024]{2,1,0:T(8,128)(2,1)} fusion(f32[8,512,1024]{2,1,0:T(8,128)} %constant_dynamic-update-slice_fusion.16, f32[8,512,1024]{2,1,0:T(8,128)} %copy.520, bf16[8,512,256]{2,1,0:T(8,128)(2,1)} %constant_dynamic-update-slice_fusion, f32[8,256,1024]{2,1,0:T(8,128)} %add_dynamic-update-slice_fusion, f32[256,1024]{1,0:T(8,128)S(1)} %fusion, ...), kind=kOutput, calls=%fused_computation.96 | convolution fusion | flops 12901679104 | bytes 53510144 | tf_op jit(solution)/shard_map/bqn,bnc->bqc/dot_general | solution.py:134
  (544 shorter events, 252.8 us)
Async XLA Ops:
  6.5 518.6 %all-gather.3.cloned.1.call-start = ((), (), s32[]{:S(2)}) async-start(), calls=%async_computation | async-start | bytes 9732096 | tf_op jit(solution)/shard_map/all_gather | solution.py:117
  7.6 24.3 %collective-permute-start = (bf16[3,20480]{1,0:T(4,128)(2,1)S(1)}, bf16[3,20480]{1,0:T(4,128)(2,1)S(1)}, u32[]{:S(2)}, u32[]{:S(2)}) collective-permute-start(bf16[3,20480]{1,0:T(4,128)(2,1)S(1)} %slice.631), channel_id=1, source_target_pairs={{0,1},{1,2},{2,3},{3,4},{4,5},{5,6},{6,7},{7,8},{8,9},{9,10},{10,1... | collective-permute-start | bytes 368648 | tf_op jit(solution)/shard_map/ppermute | solution.py:25
  15.0 103.7 %copy-start.96 = (f32[16]{0:T(128)}, f32[16]{0:T(128)S(1)}, u32[]{:S(2)}) copy-start(f32[16]{0:T(128)S(1)} %exponential_negate_fusion) | copy-start | bytes 196
  31.9 106.8 %copy-start.70 = (pred[512,512]{1,0:T(8,128)(4,1)}, pred[512,512]{1,0:T(8,128)(4,1)S(1)}, u32[]{:S(2)}) copy-start(pred[512,512]{1,0:T(8,128)(4,1)S(1)} %iota_compare_fusion) | copy-start | bytes 786436
  53.5 96.8 %collective-permute-start.3 = (bf16[256,1552]{0,1:T(8,128)(2,1)}, bf16[256,1552]{0,1:T(8,128)(2,1)}, u32[]{:S(2)}, u32[]{:S(2)}) collective-permute-start(bf16[256,1552]{0,1:T(8,128)(2,1)} %pad_maximum_fusion.19), channel_id=1, source_target_pairs={{0,2},{1,3},{2,4},{3,5},{4,6},{5,7},{6,8},{7,9},{8,10},{9,11},{10,... | collective-permute-start | bytes 2383880 | tf_op jit(solution)/shard_map/ppermute | solution.py:77
  58.5 51.3 %collective-permute-start.8 = (bf16[256,1552]{0,1:T(8,128)(2,1)S(1)}, bf16[256,1552]{0,1:T(8,128)(2,1)S(1)}, u32[]{:S(2)}, u32[]{:S(2)}) collective-permute-start(bf16[256,1552]{0,1:T(8,128)(2,1)S(1)} %pad_maximum_fusion.24), channel_id=1, source_target_pairs={{0,7},{1,6},{2,9},{3,8},{4,11},{5,10},{6,13},{7,12},{8,15},{9,14},... | collective-permute-start | bytes 2383880 | tf_op jit(solution)/shard_map/ppermute | solution.py:78
  65.3 44.5 %collective-permute-start.7 = (bf16[256,1552]{0,1:T(8,128)(2,1)S(1)}, bf16[256,1552]{0,1:T(8,128)(2,1)S(1)}, u32[]{:S(2)}, u32[]{:S(2)}) collective-permute-start(bf16[256,1552]{0,1:T(8,128)(2,1)S(1)} %pad_maximum_fusion.23), channel_id=1, source_target_pairs={{0,6},{1,7},{2,8},{3,9},{4,10},{5,11},{6,12},{7,13},{8,14},{9,15},... | collective-permute-start | bytes 2383880 | tf_op jit(solution)/shard_map/ppermute | solution.py:77
  68.3 44.6 %collective-permute-start.2 = (bf16[256,1552]{0,1:T(8,128)(2,1)S(1)}, bf16[256,1552]{0,1:T(8,128)(2,1)S(1)}, u32[]{:S(2)}, u32[]{:S(2)}) collective-permute-start(bf16[256,1552]{0,1:T(8,128)(2,1)S(1)} %pad_maximum_fusion.18), channel_id=1, source_target_pairs={{0,1},{1,0},{2,3},{3,2},{4,5},{5,4},{6,7},{7,6},{8,9},{9,8},{10,11... | collective-permute-start | bytes 2383880 | tf_op jit(solution)/shard_map/ppermute | solution.py:78
  72.2 45.0 %collective-permute-start.1 = (bf16[256,1552]{0,1:T(8,128)(2,1)S(1)}, bf16[256,1552]{0,1:T(8,128)(2,1)S(1)}, u32[]{:S(2)}, u32[]{:S(2)}) collective-permute-start(bf16[256,1552]{0,1:T(8,128)(2,1)S(1)} %pad_maximum_fusion.17), channel_id=1, source_target_pairs={{0,0},{1,1},{2,2},{3,3},{4,4},{5,5},{6,6},{7,7},{8,8},{9,9},{10,10... | collective-permute-start | bytes 2383880 | tf_op jit(solution)/shard_map/ppermute | solution.py:77
  109.8 48.0 %collective-permute-start.6 = (bf16[256,1552]{0,1:T(8,128)(2,1)}, bf16[256,1552]{0,1:T(8,128)(2,1)}, u32[]{:S(2)}, u32[]{:S(2)}) collective-permute-start(bf16[256,1552]{0,1:T(8,128)(2,1)} %pad_maximum_fusion.22), channel_id=1, source_target_pairs={{0,5},{1,4},{2,7},{3,6},{4,9},{5,8},{6,11},{7,10},{8,13},{9,12},{1... | collective-permute-start | bytes 2383880 | tf_op jit(solution)/shard_map/ppermute | solution.py:78
  109.8 48.5 %collective-permute-start.5 = (bf16[256,1552]{0,1:T(8,128)(2,1)}, bf16[256,1552]{0,1:T(8,128)(2,1)}, u32[]{:S(2)}, u32[]{:S(2)}) collective-permute-start(bf16[256,1552]{0,1:T(8,128)(2,1)} %pad_maximum_fusion.21), channel_id=1, source_target_pairs={{0,4},{1,5},{2,6},{3,7},{4,8},{5,9},{6,10},{7,11},{8,12},{9,13},{1... | collective-permute-start | bytes 2383880 | tf_op jit(solution)/shard_map/ppermute | solution.py:77
  112.9 37.9 %collective-permute-start.4 = (bf16[256,1552]{0,1:T(8,128)(2,1)}, bf16[256,1552]{0,1:T(8,128)(2,1)}, u32[]{:S(2)}, u32[]{:S(2)}) collective-permute-start(bf16[256,1552]{0,1:T(8,128)(2,1)} %pad_maximum_fusion.20), channel_id=1, source_target_pairs={{0,3},{1,2},{2,5},{3,4},{4,7},{5,6},{6,9},{7,8},{8,11},{9,10},{10,... | collective-permute-start | bytes 2383880 | tf_op jit(solution)/shard_map/ppermute | solution.py:78
  147.7 56.8 %collective-permute-start.9 = (bf16[256,1552]{0,1:T(8,128)(2,1)S(1)}, bf16[256,1552]{0,1:T(8,128)(2,1)S(1)}, u32[]{:S(2)}, u32[]{:S(2)}) collective-permute-start(bf16[256,1552]{0,1:T(8,128)(2,1)S(1)} %copy-done.68), channel_id=1, source_target_pairs={{0,8},{1,9},{2,10},{3,11},{4,12},{5,13},{6,14},{7,15},{8,0},{9,1},... | collective-permute-start | bytes 2383880 | tf_op jit(solution)/shard_map/ppermute | solution.py:77
  150.3 24.7 %collective-permute-start.15 = (bf16[256,1552]{0,1:T(8,128)(2,1)S(1)}, bf16[256,1552]{0,1:T(8,128)(2,1)S(1)}, u32[]{:S(2)}, u32[]{:S(2)}) collective-permute-start(bf16[256,1552]{0,1:T(8,128)(2,1)S(1)} %copy-done.67), channel_id=1, source_target_pairs={{0,14},{1,15},{2,0},{3,1},{4,2},{5,3},{6,4},{7,5},{8,6},{9,7},{10,... | collective-permute-start | bytes 2383880 | tf_op jit(solution)/shard_map/ppermute | solution.py:77
  150.8 52.0 %collective-permute-start.16 = (bf16[256,1552]{0,1:T(8,128)(2,1)S(1)}, bf16[256,1552]{0,1:T(8,128)(2,1)S(1)}, u32[]{:S(2)}, u32[]{:S(2)}) collective-permute-start(bf16[256,1552]{0,1:T(8,128)(2,1)S(1)} %copy-done.66), channel_id=1, source_target_pairs={{0,15},{1,14},{2,1},{3,0},{4,3},{5,2},{6,5},{7,4},{8,7},{9,6},{10,... | collective-permute-start | bytes 2383880 | tf_op jit(solution)/shard_map/ppermute | solution.py:78
  156.4 48.2 %copy-start.13 = (bf16[256,1552]{0,1:T(8,128)(2,1)}, bf16[256,1552]{0,1:T(8,128)(2,1)S(1)}, u32[]{:S(2)}) copy-start(bf16[256,1552]{0,1:T(8,128)(2,1)S(1)} %get-tuple-element.193) | copy-start | bytes 2383876
  156.4 48.2 %copy-start.16 = (bf16[256,1552]{0,1:T(8,128)(2,1)}, bf16[256,1552]{0,1:T(8,128)(2,1)S(1)}, u32[]{:S(2)}) copy-start(bf16[256,1552]{0,1:T(8,128)(2,1)S(1)} %get-tuple-element.194) | copy-start | bytes 2383876
  158.2 46.3 %collective-permute-start.10 = (bf16[256,1552]{0,1:T(8,128)(2,1)S(1)}, bf16[256,1552]{0,1:T(8,128)(2,1)S(1)}, u32[]{:S(2)}, u32[]{:S(2)}) collective-permute-start(bf16[256,1552]{0,1:T(8,128)(2,1)S(1)} %copy-done.69), channel_id=1, source_target_pairs={{0,9},{1,8},{2,11},{3,10},{4,13},{5,12},{6,15},{7,14},{8,1},{9,0},... | collective-permute-start | bytes 2383880 | tf_op jit(solution)/shard_map/ppermute | solution.py:78
  159.7 45.0 %copy-start.31 = (bf16[256,1552]{0,1:T(8,128)(2,1)}, bf16[256,1552]{0,1:T(8,128)(2,1)S(1)}, u32[]{:S(2)}) copy-start(bf16[256,1552]{0,1:T(8,128)(2,1)S(1)} %get-tuple-element.191) | copy-start | bytes 2383876
  159.7 45.0 %copy-start.33 = (bf16[256,1552]{0,1:T(8,128)(2,1)}, bf16[256,1552]{0,1:T(8,128)(2,1)S(1)}, u32[]{:S(2)}) copy-start(bf16[256,1552]{0,1:T(8,128)(2,1)S(1)} %get-tuple-element.192) | copy-start | bytes 2383876
  267.9 18.5 %copy-start.64 = (bf16[256,1552]{0,1:T(8,128)(2,1)S(1)}, bf16[256,1552]{0,1:T(8,128)(2,1)}, u32[]{:S(2)}) copy-start(bf16[256,1552]{0,1:T(8,128)(2,1)} %pad_maximum_fusion.30) | copy-start | bytes 2383876
  267.9 18.5 %copy-start.65 = (bf16[256,1552]{0,1:T(8,128)(2,1)S(1)}, bf16[256,1552]{0,1:T(8,128)(2,1)}, u32[]{:S(2)}) copy-start(bf16[256,1552]{0,1:T(8,128)(2,1)} %pad_maximum_fusion.27) | copy-start | bytes 2383876
  267.9 26.2 %copy-start.46 = (f32[256,1024]{1,0:T(8,128)S(1)}, f32[256,1024]{1,0:T(8,128)}, u32[]{:S(2)}) copy-start(f32[256,1024]{1,0:T(8,128)} %fusion.172) | copy-start | bytes 3145732
  269.4 84.9 %collective-permute-start.13 = (bf16[256,1552]{0,1:T(8,128)(2,1)S(1)}, bf16[256,1552]{0,1:T(8,128)(2,1)S(1)}, u32[]{:S(2)}, u32[]{:S(2)}) collective-permute-start(bf16[256,1552]{0,1:T(8,128)(2,1)S(1)} %copy-done.63), channel_id=1, source_target_pairs={{0,12},{1,13},{2,14},{3,15},{4,0},{5,1},{6,2},{7,3},{8,4},{9,5},{1... | collective-permute-start | bytes 2383880 | tf_op jit(solution)/shard_map/ppermute | solution.py:77
  286.4 67.8 %collective-permute-start.14 = (bf16[256,1552]{0,1:T(8,128)(2,1)S(1)}, bf16[256,1552]{0,1:T(8,128)(2,1)S(1)}, u32[]{:S(2)}, u32[]{:S(2)}) collective-permute-start(bf16[256,1552]{0,1:T(8,128)(2,1)S(1)} %copy-done.64), channel_id=1, source_target_pairs={{0,13},{1,12},{2,15},{3,14},{4,1},{5,0},{6,3},{7,2},{8,5},{9,4},{1... | collective-permute-start | bytes 2383880 | tf_op jit(solution)/shard_map/ppermute | solution.py:78
  286.5 68.0 %collective-permute-start.11 = (bf16[256,1552]{0,1:T(8,128)(2,1)S(1)}, bf16[256,1552]{0,1:T(8,128)(2,1)S(1)}, u32[]{:S(2)}, u32[]{:S(2)}) collective-permute-start(bf16[256,1552]{0,1:T(8,128)(2,1)S(1)} %copy-done.65), channel_id=1, source_target_pairs={{0,10},{1,11},{2,12},{3,13},{4,14},{5,15},{6,0},{7,1},{8,2},{9,3},... | collective-permute-start | bytes 2383880 | tf_op jit(solution)/shard_map/ppermute | solution.py:77
  286.5 67.9 %collective-permute-start.12 = (bf16[256,1552]{0,1:T(8,128)(2,1)}, bf16[256,1552]{0,1:T(8,128)(2,1)S(1)}, u32[]{:S(2)}, u32[]{:S(2)}) collective-permute-start(bf16[256,1552]{0,1:T(8,128)(2,1)} %pad_maximum_fusion.28), channel_id=1, source_target_pairs={{0,11},{1,10},{2,13},{3,12},{4,15},{5,14},{6,1},{7,0},{8,3},{9,2},... | collective-permute-start | bytes 2383880 | tf_op jit(solution)/shard_map/ppermute | solution.py:78
  359.3 17.6 %copy-start.89 = (f32[16,4]{0,1:T(4,128)}, f32[16,4]{0,1:T(4,128)S(1)}, u32[]{:S(2)}) copy-start(f32[16,4]{0,1:T(4,128)S(1)} %slice.788) | copy-start | bytes 772
  363.6 22.1 %copy-start.90 = (f32[16,4]{0,1:T(4,128)}, f32[16,4]{0,1:T(4,128)S(1)}, u32[]{:S(2)}) copy-start(f32[16,4]{0,1:T(4,128)S(1)} %slice.765) | copy-start | bytes 772
  482.2 17.3 %copy-start.50 = (bf16[1,512,256]{2,1,0:T(8,128)(2,1)S(1)}, bf16[1,512,256]{2,1,0:T(8,128)(2,1)}, u32[]{:S(2)}) copy-start(bf16[1,512,256]{2,1,0:T(8,128)(2,1)} %copy.518) | copy-start | bytes 786436
  482.2 18.1 %copy-start.49 = (bf16[1,512,256]{2,1,0:T(8,128)(2,1)S(1)}, bf16[1,512,256]{2,1,0:T(8,128)(2,1)}, u32[]{:S(2)}) copy-start(bf16[1,512,256]{2,1,0:T(8,128)(2,1)} %copy.519) | copy-start | bytes 786436
  482.2 18.8 %copy-start.41 = (f32[1,512,1024]{2,1,0:T(8,128)S(1)}, f32[1,512,1024]{2,1,0:T(8,128)}, u32[]{:S(2)}) copy-start(f32[1,512,1024]{2,1,0:T(8,128)} %copy.501) | copy-start | bytes 6291460
  (94 other events, 263.7 us)
Sparse Core Ops, SparseCore 0:
  404.3 49.3 all-gather.2

commit v11 on v10

--- a/solution.py
+++ b/solution.py
@@ -72,8 +72,8 @@
         t_same = 2 * ((head_pos // 2 + m) % pairs) + parity
         t_other = 2 * ((head_pos // 2 + m) % pairs) + 1 - parity
         p_same, p_other = payload(t_same), payload(t_other)
-        if m >= 4:
-            p_same, p_other, _ = lax.optimization_barrier((p_same, p_other, done[m - 4]))
+        if m >= 5:
+            p_same, p_other, _ = lax.optimization_barrier((p_same, p_other, done[m - 5]))
         r_same = lax.ppermute(p_same, "head", same)
         r_other = lax.ppermute(p_other, "head", other)
         first = jnp.where(parity == 0, r_same, r_other)

time: 570 us -> 582 us (1.021)
  starting transfers between devices: 50.1 us -> 69.6 us
  local copies, waits for them, and re-layouts: 160 us -> 143 us
  other arithmetic: 148 us -> 156 us
    ppermute x8, waiting for transfers between devices: 71.2 us -> 29.9 us  [on_device(): r_same = lax.ppermute(p_same, 'head', same)]
    ppermute x8, waiting for transfers between devices: 29.5 us -> 66.5 us  [on_device(): r_other = lax.ppermute(p_other, 'head', other)]
    ppermute x8, starting transfers between devices: 21.4 us -> 34.9 us  [on_device(): r_other = lax.ppermute(p_other, 'head', other)]
    broadcast_in_dim x8, local copies, waits for them, and re-layouts: 9.09 us -> 1.79 us  [on_device(): fade = jnp.exp(jnp.repeat(block_totals[k], HEADDIM))]
    exp x7, local copies, waits for them, and re-layouts: 8.32 us -> 1.1 us  [on_device(): fade = jnp.exp(jnp.repeat(block_totals[k], HEADDIM))]
    ppermute x8, starting transfers between devices: 24.9 us -> 31 us  [on_device(): r_same = lax.ppermute(p_same, 'head', same)]
    unnamed x235 -> x229, local copies, waits for them, and re-layouts: 31.2 us -> 29.8 us
  transfers between devices with their start and end apart: 18 -> 18, of which waited for: 4 -> 6; matrix products, arithmetic and copies ran while one was open for 39% -> 39% of each run, Pallas kernels for 0% -> 0%
where the time goes in v11:
time: 582 us; the launch traced here: 573 us
  other arithmetic  156 us (27%)
  local copies, waits for them, and re-layouts  143 us (25%)
  waiting for transfers between devices  96.5 us (17%)
  matrix products  91 us (16%)
  starting transfers between devices  69.6 us (12%)
  between operations  16.8 us (3%)
    ppermute x8, waiting for transfers between devices, on_device(): r_other = lax.ppermute(p_other, 'head', other)  66.5 us
    dot_general x8, matrix products, on_device(): jnp.einsum('hts,shp->thp', mix, x_heads, preferred_element_type=f32)  43.9 us
    convert_element_type x16, other arithmetic, payload(): act = jax.nn.silu(total + pick(conv_bias)).astype(jnp.bfloat16)  35.5 us
    ppermute x8, starting transfers between devices, on_device(): r_other = lax.ppermute(p_other, 'head', other)  34.9 us
    ppermute x8, starting transfers between devices, on_device(): r_same = lax.ppermute(p_same, 'head', same)  31 us
    ppermute x8, waiting for transfers between devices, on_device(): r_same = lax.ppermute(p_same, 'head', same)  29.9 us
    unnamed x229, local copies, waits for them, and re-layouts  29.8 us
    another operation x24, other arithmetic  27.6 us
  transfers between devices with their start and end apart: 18, of which 6 were waited for; matrix products, arithmetic and copies ran while one was open for 39% of the time, Pallas kernels for 0%

profile of v11, /device:TPU:30, one launch (start us, length us, event | category | flops | bytes accessed | tf_op | source)
XLA Modules:
  0.0 573.1 jit_solution(6725532968540843040)
XLA Ops:
  7.6 3.7 collective-permute-start
  15.7 13.9 %copy.471 = bf16[256,20480]{0,1:T(8,128)(2,1)} copy(bf16[256,20480]{1,0:T(8,128)(2,1)} %param.7) | data formatting | bytes 20971520 | tf_op args[0]
  31.4 3.6 copy.470
  57.5 3.2 collective-permute-start.8
  106.5 3.2 collective-permute-start.7
  128.2 4.5 broadcast_in_dim.363
  134.1 5.0 fusion.5
  139.2 5.0 fusion.3
  149.5 3.5 collective-permute-start.11
  155.8 19.6 %collective-permute-start.15 = (bf16[256,1552]{0,1:T(8,128)(2,1)S(1)}, bf16[256,1552]{0,1:T(8,128)(2,1)S(1)}, u32[]{:S(2)}, u32[]{:S(2)}) collective-permute-start(bf16[256,1552]{0,1:T(8,128)(2,1)S(1)} %copy-done.72), channel_id=1, source_target_pairs={{0,14},{1,15},{2,0},{3,1},{4,2},{5,3},{6,4},{7,5},{8,6},{9,7},{10,... | collective-permute-start | bytes 2383880 | tf_op jit(solution)/shard_map/ppermute | solution.py:77
  175.3 21.0 %collective-permute-start.16 = (bf16[256,1552]{0,1:T(8,128)(2,1)S(1)}, bf16[256,1552]{0,1:T(8,128)(2,1)S(1)}, u32[]{:S(2)}, u32[]{:S(2)}) collective-permute-start(bf16[256,1552]{0,1:T(8,128)(2,1)S(1)} %copy-done.71), channel_id=1, source_target_pairs={{0,15},{1,14},{2,1},{3,0},{4,3},{5,2},{6,5},{7,4},{8,7},{9,6},{10,... | collective-permute-start | bytes 2383880 | tf_op jit(solution)/shard_map/ppermute | solution.py:78
  199.2 14.6 %collective-permute-done.4 = bf16[256,1552]{0,1:T(8,128)(2,1)} collective-permute-done((bf16[256,1552]{0,1:T(8,128)(2,1)}, bf16[256,1552]{0,1:T(8,128)(2,1)}, u32[]{:S(2)}, u32[]{:S(2)}) %collective-permute-start.4) | collective-permute-done | bytes 794656 | tf_op jit(solution)/shard_map/ppermute | solution.py:78
  213.8 4.8 collective-permute-start.12
  221.3 9.4 %collective-permute-done.16 = bf16[256,1552]{0,1:T(8,128)(2,1)S(1)} collective-permute-done((bf16[256,1552]{0,1:T(8,128)(2,1)S(1)}, bf16[256,1552]{0,1:T(8,128)(2,1)S(1)}, u32[]{:S(2)}, u32[]{:S(2)}) %collective-permute-start.16) | collective-permute-done | bytes 794656 | tf_op jit(solution)/shard_map/ppermute | solution.py:78
  232.5 40.7 %collective-permute-done.12 = bf16[256,1552]{0,1:T(8,128)(2,1)S(1)} collective-permute-done((bf16[256,1552]{0,1:T(8,128)(2,1)S(1)}, bf16[256,1552]{0,1:T(8,128)(2,1)S(1)}, u32[]{:S(2)}, u32[]{:S(2)}) %collective-permute-start.12) | collective-permute-done | bytes 794656 | tf_op jit(solution)/shard_map/ppermute | solution.py:78
  290.6 3.1 reduce-window.66
  299.2 3.1 reduce-window.70
  321.4 5.7 fusion.10
  327.0 5.8 %fusion.4 = f32[16,64,512]{2,1,0:T(8,128)} fusion(bf16[512,16,64]{0,2,1:T(8,128)(2,1)S(1)} %bitcast.403, f32[16,512]{1,0:T(8,128)S(1)} %bitcast.413, f32[16,512]{1,0:T(8,128)S(1)} %get-tuple-element.317, f32[512,512]{1,0:T(8,128)S(1)} %copy-done.59, pred[512,512]{1,0:T(8,128)(4,1)S(1)} %copy-done.75), kind=kOutput, calls=%fused_computation.110 | convolution fusion | flops 557842432 | bytes 4521984 | tf_op jit(solution)/shard_map/hts,shp->thp/dot_general | solution.py:93
  332.8 5.7 %fusion.6 = f32[16,64,512]{2,1,0:T(8,128)} fusion(bf16[512,16,64]{0,2,1:T(8,128)(2,1)S(1)} %bitcast.404, f32[16,512]{1,0:T(8,128)S(1)} %bitcast.412, f32[16,512]{1,0:T(8,128)S(1)} %get-tuple-element.313, f32[512,512]{1,0:T(8,128)S(1)} %copy-done.57, pred[512,512]{1,0:T(8,128)(4,1)S(1)} %copy-done.75), kind=kOutput, calls=%fused_computation.112 | convolution fusion | flops 557842432 | bytes 4521984 | tf_op jit(solution)/shard_map/hts,shp->thp/dot_general | solution.py:93
  338.6 5.8 %fusion.7 = f32[16,64,512]{2,1,0:T(8,128)} fusion(bf16[512,16,64]{0,2,1:T(8,128)(2,1)S(1)} %bitcast.405, f32[16,512]{1,0:T(8,128)S(1)} %bitcast.411, f32[16,512]{1,0:T(8,128)S(1)} %get-tuple-element.311, f32[512,512]{1,0:T(8,128)S(1)} %copy-done.58, pred[512,512]{1,0:T(8,128)(4,1)S(1)} %copy-done.75), kind=kOutput, calls=%fused_computation.113 | convolution fusion | flops 557842432 | bytes 4521984 | tf_op jit(solution)/shard_map/hts,shp->thp/dot_general | solution.py:93
  344.4 5.9 %fusion.8 = f32[16,64,512]{2,1,0:T(8,128)} fusion(bf16[512,16,64]{0,2,1:T(8,128)(2,1)S(1)} %bitcast.406, f32[16,512]{1,0:T(8,128)S(1)} %bitcast.410, f32[16,512]{1,0:T(8,128)S(1)} %get-tuple-element.309, f32[512,512]{1,0:T(8,128)S(1)} %copy-done.61, pred[512,512]{1,0:T(8,128)(4,1)S(1)} %copy-done.75), kind=kOutput, calls=%fused_computation.114 | convolution fusion | flops 557842432 | bytes 4521984 | tf_op jit(solution)/shard_map/hts,shp->thp/dot_general | solution.py:93
  350.3 10.6 %fusion.40 = (f32[1,512,1024]{1,2,0:T(8,128)}, f32[512,1024]{0,1:T(8,128)}, f32[1,512,1024]{1,2,0:T(8,128)}, f32[1,512,1024]{1,2,0:T(8,128)}, f32[1,512,1024]{1,2,0:T(8,128)}) fusion(bf16[512,1024]{0,1:T(8,128)(2,1)} %copy-done.45, f32[16,64,512]{2,1,0:T(8,128)} %fusion.10, f32[1024]{0:T(1024)S(1)} %mul.1532, bf16[512,1024]{0,1:T(8,128)(2,1)} %copy-done.46, ...), kind=kLoop, calls=%fused_computation.162 | loop fusion | flops 7864320 | bytes 26218496 | tf_op jit(solution)/shard_map/jit(dynamic_update_index_in_dim)/broadcast_in_dim | solution.py:100
  369.1 28.6 %collective-permute-done.13 = bf16[256,1552]{0,1:T(8,128)(2,1)S(1)} collective-permute-done((bf16[256,1552]{0,1:T(8,128)(2,1)}, bf16[256,1552]{0,1:T(8,128)(2,1)S(1)}, u32[]{:S(2)}, u32[]{:S(2)}) %collective-permute-start.13) | collective-permute-done | bytes 794656 | tf_op jit(solution)/shard_map/ppermute | solution.py:77
  415.4 4.4 fusion.60
  440.5 8.1 %broadcast_in_dim.330 = f32[8,512,1024]{2,1,0:T(8,128)} broadcast(f32[]{:T(128)} %constant.440.clone.1), dimensions={} | broadcast | bytes 16777220 | tf_op jit(solution)/shard_map/broadcast_in_dim | solution.py:64
  465.9 3.4 constant_dynamic-update-slice_fusion.22
  479.1 4.9 fusion.9
  487.6 7.9 %broadcast_in_dim.351 = f32[8,512,16,64]{1,3,2,0:T(8,128)} broadcast(f32[8,512,16]{1,2,0:T(8,128)S(1)} %exp.291), dimensions={0,1,2} | broadcast | bytes 17039360 | tf_op jit(solution)/shard_map/broadcast_in_dim | solution.py:133
  495.5 16.4 %copy.520 = f32[8,512,1024]{2,1,0:T(8,128)} copy(f32[8,512,1024]{1,2,0:T(8,128)} %bitcast.395) | data formatting | bytes 33554432 | tf_op jit(solution)/shard_map/exp | solution.py:133
  537.4 4.6 fusion
  542.0 24.0 %add_convert_fusion = bf16[8,512,1024]{2,1,0:T(8,128)(2,1)} fusion(f32[8,512,1024]{2,1,0:T(8,128)} %constant_dynamic-update-slice_fusion.16, f32[8,512,1024]{2,1,0:T(8,128)} %copy.520, bf16[8,512,256]{2,1,0:T(8,128)(2,1)} %constant_dynamic-update-slice_fusion, f32[8,256,1024]{2,1,0:T(8,128)} %add_dynamic-update-slice_fusion, f32[256,1024]{1,0:T(8,128)S(1)} %fusion, ...), kind=kOutput, calls=%fused_computation.96 | convolution fusion | flops 12901679104 | bytes 53510144 | tf_op jit(solution)/shard_map/bqn,bnc->bqc/dot_general | solution.py:134
  (538 shorter events, 252.7 us)
Async XLA Ops:
  6.5 528.7 %all-gather.3.cloned.1.call-start = ((), (), s32[]{:S(2)}) async-start(), calls=%async_computation | async-start | bytes 9732096 | tf_op jit(solution)/shard_map/all_gather | solution.py:117
  7.6 23.7 %collective-permute-start = (bf16[3,20480]{1,0:T(4,128)(2,1)S(1)}, bf16[3,20480]{1,0:T(4,128)(2,1)S(1)}, u32[]{:S(2)}, u32[]{:S(2)}) collective-permute-start(bf16[3,20480]{1,0:T(4,128)(2,1)S(1)} %slice.631), channel_id=1, source_target_pairs={{0,1},{1,2},{2,3},{3,4},{4,5},{5,6},{6,7},{7,8},{8,9},{9,10},{10,1... | collective-permute-start | bytes 368648 | tf_op jit(solution)/shard_map/ppermute | solution.py:25
  15.0 104.3 %copy-start.93 = (f32[16]{0:T(128)}, f32[16]{0:T(128)S(1)}, u32[]{:S(2)}) copy-start(f32[16]{0:T(128)S(1)} %exponential_negate_fusion) | copy-start | bytes 196
  29.7 89.6 %copy-start.96 = (f32[16]{0:T(128)}, f32[16]{0:T(128)S(1)}, u32[]{:S(2)}) copy-start(f32[16]{0:T(128)S(1)} %dynamic_slice.510) | copy-start | bytes 196
  31.3 107.8 %copy-start.74 = (pred[512,512]{1,0:T(8,128)(4,1)}, pred[512,512]{1,0:T(8,128)(4,1)S(1)}, u32[]{:S(2)}) copy-start(pred[512,512]{1,0:T(8,128)(4,1)S(1)} %iota_compare_fusion) | copy-start | bytes 786436
  52.0 54.5 %collective-permute-start.5 = (bf16[256,1552]{0,1:T(8,128)(2,1)S(1)}, bf16[256,1552]{0,1:T(8,128)(2,1)S(1)}, u32[]{:S(2)}, u32[]{:S(2)}) collective-permute-start(bf16[256,1552]{0,1:T(8,128)(2,1)S(1)} %pad_maximum_fusion.21), channel_id=1, source_target_pairs={{0,4},{1,5},{2,6},{3,7},{4,8},{5,9},{6,10},{7,11},{8,12},{9,13},{1... | collective-permute-start | bytes 2383880 | tf_op jit(solution)/shard_map/ppermute | solution.py:77
  57.5 90.7 %collective-permute-start.8 = (bf16[256,1552]{0,1:T(8,128)(2,1)}, bf16[256,1552]{0,1:T(8,128)(2,1)}, u32[]{:S(2)}, u32[]{:S(2)}) collective-permute-start(bf16[256,1552]{0,1:T(8,128)(2,1)} %pad_maximum_fusion.24), channel_id=1, source_target_pairs={{0,7},{1,6},{2,9},{3,8},{4,11},{5,10},{6,13},{7,12},{8,15},{9,14},... | collective-permute-start | bytes 2383880 | tf_op jit(solution)/shard_map/ppermute | solution.py:78
  63.6 46.1 %collective-permute-start.6 = (bf16[256,1552]{0,1:T(8,128)(2,1)S(1)}, bf16[256,1552]{0,1:T(8,128)(2,1)S(1)}, u32[]{:S(2)}, u32[]{:S(2)}) collective-permute-start(bf16[256,1552]{0,1:T(8,128)(2,1)S(1)} %pad_maximum_fusion.22), channel_id=1, source_target_pairs={{0,5},{1,4},{2,7},{3,6},{4,9},{5,8},{6,11},{7,10},{8,13},{9,12},{1... | collective-permute-start | bytes 2383880 | tf_op jit(solution)/shard_map/ppermute | solution.py:78
  66.2 48.1 %collective-permute-start.2 = (bf16[256,1552]{0,1:T(8,128)(2,1)S(1)}, bf16[256,1552]{0,1:T(8,128)(2,1)S(1)}, u32[]{:S(2)}, u32[]{:S(2)}) collective-permute-start(bf16[256,1552]{0,1:T(8,128)(2,1)S(1)} %pad_maximum_fusion.18), channel_id=1, source_target_pairs={{0,1},{1,0},{2,3},{3,2},{4,5},{5,4},{6,7},{7,6},{8,9},{9,8},{10,11... | collective-permute-start | bytes 2383880 | tf_op jit(solution)/shard_map/ppermute | solution.py:78
  69.4 46.4 %collective-permute-start.1 = (bf16[256,1552]{0,1:T(8,128)(2,1)S(1)}, bf16[256,1552]{0,1:T(8,128)(2,1)S(1)}, u32[]{:S(2)}, u32[]{:S(2)}) collective-permute-start(bf16[256,1552]{0,1:T(8,128)(2,1)S(1)} %pad_maximum_fusion.17), channel_id=1, source_target_pairs={{0,0},{1,1},{2,2},{3,3},{4,4},{5,5},{6,6},{7,7},{8,8},{9,9},{10,10... | collective-permute-start | bytes 2383880 | tf_op jit(solution)/shard_map/ppermute | solution.py:77
  106.5 42.9 %collective-permute-start.7 = (bf16[256,1552]{0,1:T(8,128)(2,1)}, bf16[256,1552]{0,1:T(8,128)(2,1)}, u32[]{:S(2)}, u32[]{:S(2)}) collective-permute-start(bf16[256,1552]{0,1:T(8,128)(2,1)} %pad_maximum_fusion.23), channel_id=1, source_target_pairs={{0,6},{1,7},{2,8},{3,9},{4,10},{5,11},{6,12},{7,13},{8,14},{9,15},... | collective-permute-start | bytes 2383880 | tf_op jit(solution)/shard_map/ppermute | solution.py:77
  109.7 46.1 %collective-permute-start.10 = (bf16[256,1552]{0,1:T(8,128)(2,1)}, bf16[256,1552]{0,1:T(8,128)(2,1)}, u32[]{:S(2)}, u32[]{:S(2)}) collective-permute-start(bf16[256,1552]{0,1:T(8,128)(2,1)} %pad_maximum_fusion.26), channel_id=1, source_target_pairs={{0,9},{1,8},{2,11},{3,10},{4,13},{5,12},{6,15},{7,14},{8,1},{9,0},... | collective-permute-start | bytes 2383880 | tf_op jit(solution)/shard_map/ppermute | solution.py:78
  114.3 61.0 %collective-permute-start.9 = (bf16[256,1552]{0,1:T(8,128)(2,1)}, bf16[256,1552]{0,1:T(8,128)(2,1)}, u32[]{:S(2)}, u32[]{:S(2)}) collective-permute-start(bf16[256,1552]{0,1:T(8,128)(2,1)} %pad_maximum_fusion.25), channel_id=1, source_target_pairs={{0,8},{1,9},{2,10},{3,11},{4,12},{5,13},{6,14},{7,15},{8,0},{9,1},... | collective-permute-start | bytes 2383880 | tf_op jit(solution)/shard_map/ppermute | solution.py:77
  115.8 98.0 %collective-permute-start.4 = (bf16[256,1552]{0,1:T(8,128)(2,1)}, bf16[256,1552]{0,1:T(8,128)(2,1)}, u32[]{:S(2)}, u32[]{:S(2)}) collective-permute-start(bf16[256,1552]{0,1:T(8,128)(2,1)} %pad_maximum_fusion.20), channel_id=1, source_target_pairs={{0,3},{1,2},{2,5},{3,4},{4,7},{5,6},{6,9},{7,8},{8,11},{9,10},{10,... | collective-permute-start | bytes 2383880 | tf_op jit(solution)/shard_map/ppermute | solution.py:78
  148.2 70.4 %collective-permute-start.3 = (bf16[256,1552]{0,1:T(8,128)(2,1)S(1)}, bf16[256,1552]{0,1:T(8,128)(2,1)S(1)}, u32[]{:S(2)}, u32[]{:S(2)}) collective-permute-start(bf16[256,1552]{0,1:T(8,128)(2,1)S(1)} %copy-done.73), channel_id=1, source_target_pairs={{0,2},{1,3},{2,4},{3,5},{4,6},{5,7},{6,8},{7,9},{8,10},{9,11},{10,... | collective-permute-start | bytes 2383880 | tf_op jit(solution)/shard_map/ppermute | solution.py:77
  149.5 83.0 %collective-permute-start.11 = (bf16[256,1552]{0,1:T(8,128)(2,1)S(1)}, bf16[256,1552]{0,1:T(8,128)(2,1)S(1)}, u32[]{:S(2)}, u32[]{:S(2)}) collective-permute-start(bf16[256,1552]{0,1:T(8,128)(2,1)S(1)} %copy-done.69), channel_id=1, source_target_pairs={{0,10},{1,11},{2,12},{3,13},{4,14},{5,15},{6,0},{7,1},{8,2},{9,3},... | collective-permute-start | bytes 2383880 | tf_op jit(solution)/shard_map/ppermute | solution.py:77
  155.8 65.5 %collective-permute-start.15 = (bf16[256,1552]{0,1:T(8,128)(2,1)S(1)}, bf16[256,1552]{0,1:T(8,128)(2,1)S(1)}, u32[]{:S(2)}, u32[]{:S(2)}) collective-permute-start(bf16[256,1552]{0,1:T(8,128)(2,1)S(1)} %copy-done.72), channel_id=1, source_target_pairs={{0,14},{1,15},{2,0},{3,1},{4,2},{5,3},{6,4},{7,5},{8,6},{9,7},{10,... | collective-permute-start | bytes 2383880 | tf_op jit(solution)/shard_map/ppermute | solution.py:77
  175.3 55.4 %collective-permute-start.16 = (bf16[256,1552]{0,1:T(8,128)(2,1)S(1)}, bf16[256,1552]{0,1:T(8,128)(2,1)S(1)}, u32[]{:S(2)}, u32[]{:S(2)}) collective-permute-start(bf16[256,1552]{0,1:T(8,128)(2,1)S(1)} %copy-done.71), channel_id=1, source_target_pairs={{0,15},{1,14},{2,1},{3,0},{4,3},{5,2},{6,5},{7,4},{8,7},{9,6},{10,... | collective-permute-start | bytes 2383880 | tf_op jit(solution)/shard_map/ppermute | solution.py:78
  197.9 75.5 %copy-start.7 = (bf16[256,1552]{0,1:T(8,128)(2,1)}, bf16[256,1552]{0,1:T(8,128)(2,1)S(1)}, u32[]{:S(2)}) copy-start(bf16[256,1552]{0,1:T(8,128)(2,1)S(1)} %get-tuple-element.183) | copy-start | bytes 2383876
  197.9 75.5 %copy-start.11 = (bf16[256,1552]{0,1:T(8,128)(2,1)}, bf16[256,1552]{0,1:T(8,128)(2,1)S(1)}, u32[]{:S(2)}) copy-start(bf16[256,1552]{0,1:T(8,128)(2,1)S(1)} %get-tuple-element.184) | copy-start | bytes 2383876
  213.8 59.4 %collective-permute-start.12 = (bf16[256,1552]{0,1:T(8,128)(2,1)S(1)}, bf16[256,1552]{0,1:T(8,128)(2,1)S(1)}, u32[]{:S(2)}, u32[]{:S(2)}) collective-permute-start(bf16[256,1552]{0,1:T(8,128)(2,1)S(1)} %copy-done.70), channel_id=1, source_target_pairs={{0,11},{1,10},{2,13},{3,12},{4,15},{5,14},{6,1},{7,0},{8,3},{9,2},... | collective-permute-start | bytes 2383880 | tf_op jit(solution)/shard_map/ppermute | solution.py:78
  219.8 53.5 %copy-start.23 = (bf16[256,1552]{0,1:T(8,128)(2,1)}, bf16[256,1552]{0,1:T(8,128)(2,1)S(1)}, u32[]{:S(2)}) copy-start(bf16[256,1552]{0,1:T(8,128)(2,1)S(1)} %get-tuple-element.189) | copy-start | bytes 2383876
  219.8 53.5 %copy-start.26 = (bf16[256,1552]{0,1:T(8,128)(2,1)}, bf16[256,1552]{0,1:T(8,128)(2,1)S(1)}, u32[]{:S(2)}) copy-start(bf16[256,1552]{0,1:T(8,128)(2,1)S(1)} %get-tuple-element.190) | copy-start | bytes 2383876
  230.8 42.5 %copy-start.1 = (bf16[256,1552]{0,1:T(8,128)(2,1)}, bf16[256,1552]{0,1:T(8,128)(2,1)S(1)}, u32[]{:S(2)}) copy-start(bf16[256,1552]{0,1:T(8,128)(2,1)S(1)} %get-tuple-element.177) | copy-start | bytes 2383876
  230.8 42.5 %copy-start.4 = (bf16[256,1552]{0,1:T(8,128)(2,1)}, bf16[256,1552]{0,1:T(8,128)(2,1)S(1)}, u32[]{:S(2)}) copy-start(bf16[256,1552]{0,1:T(8,128)(2,1)S(1)} %get-tuple-element.178) | copy-start | bytes 2383876
  232.5 40.9 %copy-start.94 = (f32[16]{0:T(128)S(1)}, f32[16]{0:T(128)}, u32[]{:S(2)}) copy-start(f32[16]{0:T(128)} %copy-done.93) | copy-start | bytes 196
  232.5 40.9 %copy-start.97 = (f32[16]{0:T(128)S(1)}, f32[16]{0:T(128)}, u32[]{:S(2)}) copy-start(f32[16]{0:T(128)} %copy-done.96) | copy-start | bytes 196
  321.1 23.2 %copy-start.49 = (bf16[512,1024]{0,1:T(8,128)(2,1)}, bf16[512,1024]{0,1:T(8,128)(2,1)S(1)}, u32[]{:S(2)}) copy-start(bf16[512,1024]{0,1:T(8,128)(2,1)S(1)} %get-tuple-element.102) | copy-start | bytes 3145732
  360.8 36.9 %collective-permute-start.13 = (bf16[256,1552]{0,1:T(8,128)(2,1)}, bf16[256,1552]{0,1:T(8,128)(2,1)S(1)}, u32[]{:S(2)}, u32[]{:S(2)}) collective-permute-start(bf16[256,1552]{0,1:T(8,128)(2,1)} %pad_maximum_fusion.29), channel_id=1, source_target_pairs={{0,12},{1,13},{2,14},{3,15},{4,0},{5,1},{6,2},{7,3},{8,4},{9,5},{1... | collective-permute-start | bytes 2383880 | tf_op jit(solution)/shard_map/ppermute | solution.py:77
  360.8 36.9 %collective-permute-start.14 = (bf16[256,1552]{0,1:T(8,128)(2,1)}, bf16[256,1552]{0,1:T(8,128)(2,1)S(1)}, u32[]{:S(2)}, u32[]{:S(2)}) collective-permute-start(bf16[256,1552]{0,1:T(8,128)(2,1)} %pad_maximum_fusion.30), channel_id=1, source_target_pairs={{0,13},{1,12},{2,15},{3,14},{4,1},{5,0},{6,3},{7,2},{8,5},{9,4},{1... | collective-permute-start | bytes 2383880 | tf_op jit(solution)/shard_map/ppermute | solution.py:78
  369.1 29.6 %copy-start.95 = (f32[16]{0:T(128)S(1)}, f32[16]{0:T(128)}, u32[]{:S(2)}) copy-start(f32[16]{0:T(128)} %copy-done.93) | copy-start | bytes 196
  369.1 29.6 %copy-start.98 = (f32[16]{0:T(128)S(1)}, f32[16]{0:T(128)}, u32[]{:S(2)}) copy-start(f32[16]{0:T(128)} %copy-done.96) | copy-start | bytes 196
  (91 other events, 373.4 us)
Sparse Core Ops, SparseCore 0:
  421.0 52.1 all-gather.2
